TPU v7x, 512 devices: a whole 4x4x16 slice. The times are simulated.
512 devices in a mesh: dp: 128 (over x, z, core), bin: 4 (over y).
Axes of the slice: x: 4, y: 4, z: 16, core: 2. Of those that a mesh axis runs over, the one named last changes fastest.
Arguments:
- features: bfloat16 [65536, 2, 2048], P(('dp', 'bin')), may hold values from -90 to 90
- head_weight: bfloat16 [2048, 1024], P('bin'), may hold values from -9 to 9
- bin_of_row: int32 [65536, 1], P(('dp', 'bin')), may hold values from 0 to 191; in each aligned block of 128 rows (0 to 127, 128 to 255, ...) at most 2 rows name the same one
- bin_owner: int32 [192], replicated, may hold values from 0 to 127, never falling along the last dimension, each value on 1 to 2 neighbouring positions
- bin_link: int32 [192], replicated, may hold values 0 or 1
Outputs:
- grad_rows: bfloat16 [65536, 2, 1024], P(('dp', 'bin'))
- grad_weight: float32 [2048, 1024], P(('bin', 'dp'))
Inputs may be any that keep to these rules, and one draw needn't show every extreme that they name: `bin_of_row`: in the rows of one device no bin appears more than 2 times. `bin_owner`: never falls; every owner holds 1 to 2 consecutive bins.
All inputs are finite; a program needn't handle non-finite values.
Results may differ from a plain program's by a relative error of at most 0.012.
Values may be sent and summed in bfloat16 or wider, within the bound.
No kernel may reach another device: no remote copies, remote signals or barrier semaphores. Data moves between devices by JAX's collectives and lax.ppermute only.
A program may use at most 64 MiB of HBM per device.

v0:
```python
import jax
import jax.numpy as jnp
from jax import lax
from jax.sharding import PartitionSpec as P

MOSTB = 2


SOFTMAX_TEMP_SCALE = 0.1


def allowed_mask(valid, first, bin_link, group_slots, per_bin):
    per_owner = per_bin * MOSTB
    position = jnp.arange(group_slots, dtype=jnp.int32)
    local_bin = position % per_owner // per_bin
    padded = jnp.concatenate([bin_link, jnp.zeros((MOSTB,), jnp.int32)])
    nearby = lax.dynamic_slice(padded, (first,), (MOSTB,))
    lower = jnp.minimum(local_bin[:, None], local_bin[None, :])
    linked = jnp.zeros((group_slots, group_slots), jnp.int32)
    for height in range(MOSTB):
        linked = linked + jnp.where(lower == height, nearby[height], 0)
    spacing = jnp.abs(local_bin[:, None] - local_bin[None, :])
    paired = valid[:, None] & valid[None, :]
    allowed = paired & ((spacing == 0) | (spacing == 1) & (linked == 1))
    allowed = allowed | (position[:, None] == position[None, :])
    return allowed.astype(jnp.float32)


def contrast(query_rows, key_matrix, allowed, valid):
    similarity_scores = (
        lax.dot_general(
            query_rows, key_matrix, (((1,), (1,)), ((), ())), preferred_element_type=jnp.float32
        )
        / SOFTMAX_TEMP_SCALE
    )
    weights = allowed * jnp.exp(similarity_scores)
    shares = weights / jnp.sum(weights, axis=1, keepdims=True)
    position = jnp.arange(query_rows.shape[0], dtype=jnp.int32)
    diagonal = (position[:, None] == position[None, :]).astype(jnp.float32)
    logit_gradient = ((shares - diagonal) * valid[:, None]).astype(jnp.bfloat16)
    query_gradient = (
        jnp.dot(logit_gradient, key_matrix, preferred_element_type=jnp.float32) / SOFTMAX_TEMP_SCALE
    ).astype(jnp.bfloat16)
    key_gradient_rows = (
        lax.dot_general(
            logit_gradient, query_rows, (((0,), (0,)), ((), ())), preferred_element_type=jnp.float32
        )
        / SOFTMAX_TEMP_SCALE
    ).astype(jnp.bfloat16)
    return jnp.stack([query_gradient, key_gradient_rows], axis=1)


def local(features, head_weight, bin_of_row, bin_owner, bin_link):
    rows_dev, views, feat_dim = features.shape
    part_rows, emb_dim = head_weight.shape
    sources = lax.axis_size("dp")
    bin_count = bin_owner.shape[0]
    per_bin = max(2, 2 * rows_dev // bin_count)
    per_owner = per_bin * MOSTB
    group_slots = sources * per_owner
    flat = features.reshape(rows_dev * views, feat_dim)
    columns = flat
    folded = jnp.dot(
        columns,
        lax.all_gather(head_weight, "bin", axis=0, tiled=True),
        preferred_element_type=jnp.float32,
    )
    embedded = folded.reshape(rows_dev, views, emb_dim)
    scale = lax.rsqrt(jnp.sum(embedded * embedded, axis=2, keepdims=True) + 1e-06)
    unit = embedded * scale
    sent = unit.astype(jnp.bfloat16)
    row_bins = bin_of_row[:, 0]
    lookup = row_bins[:, None] == jnp.arange(bin_count, dtype=jnp.int32)[None, :]
    owner = jnp.sum(jnp.where(lookup, bin_owner[None, :], 0), axis=1)
    first_by_bin = jnp.sum((bin_owner[None, :] < bin_owner[:, None]).astype(jnp.int32), axis=1)
    local_bin = row_bins - jnp.sum(jnp.where(lookup, first_by_bin[None, :], 0), axis=1)
    order = jnp.arange(rows_dev, dtype=jnp.int32)
    earlier = (row_bins[:, None] == row_bins[None, :]) & (order[None, :] < order[:, None])
    seat = jnp.sum(earlier.astype(jnp.int32), axis=1)
    target = owner * per_owner + local_bin * per_bin + seat
    outbox = jnp.zeros((group_slots, views, emb_dim), jnp.bfloat16).at[target].set(sent)
    filled = (
        jnp.zeros((group_slots,), jnp.bfloat16).at[target].set(jnp.ones((rows_dev,), jnp.bfloat16))
    )
    inbox, present = (
        lax.all_to_all(
            outbox.reshape(sources, per_owner, views, emb_dim),
            "dp",
            split_axis=0,
            concat_axis=0,
            tiled=True,
        ),
        lax.all_to_all(
            filled.reshape(sources, per_owner), "dp", split_axis=0, concat_axis=0, tiled=True
        ),
    )
    inbox = inbox.reshape(group_slots, views, emb_dim)
    valid = present.reshape(group_slots) > 0.5
    first = jnp.sum((bin_owner < lax.axis_index("dp")).astype(jnp.int32))
    allowed = allowed_mask(valid, first, bin_link, group_slots, per_bin)
    grads = contrast(inbox[:, 0], inbox[:, 1], allowed, valid.astype(jnp.float32))
    returned = lax.all_to_all(
        grads.reshape(sources, per_owner, views, emb_dim),
        "dp",
        split_axis=0,
        concat_axis=0,
        tiled=True,
    )
    row_grads = returned.reshape(group_slots, views, emb_dim)[target].astype(jnp.float32)
    grad_rows = (
        scale * (row_grads - unit * jnp.sum(unit * row_grads, axis=2, keepdims=True))
    ).astype(jnp.bfloat16)
    column_start = lax.axis_index("bin") * part_rows
    trunk = lax.all_gather(features, "bin", axis=0, tiled=True)
    outgrad = lax.all_gather(grad_rows, "bin", axis=0, tiled=True)
    columns = lax.dynamic_slice_in_dim(trunk, column_start, part_rows, 2)
    count = trunk.shape[0]
    local_grad = lax.dot_general(
        columns.reshape(count * views, part_rows),
        outgrad.reshape(count * views, emb_dim),
        (((0,), (0,)), ((), ())),
        preferred_element_type=jnp.float32,
    )
    grad_weight = lax.psum_scatter(local_grad, "dp", scatter_dimension=0, tiled=True) / rows_dev
    return (grad_rows, grad_weight)


def solution(mesh):
    return jax.shard_map(
        local,
        mesh=mesh,
        in_specs=(P(("dp", "bin"), None, None), P("bin", None), P(("dp", "bin"), None), P(), P()),
        out_specs=(P(("dp", "bin"), None, None), P(("bin", "dp"), None)),
        check_vma=False,
    )
```

profile of v0, /device:TPU:6, one launch (start us, length us, event | category | flops | bytes accessed | tf_op | source)
XLA Modules:
  0.0 725.5 jit_solution(15989342569008482530)
XLA Ops:
  7.2 0.0 all-gather.4.cloned.1.call-start
  7.2 0.7 all-gather.4.cloned.1.call-update
  7.9 0.9 convert_reduce_fusion.1
  8.8 0.9 convert_reduce_fusion
  9.8 0.8 select_reduce_fusion.1
  10.6 0.7 fusion.28
  11.2 1.3 scatter_custom_fusion
  12.6 0.8 all_to_all.16
  13.4 19.9 %all-to-all-start = ((bf16[128,1,4]{2,1,0:T(2,128)(2,1)}), bf16[128,1,4]{2,1,0:T(2,128)(2,1)S(1)}, u32[]{:S(2)}, u32[]{:S(2)}) async-start(bf16[128,1,4]{2,1,0:T(2,128)(2,1)} %all_to_all.16), calls=%async_computation | async-start | bytes 131072 | tf_op jit(solution)/shard_map/all_to_all | solution.py:93
  33.3 2.6 copy.35
  35.9 0.0 copy-start.1
  35.9 34.6 %all-gather.4.cloned.1.call-done = bf16[2048,1024]{1,0:T(8,128)(2,1)} async-done(((bf16[512,1024]{1,0:T(8,128)(2,1)}), bf16[2048,1024]{1,0:T(8,128)(2,1)}) %all-gather.4.cloned.1.call-update) | async-done | bytes 4194320 | tf_op jit(solution)/shard_map/all_gather | solution.py:65
  70.5 3.5 multiply_reduce_fusion
  74.1 0.0 copy-done.1
  74.1 0.1 multiply_convert_fusion.3
  74.2 1.3 copy.29
  75.5 1.1 broadcast_in_dim.68
  76.6 10.9 %scatter_fusion = bf16[512,2,1024]{2,1,0:T(2,128)(2,1)S(1)} fusion(bf16[512,2,1024]{2,1,0:T(2,128)(2,1)S(1)} %broadcast_in_dim.68, s32[128]{0:T(128)S(1)} %fusion.28, bf16[128,2,1024]{2,1,0:T(2,128)(2,1)} %copy.29), kind=kCustom, calls=%fused_computation.2 | custom fusion | bytes 1573376 | tf_op jit(solution)/shard_map/scatter | solution.py:81
  87.5 0.0 copy-start
  87.5 0.0 all-to-all-done
  87.5 1.3 copy-done
  88.8 0.0 copy-start.3
  88.8 0.0 copy-start.4
  88.9 17.2 %all-to-all-start.1 = ((bf16[128,4,2,1024]{3,2,1,0:T(2,128)(2,1)}), bf16[128,4,2,1024]{3,2,1,0:T(2,128)(2,1)S(1)}, u32[]{:S(2)}, u32[]{:S(2)}) async-start(bf16[128,4,2,1024]{3,2,1,0:T(2,128)(2,1)} %bitcast.47), calls=%async_computation.1 | async-start | bytes 4194304 | tf_op jit(solution)/shard_map/all_to_all | solution.py:86
  106.0 0.0 copy-done.3
  106.0 0.6 fusion.27
  108.6 0.0 copy-done.4
  108.6 0.1 pad_dynamic-slice_fusion
  108.7 0.6 fusion.35
  109.3 0.2 compare_reduce_fusion
  109.5 0.1 gt.22
  109.6 93.9 %all-to-all-done.1 = bf16[128,4,2,1024]{3,2,1,0:T(2,128)(2,1)S(1)} async-done(((bf16[128,4,2,1024]{3,2,1,0:T(2,128)(2,1)}), bf16[128,4,2,1024]{3,2,1,0:T(2,128)(2,1)S(1)}, u32[]{:S(2)}, u32[]{:S(2)}) %all-to-all-start.1) | async-done | bytes 2097184 | tf_op jit(solution)/shard_map/all_to_all | solution.py:86
  203.6 3.0 fusion.34
  206.5 2.7 fusion.36
  209.2 0.8 multiply_convert_fusion.1
  210.1 1.8 multiply_convert_fusion
  211.9 0.4 stack.9
  212.3 1.5 stack.10
  213.8 2.7 pad_maximum_fusion
  216.5 10.3 %all-to-all-start.2 = ((bf16[128,4,2,1024]{3,1,2,0:T(4,128)(2,1)}), bf16[128,4,2,1024]{3,1,2,0:T(4,128)(2,1)S(1)}, u32[]{:S(2)}, u32[]{:S(2)}) async-start(bf16[128,4,2,1024]{3,1,2,0:T(4,128)(2,1)} %pad_maximum_fusion), calls=%async_computation.2 | async-start | bytes 4194304 | tf_op jit(solution)/shard_map/all_to_all | solution.py:102
  226.8 0.0 all-gather.6.cloned.1.call-start
  226.8 0.7 all-gather.6.cloned.1.call-update
  227.5 0.0 all-gather.8.cloned.1.call-start
  227.6 96.7 %all-to-all-done.2 = bf16[128,4,2,1024]{3,1,2,0:T(4,128)(2,1)S(1)} async-done(((bf16[128,4,2,1024]{3,1,2,0:T(4,128)(2,1)}), bf16[128,4,2,1024]{3,1,2,0:T(4,128)(2,1)S(1)}, u32[]{:S(2)}, u32[]{:S(2)}) %all-to-all-start.2) | async-done | bytes 2097184 | tf_op jit(solution)/shard_map/all_to_all | solution.py:102
  324.3 3.7 copy.33
  328.0 3.2 gather_fusion
  331.2 2.1 fusion.9
  333.3 0.0 all-gather.8.cloned.1.call-update
  333.3 0.0 all-reduce.4.cloned.1.call-start
  333.4 0.0 all-gather.6.cloned.1.call-done
  333.4 32.3 %all-gather.8.cloned.1.call-done = bf16[512,2,1024]{2,0,1:T(8,128)(2,1)} async-done(((bf16[128,2,1024]{2,0,1:T(8,128)(2,1)}), bf16[512,2,1024]{2,0,1:T(8,128)(2,1)}) %all-gather.8.cloned.1.call-update) | async-done | bytes 2097168 | tf_op jit(solution)/shard_map/all_gather | solution.py:115
  365.8 4.5 convolution_bitcast_fusion
  370.3 0.0 copy-start.2
  370.3 0.0 all-reduce.4.cloned.1.call-update
  370.3 1.3 dynamic-slice
  372.3 0.0 copy-done.2
  372.3 1.3 copy.36
  373.6 344.0 %all-reduce.4.cloned.1.call-done = f32[512,1024]{1,0:T(8,128)} async-done(((f32[512,1024]{1,0:T(8,128)}), f32[512,1024]{1,0:T(8,128)}) %all-reduce.4.cloned.1.call-update) | async-done | bytes 2097168
  717.6 1.4 dynamic-slice_multiply_fusion
  (5 shorter events, 0.0 us)
Async XLA Ops:
  7.2 63.3 %all-gather.4.cloned.1.call-start = ((), (), s32[]{:S(2)}) async-start(), calls=%async_computation.3 | async-start | bytes 5242880 | tf_op jit(solution)/shard_map/all_gather | solution.py:65
  13.4 74.2 %all-to-all-start = ((bf16[128,1,4]{2,1,0:T(2,128)(2,1)}), bf16[128,1,4]{2,1,0:T(2,128)(2,1)S(1)}, u32[]{:S(2)}, u32[]{:S(2)}) async-start(bf16[128,1,4]{2,1,0:T(2,128)(2,1)} %all_to_all.16), calls=%async_computation | async-start | bytes 131072 | tf_op jit(solution)/shard_map/all_to_all | solution.py:93
  35.9 38.2 %copy-start.1 = (bf16[128,2,2048]{0,2,1:T(8,128)(2,1)}, bf16[128,2,2048]{0,2,1:T(8,128)(2,1)S(1)}, u32[]{:S(2)}) copy-start(bf16[128,2,2048]{0,2,1:T(8,128)(2,1)S(1)} %copy.35) | copy-start | bytes 3145732
  87.5 1.4 copy-start
  88.8 17.2 %copy-start.3 = (s32[192]{0:T(256)S(1)}, s32[192]{0:T(256)}, u32[]{:S(2)}) copy-start(s32[192]{0:T(256)} %param.8) | copy-start | bytes 2308
  88.8 19.8 %copy-start.4 = (s32[192]{0:T(256)S(1)}, s32[192]{0:T(256)}, u32[]{:S(2)}) copy-start(s32[192]{0:T(256)} %param.9) | copy-start | bytes 2308
  88.9 114.7 %all-to-all-start.1 = ((bf16[128,4,2,1024]{3,2,1,0:T(2,128)(2,1)}), bf16[128,4,2,1024]{3,2,1,0:T(2,128)(2,1)S(1)}, u32[]{:S(2)}, u32[]{:S(2)}) async-start(bf16[128,4,2,1024]{3,2,1,0:T(2,128)(2,1)} %bitcast.47), calls=%async_computation.1 | async-start | bytes 4194304 | tf_op jit(solution)/shard_map/all_to_all | solution.py:86
  216.5 107.8 %all-to-all-start.2 = ((bf16[128,4,2,1024]{3,1,2,0:T(4,128)(2,1)}), bf16[128,4,2,1024]{3,1,2,0:T(4,128)(2,1)S(1)}, u32[]{:S(2)}, u32[]{:S(2)}) async-start(bf16[128,4,2,1024]{3,1,2,0:T(4,128)(2,1)} %pad_maximum_fusion), calls=%async_computation.2 | async-start | bytes 4194304 | tf_op jit(solution)/shard_map/all_to_all | solution.py:102
  226.8 106.7 %all-gather.6.cloned.1.call-start = ((), (), s32[]{:S(2)}) async-start(), calls=%async_computation.4 | async-start | bytes 5242880 | tf_op jit(solution)/shard_map/all_gather | solution.py:114
  227.5 138.3 %all-gather.8.cloned.1.call-start = ((), (), s32[]{:S(2)}) async-start(), calls=%async_computation.5 | async-start | bytes 2621440 | tf_op jit(solution)/shard_map/all_gather | solution.py:115
  333.3 384.3 %all-reduce.4.cloned.1.call-start = ((), (), s32[]{:S(2)}) async-start(), calls=%async_computation.6 | async-start | bytes 4194304
  370.3 2.0 copy-start.2
Sparse Core Ops, SparseCore 0:
  10.1 60.3 all-gather.3
  229.7 59.2 all-gather.5
  333.5 32.2 all-gather.7
  370.4 347.1 all-reduce.3
where the time goes:
time: 728 us; the launch traced here: 726 us
  waiting for transfers between devices  603 us (83%)
  starting transfers between devices  47.5 us (7%)
  local copies, waits for them, and re-layouts  34.5 us (5%)
  between operations  16.6 us (2%)
  matrix products  13.4 us (2%)
  other arithmetic  10.5 us (1%)
    unnamed x5, waiting for transfers between devices  345 us
    all_to_all x1, waiting for transfers between devices, local(): lax.all_to_all(grads.reshape(sources, per_owner, views, emb_dim), 'dp', s...  96.7 us
    all_to_all x1, waiting for transfers between devices, local(): lax.all_to_all(outbox.reshape(sources, per_owner, views, emb_dim), 'dp',...  93.9 us
    all_gather x1, waiting for transfers between devices, local(): lax.all_gather(head_weight, 'bin', axis=0, tiled=True)  34.6 us
    all_gather x1, waiting for transfers between devices, local(): outgrad = lax.all_gather(grad_rows, 'bin', axis=0, tiled=True)  32.3 us
    all_to_all x1, starting transfers between devices, local(): lax.all_to_all(filled.reshape(sources, per_owner), 'dp', split_axis=0, co...  19.9 us
    all_to_all x1, starting transfers between devices, local(): lax.all_to_all(outbox.reshape(sources, per_owner, views, emb_dim), 'dp',...  17.2 us
  transfers between devices with their start and end apart: 7, of which 5 were waited for; matrix products, arithmetic and copies ran while one was open for 5% of the time, Pallas kernels for 0%

commit v1 on v0

--- a/solution.py
+++ b/solution.py
@@ -1,12 +1,17 @@
 import jax
 import jax.numpy as jnp
 from jax import lax
+from jax.sharding import Mesh
 from jax.sharding import PartitionSpec as P
 
 MOSTB = 2
 
 
 SOFTMAX_TEMP_SCALE = 0.1
+
+DP_PARTS = (("dx", 4), ("dz", 16), ("dc", 2))
+DP = tuple(name for name, _ in DP_PARTS)
+EMPTY_MARK = 4.0
 
 
 def allowed_mask(valid, first, bin_link, group_slots, per_bin):
@@ -50,18 +55,27 @@
     return jnp.stack([query_gradient, key_gradient_rows], axis=1)
 
 
+def dp_index():
+    index = 0
+    for name, size in DP_PARTS:
+        index = index * size + lax.axis_index(name)
+    return index
+
+
 def local(features, head_weight, bin_of_row, bin_owner, bin_link):
     rows_dev, views, feat_dim = features.shape
     part_rows, emb_dim = head_weight.shape
-    sources = lax.axis_size("dp")
+    sources = 1
+    for _, size in DP_PARTS:
+        sources *= size
+    bins_n = lax.axis_size("bin")
     bin_count = bin_owner.shape[0]
     per_bin = max(2, 2 * rows_dev // bin_count)
     per_owner = per_bin * MOSTB
     group_slots = sources * per_owner
     flat = features.reshape(rows_dev * views, feat_dim)
-    columns = flat
     folded = jnp.dot(
-        columns,
+        flat,
         lax.all_gather(head_weight, "bin", axis=0, tiled=True),
         preferred_element_type=jnp.float32,
     )
@@ -78,30 +92,24 @@
     earlier = (row_bins[:, None] == row_bins[None, :]) & (order[None, :] < order[:, None])
     seat = jnp.sum(earlier.astype(jnp.int32), axis=1)
     target = owner * per_owner + local_bin * per_bin + seat
-    outbox = jnp.zeros((group_slots, views, emb_dim), jnp.bfloat16).at[target].set(sent)
-    filled = (
-        jnp.zeros((group_slots,), jnp.bfloat16).at[target].set(jnp.ones((rows_dev,), jnp.bfloat16))
-    )
-    inbox, present = (
-        lax.all_to_all(
-            outbox.reshape(sources, per_owner, views, emb_dim),
-            "dp",
-            split_axis=0,
-            concat_axis=0,
-            tiled=True,
-        ),
-        lax.all_to_all(
-            filled.reshape(sources, per_owner), "dp", split_axis=0, concat_axis=0, tiled=True
-        ),
+    empty = jnp.zeros((group_slots, views, emb_dim), jnp.bfloat16).at[:, 0, 0].set(EMPTY_MARK)
+    outbox = empty.at[target].set(sent)
+    inbox = lax.all_to_all(
+        outbox.reshape(sources, per_owner, views, emb_dim),
+        DP,
+        split_axis=0,
+        concat_axis=0,
+        tiled=True,
     )
     inbox = inbox.reshape(group_slots, views, emb_dim)
-    valid = present.reshape(group_slots) > 0.5
-    first = jnp.sum((bin_owner < lax.axis_index("dp")).astype(jnp.int32))
+    valid = inbox[:, 0, 0] < 2.0
+    inbox = jnp.where(valid[:, None, None], inbox, jnp.zeros_like(inbox))
+    first = jnp.sum((bin_owner < dp_index()).astype(jnp.int32))
     allowed = allowed_mask(valid, first, bin_link, group_slots, per_bin)
     grads = contrast(inbox[:, 0], inbox[:, 1], allowed, valid.astype(jnp.float32))
     returned = lax.all_to_all(
         grads.reshape(sources, per_owner, views, emb_dim),
-        "dp",
+        DP,
         split_axis=0,
         concat_axis=0,
         tiled=True,
@@ -110,26 +118,38 @@
     grad_rows = (
         scale * (row_grads - unit * jnp.sum(unit * row_grads, axis=2, keepdims=True))
     ).astype(jnp.bfloat16)
-    column_start = lax.axis_index("bin") * part_rows
-    trunk = lax.all_gather(features, "bin", axis=0, tiled=True)
+    columns = lax.all_to_all(
+        features.reshape(rows_dev, views, bins_n, part_rows),
+        "bin",
+        split_axis=2,
+        concat_axis=0,
+        tiled=True,
+    )
     outgrad = lax.all_gather(grad_rows, "bin", axis=0, tiled=True)
-    columns = lax.dynamic_slice_in_dim(trunk, column_start, part_rows, 2)
-    count = trunk.shape[0]
+    count = columns.shape[0]
+    sizes = [size for _, size in DP_PARTS]
+    columns = columns.reshape(count * views, *sizes, part_rows // sources)
+    columns = jnp.transpose(columns, (0, 3, 2, 1, 4)).reshape(count * views, part_rows)
     local_grad = lax.dot_general(
-        columns.reshape(count * views, part_rows),
+        columns,
         outgrad.reshape(count * views, emb_dim),
         (((0,), (0,)), ((), ())),
         preferred_element_type=jnp.float32,
     )
-    grad_weight = lax.psum_scatter(local_grad, "dp", scatter_dimension=0, tiled=True) / rows_dev
+    for name in ("dc", "dz", "dx"):
+        local_grad = lax.psum_scatter(local_grad, name, scatter_dimension=0, tiled=True)
+    grad_weight = local_grad / rows_dev
     return (grad_rows, grad_weight)
 
 
 def solution(mesh):
+    sizes = [size for _, size in DP_PARTS]
+    devices = mesh.devices.reshape(*sizes, mesh.devices.shape[1])
+    parted = Mesh(devices, (*DP, "bin"))
     return jax.shard_map(
         local,
-        mesh=mesh,
-        in_specs=(P(("dp", "bin"), None, None), P("bin", None), P(("dp", "bin"), None), P(), P()),
-        out_specs=(P(("dp", "bin"), None, None), P(("bin", "dp"), None)),
+        mesh=parted,
+        in_specs=(P((*DP, "bin"), None, None), P("bin", None), P((*DP, "bin"), None), P(), P()),
+        out_specs=(P((*DP, "bin"), None, None), P(("bin", *DP), None)),
         check_vma=False,
     )

time: 728 us -> 663 us (0.911)
  waiting for transfers between devices: 603 us -> 388 us
  local copies, waits for them, and re-layouts: 34.5 us -> 181 us
  blocking collectives: 0 us -> 23.2 us
  starting transfers between devices: 47.5 us -> 27.9 us
    unnamed x5 -> x7, waiting for transfers between devices: 345 us -> 125 us
    reshape x0 -> x5, local copies, waits for them, and re-layouts: none -> 77 us  [the longest x1 73.1 us: local(): columns = columns.reshape(count * views, *sizes, part_rows // sources)]
    transpose x0 -> x1, local copies, waits for them, and re-layouts: none -> 76.1 us  [local(): jnp.transpose(columns, (0, 3, 2, 1, 4)).reshape(count * views, part_rows)]
    all_gather x1, waiting for transfers between devices: 32.3 us -> 0.02 us  [local(): outgrad = lax.all_gather(grad_rows, 'bin', axis=0, tiled=True)]
    all_gather x1, waiting for transfers between devices: 34.6 us -> 59.3 us  [local(): lax.all_gather(head_weight, 'bin', axis=0, tiled=True)]
    all_to_all x0 -> x1, blocking collectives: none -> 23.2 us  [local(): lax.all_to_all(features.reshape(rows_dev, views, bins_n, part_rows), 'bin...]
    all_to_all x3 -> x2, starting transfers between devices: 47.4 us -> 27.7 us  [the longest x1 17.2 us: local(): lax.all_to_all(outbox.reshape(sources, per_owner, views, emb_dim), DP, sp...]
    reduce_scatter x0 -> x1, waiting for transfers between devices: none -> 12.3 us  [local(): lax.psum_scatter(local_grad, name, scatter_dimension=0, tiled=True)]
  transfers between devices with their start and end apart: 7 -> 7, of which waited for: 5 -> 6; matrix products, arithmetic and copies ran while one was open for 5% -> 24% of each run, Pallas kernels for 0% -> 0%
where the time goes in v1:
time: 663 us; the launch traced here: 660 us
  waiting for transfers between devices  388 us (59%)
  local copies, waits for them, and re-layouts  181 us (27%)
  starting transfers between devices  27.9 us (4%)
  blocking collectives  23.2 us (3%)
  between operations  16.6 us (3%)
  matrix products  12.3 us (2%)
  other arithmetic  10.7 us (2%)
    unnamed x7, waiting for transfers between devices  125 us
    all_to_all x1, waiting for transfers between devices, local(): lax.all_to_all(grads.reshape(sources, per_owner, views, emb_dim), DP, spl...  97.4 us
    all_to_all x1, waiting for transfers between devices, local(): lax.all_to_all(outbox.reshape(sources, per_owner, views, emb_dim), DP, sp...  94.2 us
    transpose x1, local copies, waits for them, and re-layouts, local(): jnp.transpose(columns, (0, 3, 2, 1, 4)).reshape(count * views, part_rows)  76.1 us
    reshape x1, local copies, waits for them, and re-layouts, local(): columns = columns.reshape(count * views, *sizes, part_rows // sources)  73.1 us
    all_gather x1, waiting for transfers between devices, local(): lax.all_gather(head_weight, 'bin', axis=0, tiled=True)  59.3 us
    all_to_all x1, blocking collectives, local(): lax.all_to_all(features.reshape(rows_dev, views, bins_n, part_rows), 'bin...  23.2 us
    all_to_all x1, starting transfers between devices, local(): lax.all_to_all(outbox.reshape(sources, per_owner, views, emb_dim), DP, sp...  17.2 us
  transfers between devices with their start and end apart: 7, of which 6 were waited for; matrix products, arithmetic and copies ran while one was open for 24% of the time, Pallas kernels for 0%

profile of v1, /device:TPU:6, one launch (start us, length us, event | category | flops | bytes accessed | tf_op | source)
XLA Modules:
  0.0 660.2 jit_solution(16799873341460603890)
XLA Ops:
  7.2 0.0 all-gather.3.cloned.1.call-start
  7.2 0.7 all-gather.3.cloned.1.call-update
  7.9 0.9 convert_reduce_fusion.1
  8.8 0.9 convert_reduce_fusion
  9.8 0.8 select_reduce_fusion.1
  10.6 0.7 fusion.28
  11.2 59.3 %all-gather.3.cloned.1.call-done = bf16[2048,1024]{1,0:T(8,128)(2,1)} async-done(((bf16[512,1024]{1,0:T(8,128)(2,1)}), bf16[2048,1024]{1,0:T(8,128)(2,1)}) %all-gather.3.cloned.1.call-update) | async-done | bytes 4194320 | tf_op jit(solution)/shard_map/all_gather | solution.py:79
  70.5 3.9 multiply_reduce_fusion
  74.4 0.0 copy-start.6
  74.4 0.1 multiply_convert_fusion.3
  74.6 0.8 copy-done.3
  75.4 0.5 copy.33
  75.9 1.1 scatter.12
  77.0 4.3 scatter_fusion
  81.3 1.3 copy-done
  82.7 17.2 %all-to-all-start = ((bf16[128,4,2,1024]{3,2,1,0:T(2,128)(2,1)}), bf16[128,4,2,1024]{3,2,1,0:T(2,128)(2,1)S(1)}, u32[]{:S(2)}, u32[]{:S(2)}) async-start(bf16[128,4,2,1024]{3,2,1,0:T(2,128)(2,1)} %bitcast.64), calls=%async_computation | async-start | bytes 4194304 | tf_op jit(solution)/shard_map/all_to_all | solution.py:97
  99.9 0.0 copy-done.5
  99.9 0.6 fusion.27
  102.4 0.0 copy-done.7
  102.5 0.1 pad_dynamic-slice_fusion
  102.5 0.6 fusion.31
  103.1 94.2 %all-to-all-done = bf16[128,4,2,1024]{3,2,1,0:T(2,128)(2,1)S(1)} async-done(((bf16[128,4,2,1024]{3,2,1,0:T(2,128)(2,1)}), bf16[128,4,2,1024]{3,2,1,0:T(2,128)(2,1)S(1)}, u32[]{:S(2)}, u32[]{:S(2)}) %all-to-all-start) | async-done | bytes 2097184 | tf_op jit(solution)/shard_map/all_to_all | solution.py:97
  197.3 0.6 copy.44
  198.0 0.2 compare_reduce_fusion
  198.1 0.4 broadcast_select_fusion
  198.5 2.7 fusion.32
  201.2 0.8 multiply_convert_fusion.1
  202.0 0.7 multiply_convert_fusion
  202.7 0.4 stack.9
  203.1 0.4 stack.10
  203.6 2.7 pad_maximum_fusion
  206.3 10.5 %all-to-all-start.1 = ((bf16[128,4,2,1024]{3,1,2,0:T(4,128)(2,1)}), bf16[128,4,2,1024]{3,1,2,0:T(4,128)(2,1)S(1)}, u32[]{:S(2)}, u32[]{:S(2)}) async-start(bf16[128,4,2,1024]{3,1,2,0:T(4,128)(2,1)} %pad_maximum_fusion), calls=%async_computation.1 | async-start | bytes 4194304 | tf_op jit(solution)/shard_map/all_to_all | solution.py:110
  216.8 0.0 all-gather.5.cloned.1.call-start
  216.9 0.0 copy-start.4
  216.9 97.4 %all-to-all-done.1 = bf16[128,4,2,1024]{3,1,2,0:T(4,128)(2,1)S(1)} async-done(((bf16[128,4,2,1024]{3,1,2,0:T(4,128)(2,1)}), bf16[128,4,2,1024]{3,1,2,0:T(4,128)(2,1)S(1)}, u32[]{:S(2)}, u32[]{:S(2)}) %all-to-all-start.1) | async-done | bytes 2097184 | tf_op jit(solution)/shard_map/all_to_all | solution.py:110
  314.3 3.8 copy.37
  318.1 3.3 gather_fusion
  321.4 2.1 fusion.9
  323.5 0.0 all-gather.5.cloned.1.call-update
  323.5 0.0 reduce-scatter.6.cloned.1.call-start
  323.6 0.7 copy.61
  324.3 23.2 %all_to_all.25 = bf16[128,2,4,512]{3,1,0,2:T(2,128)(2,1)S(1)} all-to-all(bf16[128,2,4,512]{3,1,0,2:T(2,128)(2,1)S(1)} %bitcast.66), channel_id=1, replica_groups=mesh['dx'=4,'dz'=16,'dc'=2,'bin'=4] {'bin'}, dimensions={2} | all-to-all | bytes 2097152 | tf_op jit(solution)/shard_map/all_to_all | solution.py:121
  347.5 73.1 %reshape.155 = bf16[1024,4,16,2,4]{4,3,2,1,0:T(2,128)(2,1)} reshape(bf16[4,128,2,1,512]{4,2,1,0,3:T(2,128)(2,1)S(1)} %bitcast.65) | data formatting | bytes 2097152 | tf_op jit(solution)/shard_map/reshape | solution.py:131
  420.6 76.1 %copy.41 = bf16[1024,2,16,4,4]{0,4,3,2,1:T(4,128)(2,1)S(1)} copy(bf16[1024,2,16,4,4]{4,1,2,3,0:T(2,128)(2,1)} %bitcast.61) | data formatting | bytes 2097152 | tf_op jit(solution)/shard_map/transpose | solution.py:132
  496.7 0.3 reshape.156
  497.0 0.0 all-gather.5.cloned.1.call-done
  497.0 3.7 copy.39
  500.8 2.2 reshape.153
  503.1 4.2 convolution_bitcast_fusion
  507.3 0.0 reduce-scatter.6.cloned.1.call-update
  507.3 0.0 copy-start.1
  507.3 0.0 reduce-scatter.8.cloned.1.call-start
  507.4 12.3 %reduce-scatter.6.cloned.1.call-done = f32[256,1024]{0,1:T(8,128)} async-done(((f32[512,1024]{0,1:T(8,128)}), f32[256,1024]{0,1:T(8,128)}) %reduce-scatter.6.cloned.1.call-update) | async-done | bytes 1048592 | tf_op jit(solution)/shard_map/reduce_scatter | solution.py:140
  519.6 2.5 copy.45
  522.2 0.0 reduce-scatter.8.cloned.1.call-update
  522.2 0.0 all-reduce.4.cloned.1.call-start
  522.3 72.1 %reduce-scatter.8.cloned.1.call-done = f32[16,1024]{1,0:T(8,128)} async-done(((f32[256,1024]{1,0:T(8,128)}), f32[16,1024]{1,0:T(8,128)}) %reduce-scatter.8.cloned.1.call-update) | async-done | bytes 65552
  594.3 1.8 copy.46
  596.2 0.0 all-reduce.4.cloned.1.call-update
  596.2 1.3 dynamic-slice.6
  598.1 1.3 copy.42
  599.5 52.2 %all-reduce.4.cloned.1.call-done = f32[16,1024]{0,1:T(8,128)} async-done(((f32[16,1024]{0,1:T(8,128)}), f32[16,1024]{0,1:T(8,128)}) %all-reduce.4.cloned.1.call-update) | async-done | bytes 65552
  651.6 1.2 dynamic-slice_multiply_fusion
  652.9 0.8 copy.43
  (13 shorter events, 0.0 us)
Async XLA Ops:
  7.2 63.3 %all-gather.3.cloned.1.call-start = ((), (), s32[]{:S(2)}) async-start(), calls=%async_computation.5 | async-start | bytes 5242880 | tf_op jit(solution)/shard_map/all_gather | solution.py:79
  74.4 1.0 copy-start.3
  74.4 1.5 copy-start.6
  81.3 1.4 copy-start
  82.7 17.2 %copy-start.5 = (s32[192]{0:T(256)S(1)}, s32[192]{0:T(256)}, u32[]{:S(2)}) copy-start(s32[192]{0:T(256)} %param.10) | copy-start | bytes 2308
  82.7 19.8 %copy-start.7 = (s32[192]{0:T(256)S(1)}, s32[192]{0:T(256)}, u32[]{:S(2)}) copy-start(s32[192]{0:T(256)} %param.11) | copy-start | bytes 2308
  82.7 114.6 %all-to-all-start = ((bf16[128,4,2,1024]{3,2,1,0:T(2,128)(2,1)}), bf16[128,4,2,1024]{3,2,1,0:T(2,128)(2,1)S(1)}, u32[]{:S(2)}, u32[]{:S(2)}) async-start(bf16[128,4,2,1024]{3,2,1,0:T(2,128)(2,1)} %bitcast.64), calls=%async_computation | async-start | bytes 4194304 | tf_op jit(solution)/shard_map/all_to_all | solution.py:97
  206.3 108.0 %all-to-all-start.1 = ((bf16[128,4,2,1024]{3,1,2,0:T(4,128)(2,1)}), bf16[128,4,2,1024]{3,1,2,0:T(4,128)(2,1)S(1)}, u32[]{:S(2)}, u32[]{:S(2)}) async-start(bf16[128,4,2,1024]{3,1,2,0:T(4,128)(2,1)} %pad_maximum_fusion), calls=%async_computation.1 | async-start | bytes 4194304 | tf_op jit(solution)/shard_map/all_to_all | solution.py:110
  216.8 280.2 %all-gather.5.cloned.1.call-start = ((), (), s32[]{:S(2)}) async-start(), calls=%async_computation.6 | async-start | bytes 2621440 | tf_op jit(solution)/shard_map/all_gather | solution.py:128
  216.9 104.5 %copy-start.4 = (f32[128,2,1024]{2,0,1:T(8,128)S(1)}, f32[128,2,1024]{2,0,1:T(8,128)}, u32[]{:S(2)}) copy-start(f32[128,2,1024]{2,0,1:T(8,128)} %copy-done.3) | copy-start | bytes 3145732
  318.1 5.5 copy-start.2
  323.5 196.1 %reduce-scatter.6.cloned.1.call-start = ((), (), s32[]{:S(2)}) async-start(), calls=%async_computation.7 | async-start | bytes 3145728 | tf_op jit(solution)/shard_map/reduce_scatter | solution.py:140
  507.3 90.8 %copy-start.1 = (bf16[128,2,1024]{2,0,1:T(8,128)(2,1)S(1)}, bf16[128,2,1024]{2,0,1:T(8,128)(2,1)}, u32[]{:S(2)}) copy-start(bf16[128,2,1024]{2,0,1:T(8,128)(2,1)} %fusion.9) | copy-start | bytes 1572868
  507.3 87.0 %reduce-scatter.8.cloned.1.call-start = ((), (), s32[]{:S(2)}) async-start(), calls=%async_computation.8 | async-start | bytes 1114112
  522.2 129.4 %all-reduce.4.cloned.1.call-start = ((), (), s32[]{:S(2)}) async-start(), calls=%async_computation.9 | async-start | bytes 1048576
Sparse Core Ops, SparseCore 0:
  10.1 60.3 all-gather.2
  323.6 35.8 all-gather.4
  507.4 12.1 reduce-scatter.5
  522.5 71.7 reduce-scatter.7
  596.5 55.0 all-reduce.3

commit v2 on v1

--- a/solution.py
+++ b/solution.py
@@ -118,26 +118,26 @@
     grad_rows = (
         scale * (row_grads - unit * jnp.sum(unit * row_grads, axis=2, keepdims=True))
     ).astype(jnp.bfloat16)
-    columns = lax.all_to_all(
-        features.reshape(rows_dev, views, bins_n, part_rows),
-        "bin",
-        split_axis=2,
-        concat_axis=0,
-        tiled=True,
-    )
+    column_start = lax.axis_index("bin") * part_rows
+    trunk = lax.all_gather(features, "bin", axis=0, tiled=True)
     outgrad = lax.all_gather(grad_rows, "bin", axis=0, tiled=True)
-    count = columns.shape[0]
-    sizes = [size for _, size in DP_PARTS]
-    columns = columns.reshape(count * views, *sizes, part_rows // sources)
-    columns = jnp.transpose(columns, (0, 3, 2, 1, 4)).reshape(count * views, part_rows)
+    columns = lax.dynamic_slice_in_dim(trunk, column_start, part_rows, 2)
+    count = trunk.shape[0]
     local_grad = lax.dot_general(
-        columns,
+        columns.reshape(count * views, part_rows),
         outgrad.reshape(count * views, emb_dim),
         (((0,), (0,)), ((), ())),
         preferred_element_type=jnp.float32,
     )
-    for name in ("dc", "dz", "dx"):
-        local_grad = lax.psum_scatter(local_grad, name, scatter_dimension=0, tiled=True)
+    sizes = [size for _, size in DP_PARTS]
+    per_dev = part_rows // sources
+    local_grad = jnp.transpose(local_grad.reshape(*sizes, per_dev, emb_dim), (2, 0, 1, 3, 4))
+    local_grad = lax.psum_scatter(
+        local_grad.reshape(part_rows, emb_dim), "dc", scatter_dimension=0, tiled=True
+    )
+    planes = local_grad.reshape(sizes[0] * sizes[1], per_dev, emb_dim).astype(jnp.bfloat16)
+    planes = lax.all_to_all(planes, ("dx", "dz"), split_axis=0, concat_axis=0, tiled=True)
+    local_grad = jnp.sum(planes.astype(jnp.float32), axis=0)
     grad_weight = local_grad / rows_dev
     return (grad_rows, grad_weight)
 

time: 663 us -> 447 us (0.67)
  local copies, waits for them, and re-layouts: 181 us -> 32.1 us
  waiting for transfers between devices: 388 us -> 332 us
  blocking collectives: 23.2 us -> 0 us
  starting transfers between devices: 27.9 us -> 43.8 us
    unnamed x7 -> x4, waiting for transfers between devices: 125 us -> 1.41 us
    transpose x1, local copies, waits for them, and re-layouts: 76.1 us -> 1.36 us  [local(): jnp.transpose(local_grad.reshape(*sizes, per_dev, emb_dim), (2, 0, 1, 3, 4))]
    reshape x3 -> x2, local copies, waits for them, and re-layouts: 74.1 us -> 2.23 us  [the longest x1 1.79 us: local(): local_grad.reshape(part_rows, emb_dim)]
    all_to_all x0 -> x1, waiting for transfers between devices: none -> 30.9 us  [local(): lax.all_to_all(planes, ('dx', 'dz'), split_axis=0, concat_axis=0, tiled=T...]
    all_gather x1, waiting for transfers between devices: 0.02 us -> 29 us  [local(): outgrad = lax.all_gather(grad_rows, 'bin', axis=0, tiled=True)]
    all_to_all x1 -> x0, blocking collectives: 23.2 us -> none  [local(): lax.all_to_all(features.reshape(rows_dev, views, bins_n, part_rows), 'bin...]
    all_to_all x0 -> x1, starting transfers between devices: none -> 15.9 us  [local(): lax.all_to_all(planes, ('dx', 'dz'), split_axis=0, concat_axis=0, tiled=T...]
    reduce_scatter x1, waiting for transfers between devices: 12.3 us -> 20.3 us  [local(): lax.psum_scatter(local_grad.reshape(part_rows, emb_dim), 'dc', scatter_di...]
  transfers between devices with their start and end apart: 7 -> 7, of which waited for: 6 -> 6; matrix products, arithmetic and copies ran while one was open for 24% -> 4% of each run, Pallas kernels for 0% -> 0%
where the time goes in v2:
time: 447 us; the launch traced here: 446 us
  waiting for transfers between devices  332 us (74%)
  starting transfers between devices  43.8 us (10%)
  local copies, waits for them, and re-layouts  32.1 us (7%)
  between operations  16 us (4%)
  other arithmetic  11.6 us (3%)
  matrix products  11.1 us (2%)
    all_to_all x1, waiting for transfers between devices, local(): lax.all_to_all(grads.reshape(sources, per_owner, views, emb_dim), DP, spl...  96.7 us
    all_to_all x1, waiting for transfers between devices, local(): lax.all_to_all(outbox.reshape(sources, per_owner, views, emb_dim), DP, sp...  94.2 us
    all_gather x1, waiting for transfers between devices, local(): lax.all_gather(head_weight, 'bin', axis=0, tiled=True)  59.3 us
    all_to_all x1, waiting for transfers between devices, local(): lax.all_to_all(planes, ('dx', 'dz'), split_axis=0, concat_axis=0, tiled=T...  30.9 us
    all_gather x1, waiting for transfers between devices, local(): outgrad = lax.all_gather(grad_rows, 'bin', axis=0, tiled=True)  29 us
    reduce_scatter x1, waiting for transfers between devices, local(): lax.psum_scatter(local_grad.reshape(part_rows, emb_dim), 'dc', scatter_di...  20.3 us
    all_to_all x1, starting transfers between devices, local(): lax.all_to_all(outbox.reshape(sources, per_owner, views, emb_dim), DP, sp...  17.2 us
    all_to_all x1, starting transfers between devices, local(): lax.all_to_all(planes, ('dx', 'dz'), split_axis=0, concat_axis=0, tiled=T...  15.9 us
  transfers between devices with their start and end apart: 7, of which 6 were waited for; matrix products, arithmetic and copies ran while one was open for 4% of the time, Pallas kernels for 0%

profile of v2, /device:TPU:6, one launch (start us, length us, event | category | flops | bytes accessed | tf_op | source)
XLA Modules:
  0.0 446.2 jit_solution(5971562317251444942)
XLA Ops:
  7.2 0.0 all-gather.4.cloned.1.call-start
  7.2 0.7 all-gather.4.cloned.1.call-update
  7.9 0.9 convert_reduce_fusion.2
  8.8 0.9 convert_reduce_fusion.1
  9.8 0.8 select_reduce_fusion.1
  10.6 0.7 fusion.34
  11.2 59.3 %all-gather.4.cloned.1.call-done = bf16[2048,1024]{1,0:T(8,128)(2,1)} async-done(((bf16[512,1024]{1,0:T(8,128)(2,1)}), bf16[2048,1024]{1,0:T(8,128)(2,1)}) %all-gather.4.cloned.1.call-update) | async-done | bytes 4194320 | tf_op jit(solution)/shard_map/all_gather | solution.py:79
  70.5 3.9 multiply_reduce_fusion
  74.4 0.0 copy-start.2
  74.4 0.0 copy-start.5
  74.4 0.1 multiply_convert_fusion.3
  74.6 0.8 copy-done.2
  75.4 0.5 copy.41
  76.0 0.0 copy-done.5
  76.0 1.1 scatter.12
  77.1 4.4 scatter_fusion
  81.4 0.0 copy-start
  81.4 1.3 copy-done
  82.8 17.2 %all-to-all-start = ((bf16[128,4,2,1024]{3,2,1,0:T(2,128)(2,1)}), bf16[128,4,2,1024]{3,2,1,0:T(2,128)(2,1)S(1)}, u32[]{:S(2)}, u32[]{:S(2)}) async-start(bf16[128,4,2,1024]{3,2,1,0:T(2,128)(2,1)} %bitcast.52), calls=%async_computation | async-start | bytes 4194304 | tf_op jit(solution)/shard_map/all_to_all | solution.py:97
  100.0 0.6 fusion.33
  102.5 0.0 copy-done.6
  102.5 0.1 pad_dynamic-slice_fusion
  102.6 0.6 fusion.37
  103.2 94.2 %all-to-all-done = bf16[128,4,2,1024]{3,2,1,0:T(2,128)(2,1)S(1)} async-done(((bf16[128,4,2,1024]{3,2,1,0:T(2,128)(2,1)}), bf16[128,4,2,1024]{3,2,1,0:T(2,128)(2,1)S(1)}, u32[]{:S(2)}, u32[]{:S(2)}) %all-to-all-start) | async-done | bytes 2097184 | tf_op jit(solution)/shard_map/all_to_all | solution.py:97
  197.4 0.6 copy.53
  198.0 0.2 compare_reduce_fusion
  198.2 0.4 broadcast_select_fusion
  198.6 2.7 fusion.38
  201.3 0.7 multiply_convert_fusion
  202.0 0.8 multiply_convert_fusion.1
  202.8 0.4 stack.9
  203.2 0.4 stack.10
  203.7 2.7 pad_maximum_fusion
  206.3 10.5 %all-to-all-start.1 = ((bf16[128,4,2,1024]{3,1,2,0:T(4,128)(2,1)}), bf16[128,4,2,1024]{3,1,2,0:T(4,128)(2,1)S(1)}, u32[]{:S(2)}, u32[]{:S(2)}) async-start(bf16[128,4,2,1024]{3,1,2,0:T(4,128)(2,1)} %pad_maximum_fusion), calls=%async_computation.1 | async-start | bytes 4194304 | tf_op jit(solution)/shard_map/all_to_all | solution.py:110
  216.9 0.0 all-gather.6.cloned.1.call-start
  216.9 0.7 all-gather.6.cloned.1.call-update
  217.6 0.0 all-gather.8.cloned.1.call-start
  217.7 96.7 %all-to-all-done.1 = bf16[128,4,2,1024]{3,1,2,0:T(4,128)(2,1)S(1)} async-done(((bf16[128,4,2,1024]{3,1,2,0:T(4,128)(2,1)}), bf16[128,4,2,1024]{3,1,2,0:T(4,128)(2,1)S(1)}, u32[]{:S(2)}, u32[]{:S(2)}) %all-to-all-start.1) | async-done | bytes 2097184 | tf_op jit(solution)/shard_map/all_to_all | solution.py:110
  314.4 3.7 copy.45
  318.1 3.2 gather_fusion
  321.3 2.1 fusion.14
  323.5 0.0 all-gather.8.cloned.1.call-update
  323.5 0.0 reduce-scatter.2.cloned.1.call-start
  323.5 0.0 all-gather.6.cloned.1.call-done
  323.6 1.9 constant_dynamic-slice_fusion
  325.5 0.4 reshape.153
  326.0 0.5 copy.47
  326.5 0.4 dot_general.24
  326.9 29.0 %all-gather.8.cloned.1.call-done = bf16[512,2,1024]{2,0,1:T(8,128)(2,1)} async-done(((bf16[128,2,1024]{2,0,1:T(8,128)(2,1)}), bf16[512,2,1024]{2,0,1:T(8,128)(2,1)}) %all-gather.8.cloned.1.call-update) | async-done | bytes 2097168 | tf_op jit(solution)/shard_map/all_gather | solution.py:123
  355.9 3.7 copy.48
  359.7 2.2 reshape.173
  361.9 3.1 fusion.5
  365.0 1.4 copy.50
  366.3 1.8 reshape.155
  368.1 0.0 reduce-scatter.2.cloned.1.call-update
  368.1 0.0 copy-start.1
  368.2 20.3 %reduce-scatter.2.cloned.1.call-done = f32[256,1024]{1,0:T(8,128)} async-done(((f32[512,1024]{1,0:T(8,128)}), f32[256,1024]{1,0:T(8,128)}) %reduce-scatter.2.cloned.1.call-update) | async-done | bytes 1048592 | tf_op jit(solution)/shard_map/reduce_scatter | solution.py:135
  388.4 1.3 convert_element_type.58
  389.7 1.0 convert_element_type.59
  390.7 15.9 %all-to-all-start.2 = ((bf16[64,4,1024]{2,1,0:T(4,128)(2,1)}), bf16[64,4,1024]{2,1,0:T(4,128)(2,1)S(1)}, u32[]{:S(2)}, u32[]{:S(2)}) async-start(bf16[64,4,1024]{2,1,0:T(4,128)(2,1)} %convert_element_type.59), calls=%async_computation.3 | async-start | bytes 1048576 | tf_op jit(solution)/shard_map/all_to_all | solution.py:139
  406.7 1.3 copy.51
  408.0 30.9 %all-to-all-done.2 = bf16[64,4,1024]{2,1,0:T(4,128)(2,1)S(1)} async-done(((bf16[64,4,1024]{2,1,0:T(4,128)(2,1)}), bf16[64,4,1024]{2,1,0:T(4,128)(2,1)S(1)}, u32[]{:S(2)}, u32[]{:S(2)}) %all-to-all-start.2) | async-done | bytes 524320 | tf_op jit(solution)/shard_map/all_to_all | solution.py:139
  438.8 0.2 convert_reduce_fusion
  439.1 0.6 broadcast_multiply_fusion
  (10 shorter events, 0.0 us)
Async XLA Ops:
  7.2 63.3 %all-gather.4.cloned.1.call-start = ((), (), s32[]{:S(2)}) async-start(), calls=%async_computation.4 | async-start | bytes 5242880 | tf_op jit(solution)/shard_map/all_gather | solution.py:79
  74.4 1.0 copy-start.2
  74.4 1.5 copy-start.5
  81.4 1.4 copy-start
  82.8 17.2 %copy-start.4 = (s32[192]{0:T(256)S(1)}, s32[192]{0:T(256)}, u32[]{:S(2)}) copy-start(s32[192]{0:T(256)} %param.10) | copy-start | bytes 2308
  82.8 19.8 %copy-start.6 = (s32[192]{0:T(256)S(1)}, s32[192]{0:T(256)}, u32[]{:S(2)}) copy-start(s32[192]{0:T(256)} %param.11) | copy-start | bytes 2308
  82.8 114.6 %all-to-all-start = ((bf16[128,4,2,1024]{3,2,1,0:T(2,128)(2,1)}), bf16[128,4,2,1024]{3,2,1,0:T(2,128)(2,1)S(1)}, u32[]{:S(2)}, u32[]{:S(2)}) async-start(bf16[128,4,2,1024]{3,2,1,0:T(2,128)(2,1)} %bitcast.52), calls=%async_computation | async-start | bytes 4194304 | tf_op jit(solution)/shard_map/all_to_all | solution.py:97
  206.3 108.0 %all-to-all-start.1 = ((bf16[128,4,2,1024]{3,1,2,0:T(4,128)(2,1)}), bf16[128,4,2,1024]{3,1,2,0:T(4,128)(2,1)S(1)}, u32[]{:S(2)}, u32[]{:S(2)}) async-start(bf16[128,4,2,1024]{3,1,2,0:T(4,128)(2,1)} %pad_maximum_fusion), calls=%async_computation.1 | async-start | bytes 4194304 | tf_op jit(solution)/shard_map/all_to_all | solution.py:110
  216.9 106.7 %all-gather.6.cloned.1.call-start = ((), (), s32[]{:S(2)}) async-start(), calls=%async_computation.5 | async-start | bytes 5242880 | tf_op jit(solution)/shard_map/all_gather | solution.py:122
  217.6 138.3 %all-gather.8.cloned.1.call-start = ((), (), s32[]{:S(2)}) async-start(), calls=%async_computation.6 | async-start | bytes 2621440 | tf_op jit(solution)/shard_map/all_gather | solution.py:123
  217.7 103.6 %copy-start.3 = (f32[128,2,1024]{2,0,1:T(8,128)S(1)}, f32[128,2,1024]{2,0,1:T(8,128)}, u32[]{:S(2)}) copy-start(f32[128,2,1024]{2,0,1:T(8,128)} %copy-done.2) | copy-start | bytes 3145732
  323.5 65.0 %reduce-scatter.2.cloned.1.call-start = ((), (), s32[]{:S(2)}) async-start(), calls=%async_computation.7 | async-start | bytes 3145728 | tf_op jit(solution)/shard_map/reduce_scatter | solution.py:135
  368.1 38.5 %copy-start.1 = (bf16[128,2,1024]{2,0,1:T(8,128)(2,1)S(1)}, bf16[128,2,1024]{2,0,1:T(8,128)(2,1)}, u32[]{:S(2)}) copy-start(bf16[128,2,1024]{2,0,1:T(8,128)(2,1)} %fusion.14) | copy-start | bytes 1572868
  390.7 48.1 %all-to-all-start.2 = ((bf16[64,4,1024]{2,1,0:T(4,128)(2,1)}), bf16[64,4,1024]{2,1,0:T(4,128)(2,1)S(1)}, u32[]{:S(2)}, u32[]{:S(2)}) async-start(bf16[64,4,1024]{2,1,0:T(4,128)(2,1)} %convert_element_type.59), calls=%async_computation.3 | async-start | bytes 1048576 | tf_op jit(solution)/shard_map/all_to_all | solution.py:139
Sparse Core Ops, SparseCore 0:
  10.1 60.3 all-gather.3
  219.8 55.5 all-gather.5
  323.6 32.2 all-gather.7
  368.3 20.1 reduce-scatter.1

commit v3 on v2

--- a/solution.py
+++ b/solution.py
@@ -74,11 +74,12 @@
     per_owner = per_bin * MOSTB
     group_slots = sources * per_owner
     flat = features.reshape(rows_dev * views, feat_dim)
-    folded = jnp.dot(
-        flat,
-        lax.all_gather(head_weight, "bin", axis=0, tiled=True),
-        preferred_element_type=jnp.float32,
-    )
+    halves = head_weight.reshape(2, part_rows // 2, emb_dim)
+    half = lax.dynamic_index_in_dim(halves, lax.axis_index("dc"), 0, keepdims=False)
+    blocks = lax.all_gather(half, "bin", axis=0)
+    blocks = lax.all_gather(blocks, "dc", axis=0)
+    weight = jnp.transpose(blocks, (1, 0, 2, 3)).reshape(feat_dim, emb_dim)
+    folded = jnp.dot(flat, weight, preferred_element_type=jnp.float32)
     embedded = folded.reshape(rows_dev, views, emb_dim)
     scale = lax.rsqrt(jnp.sum(embedded * embedded, axis=2, keepdims=True) + 1e-06)
     unit = embedded * scale

time: 447 us -> 466 us (1.043)
  blocking collectives: 0 us -> 47.9 us
  waiting for transfers between devices: 332 us -> 310 us
  starting transfers between devices: 43.8 us -> 27.9 us
  local copies, waits for them, and re-layouts: 32.1 us -> 42.5 us
    all_to_all x0 -> x1, blocking collectives: none -> 47.9 us  [local(): lax.all_to_all(planes, ('dx', 'dz'), split_axis=0, concat_axis=0, tiled=T...]
    all_to_all x1 -> x0, waiting for transfers between devices: 30.9 us -> none  [local(): lax.all_to_all(planes, ('dx', 'dz'), split_axis=0, concat_axis=0, tiled=T...]
    all_to_all x1 -> x0, starting transfers between devices: 15.9 us -> none  [local(): lax.all_to_all(planes, ('dx', 'dz'), split_axis=0, concat_axis=0, tiled=T...]
    all_gather x1 -> x2, waiting for transfers between devices: 59.3 us -> 68.9 us  [the longest x1 44.4 us: local(): blocks = lax.all_gather(half, 'bin', axis=0)]
    scatter x1, local copies, waits for them, and re-layouts: 4.36 us -> 10.9 us  [local(): outbox = empty.at[target].set(sent)]
where the time goes in v3:
time: 466 us; the launch traced here: 465 us
  waiting for transfers between devices  310 us (67%)
  blocking collectives  47.9 us (10%)
  local copies, waits for them, and re-layouts  42.5 us (9%)
  starting transfers between devices  27.9 us (6%)
  between operations  16 us (3%)
  other arithmetic  11.3 us (2%)
  matrix products  9.2 us (2%)
    all_to_all x1, waiting for transfers between devices, local(): lax.all_to_all(grads.reshape(sources, per_owner, views, emb_dim), DP, spl...  96.7 us
    all_to_all x1, waiting for transfers between devices, local(): lax.all_to_all(outbox.reshape(sources, per_owner, views, emb_dim), DP, sp...  94.3 us
    all_to_all x1, blocking collectives, local(): lax.all_to_all(planes, ('dx', 'dz'), split_axis=0, concat_axis=0, tiled=T...  47.9 us
    all_gather x1, waiting for transfers between devices, local(): blocks = lax.all_gather(half, 'bin', axis=0)  44.4 us
    all_gather x1, waiting for transfers between devices, local(): outgrad = lax.all_gather(grad_rows, 'bin', axis=0, tiled=True)  28.9 us
    all_gather x1, waiting for transfers between devices, local(): blocks = lax.all_gather(blocks, 'dc', axis=0)  24.5 us
    reduce_scatter x1, waiting for transfers between devices, local(): lax.psum_scatter(local_grad.reshape(part_rows, emb_dim), 'dc', scatter_di...  20.3 us
    all_to_all x1, starting transfers between devices, local(): lax.all_to_all(outbox.reshape(sources, per_owner, views, emb_dim), DP, sp...  17.2 us
  transfers between devices with their start and end apart: 7, of which 6 were waited for; matrix products, arithmetic and copies ran while one was open for 4% of the time, Pallas kernels for 0%

profile of v3, /device:TPU:6, one launch (start us, length us, event | category | flops | bytes accessed | tf_op | source)
XLA Modules:
  0.0 464.6 jit_solution(9819966063306740438)
XLA Ops:
  7.2 0.0 all-gather.6.cloned.1.call-start
  7.2 1.2 copy-done
  8.4 0.8 constant_dynamic-slice_fusion.1
  9.2 0.0 all-gather.6.cloned.1.call-update
  9.2 0.0 all-gather.12.cloned.1.call-start
  9.3 44.4 %all-gather.6.cloned.1.call-done = bf16[4,256,1024]{2,1,0:T(8,128)(2,1)} async-done(((bf16[1,256,1024]{2,1,0:T(8,128)(2,1)}), bf16[4,256,1024]{2,1,0:T(8,128)(2,1)}) %all-gather.6.cloned.1.call-update) | async-done | bytes 2097168 | tf_op jit(solution)/shard_map/all_gather | solution.py:79
  53.7 1.2 reshape.174
  55.0 0.2 convert_reduce_fusion.2
  55.1 0.2 convert_reduce_fusion.1
  55.3 0.1 select_reduce_fusion.1
  55.5 24.5 %all-gather.12.cloned.1.call-done = bf16[8,256,1024]{2,1,0:T(8,128)(2,1)} async-done(((bf16[4,256,1024]{2,1,0:T(8,128)(2,1)}), bf16[8,256,1024]{2,1,0:T(8,128)(2,1)}) %all-gather.12.cloned.1.call-update) | async-done | bytes 4194320 | tf_op jit(solution)/shard_map/all_gather | solution.py:80
  80.0 2.7 copy.25
  82.7 1.3 multiply_reduce_fusion.1
  84.1 0.6 reshape.175
  84.7 0.1 rsqrt.13
  84.9 0.2 copy-done.4
  85.1 0.7 copy-done.2
  85.7 1.2 multiply_convert_fusion.4
  87.0 1.1 scatter.12
  88.1 10.9 %scatter_fusion = bf16[512,2,1024]{2,1,0:T(2,128)(2,1)S(1)} fusion(bf16[512,2,1024]{2,1,0:T(2,128)(2,1)S(1)} %scatter.12, s32[128]{0:T(128)S(1)} %fusion.22, bf16[128,2,1024]{2,1,0:T(2,128)(2,1)} %multiply_convert_fusion.4), kind=kCustom, calls=%fused_computation.1 | custom fusion | bytes 1573376 | tf_op jit(solution)/shard_map/scatter | solution.py:97
  98.9 1.3 copy-done.1
  100.3 17.2 %all-to-all-start = ((bf16[128,4,2,1024]{3,2,1,0:T(2,128)(2,1)}), bf16[128,4,2,1024]{3,2,1,0:T(2,128)(2,1)S(1)}, u32[]{:S(2)}, u32[]{:S(2)}) async-start(bf16[128,4,2,1024]{3,2,1,0:T(2,128)(2,1)} %bitcast.56), calls=%async_computation | async-start | bytes 4194304 | tf_op jit(solution)/shard_map/all_to_all | solution.py:98
  117.5 0.6 fusion.21
  120.0 0.1 pad_dynamic-slice_fusion
  120.1 0.6 fusion.25
  120.7 94.3 %all-to-all-done = bf16[128,4,2,1024]{3,2,1,0:T(2,128)(2,1)S(1)} async-done(((bf16[128,4,2,1024]{3,2,1,0:T(2,128)(2,1)}), bf16[128,4,2,1024]{3,2,1,0:T(2,128)(2,1)S(1)}, u32[]{:S(2)}, u32[]{:S(2)}) %all-to-all-start) | async-done | bytes 2097184 | tf_op jit(solution)/shard_map/all_to_all | solution.py:98
  215.0 0.6 copy.34
  215.6 0.2 compare_reduce_fusion
  215.8 0.4 broadcast_select_fusion
  216.2 2.7 fusion.26
  218.9 0.8 multiply_convert_fusion.1
  219.6 1.7 multiply_convert_fusion
  221.4 0.4 stack.9
  221.8 1.5 stack.10
  223.3 2.7 pad_maximum_fusion
  225.9 10.3 %all-to-all-start.1 = ((bf16[128,4,2,1024]{3,1,2,0:T(4,128)(2,1)}), bf16[128,4,2,1024]{3,1,2,0:T(4,128)(2,1)S(1)}, u32[]{:S(2)}, u32[]{:S(2)}) async-start(bf16[128,4,2,1024]{3,1,2,0:T(4,128)(2,1)} %pad_maximum_fusion), calls=%async_computation.1 | async-start | bytes 4194304 | tf_op jit(solution)/shard_map/all_to_all | solution.py:111
  236.3 0.0 all-gather.8.cloned.1.call-start
  236.3 0.7 all-gather.8.cloned.1.call-update
  237.0 0.0 all-gather.10.cloned.1.call-start
  237.0 96.7 %all-to-all-done.1 = bf16[128,4,2,1024]{3,1,2,0:T(4,128)(2,1)S(1)} async-done(((bf16[128,4,2,1024]{3,1,2,0:T(4,128)(2,1)}), bf16[128,4,2,1024]{3,1,2,0:T(4,128)(2,1)S(1)}, u32[]{:S(2)}, u32[]{:S(2)}) %all-to-all-start.1) | async-done | bytes 2097184 | tf_op jit(solution)/shard_map/all_to_all | solution.py:111
  333.7 3.7 copy.29
  337.5 3.2 gather_fusion
  340.7 1.1 reshape.182
  341.8 1.8 multiply_reduce_fusion
  343.6 0.1 mul.96
  343.8 1.7 multiply_convert_fusion.2
  345.5 0.0 all-gather.10.cloned.1.call-update
  345.5 0.3 reduce-scatter.2.cloned.1.call-start
  345.8 0.0 all-gather.8.cloned.1.call-done
  345.8 1.9 constant_dynamic-slice_fusion
  347.7 0.4 reshape.179
  348.2 0.5 copy.30
  348.7 1.2 dot_general.27
  350.0 28.9 %all-gather.10.cloned.1.call-done = bf16[512,2,1024]{2,1,0:T(2,128)(2,1)} async-done(((bf16[128,2,1024]{2,1,0:T(2,128)(2,1)}), bf16[512,2,1024]{2,1,0:T(2,128)(2,1)}) %all-gather.10.cloned.1.call-update) | async-done | bytes 2097168 | tf_op jit(solution)/shard_map/all_gather | solution.py:124
  378.9 2.7 reshape.200
  381.6 2.7 fusion.2
  384.3 1.4 copy.32
  385.7 1.8 reshape.181
  387.5 20.3 %reduce-scatter.2.cloned.1.call-done = f32[256,1024]{1,0:T(8,128)} async-done(((f32[512,1024]{1,0:T(8,128)}), f32[256,1024]{1,0:T(8,128)}) %reduce-scatter.2.cloned.1.call-update) | async-done | bytes 1048592 | tf_op jit(solution)/shard_map/reduce_scatter | solution.py:136
  407.8 1.3 convert_element_type.66
  409.1 0.2 convert_element_type.67
  409.3 47.9 %all_to_all.15 = bf16[64,4,1024]{2,1,0:T(4,128)(2,1)S(1)} all-to-all(bf16[64,4,1024]{2,1,0:T(4,128)(2,1)S(1)} %convert_element_type.67), channel_id=1, replica_groups=mesh['dx'=4,'dz'=16,'dc'=2,'bin'=4] {'dx','dz'}, dimensions={0} | all-to-all | bytes 1048576 | tf_op jit(solution)/shard_map/all_to_all | solution.py:140
  457.2 0.2 convert_reduce_fusion
  457.5 0.6 broadcast_multiply_fusion
  (25 shorter events, 0.1 us)
Async XLA Ops:
  7.2 1.2 copy-start
  7.2 46.5 %copy-start.5 = (bf16[128,2,2048]{2,1,0:T(2,128)(2,1)S(1)}, bf16[128,2,2048]{2,1,0:T(2,128)(2,1)}, u32[]{:S(2)}) copy-start(bf16[128,2,2048]{2,1,0:T(2,128)(2,1)} %param.7) | copy-start | bytes 3145732
  7.2 46.5 %all-gather.6.cloned.1.call-start = ((), (), s32[]{:S(2)}) async-start(), calls=%async_computation.4 | async-start | bytes 2621440 | tf_op jit(solution)/shard_map/all_gather | solution.py:79
  9.2 70.8 %all-gather.12.cloned.1.call-start = ((), (), s32[]{:S(2)}) async-start(), calls=%async_computation.8 | async-start | bytes 6291456 | tf_op jit(solution)/shard_map/all_gather | solution.py:80
  53.7 1.3 copy-start.9
  53.7 1.5 copy-start.7
  80.0 2.7 copy-start.6
  84.1 1.0 copy-start.4
  84.1 2.9 copy-start.8
  84.7 1.0 copy-start.2
  98.9 1.4 copy-start.1
  100.3 19.8 %copy-start.10 = (s32[192]{0:T(256)S(1)}, s32[192]{0:T(256)}, u32[]{:S(2)}) copy-start(s32[192]{0:T(256)} %param.11) | copy-start | bytes 2308
  100.3 114.7 %all-to-all-start = ((bf16[128,4,2,1024]{3,2,1,0:T(2,128)(2,1)}), bf16[128,4,2,1024]{3,2,1,0:T(2,128)(2,1)S(1)}, u32[]{:S(2)}, u32[]{:S(2)}) async-start(bf16[128,4,2,1024]{3,2,1,0:T(2,128)(2,1)} %bitcast.56), calls=%async_computation | async-start | bytes 4194304 | tf_op jit(solution)/shard_map/all_to_all | solution.py:98
  225.9 107.8 %all-to-all-start.1 = ((bf16[128,4,2,1024]{3,1,2,0:T(4,128)(2,1)}), bf16[128,4,2,1024]{3,1,2,0:T(4,128)(2,1)S(1)}, u32[]{:S(2)}, u32[]{:S(2)}) async-start(bf16[128,4,2,1024]{3,1,2,0:T(4,128)(2,1)} %pad_maximum_fusion), calls=%async_computation.1 | async-start | bytes 4194304 | tf_op jit(solution)/shard_map/all_to_all | solution.py:111
  236.3 109.5 %all-gather.8.cloned.1.call-start = ((), (), s32[]{:S(2)}) async-start(), calls=%async_computation.5 | async-start | bytes 5242880 | tf_op jit(solution)/shard_map/all_gather | solution.py:123
  237.0 141.9 %all-gather.10.cloned.1.call-start = ((), (), s32[]{:S(2)}) async-start(), calls=%async_computation.6 | async-start | bytes 2621440 | tf_op jit(solution)/shard_map/all_gather | solution.py:124
  340.7 3.1 copy-start.3
  345.5 62.3 %reduce-scatter.2.cloned.1.call-start = ((), (), s32[]{:S(2)}) async-start(), calls=%async_computation.7 | async-start | bytes 3145728 | tf_op jit(solution)/shard_map/reduce_scatter | solution.py:136
Sparse Core Ops, SparseCore 0:
  10.7 42.9 all-gather.5
  55.8 24.1 all-gather.11
  239.2 56.4 all-gather.7
  345.6 33.2 all-gather.9
  387.6 20.1 reduce-scatter.1

commit v4 on v3

--- a/solution.py
+++ b/solution.py
@@ -74,11 +74,9 @@
     per_owner = per_bin * MOSTB
     group_slots = sources * per_owner
     flat = features.reshape(rows_dev * views, feat_dim)
-    halves = head_weight.reshape(2, part_rows // 2, emb_dim)
-    half = lax.dynamic_index_in_dim(halves, lax.axis_index("dc"), 0, keepdims=False)
-    blocks = lax.all_gather(half, "bin", axis=0)
-    blocks = lax.all_gather(blocks, "dc", axis=0)
-    weight = jnp.transpose(blocks, (1, 0, 2, 3)).reshape(feat_dim, emb_dim)
+    copies = jnp.broadcast_to(head_weight[None], (bins_n, part_rows, emb_dim))
+    weight = lax.all_to_all(copies, "bin", split_axis=0, concat_axis=0, tiled=True)
+    weight = weight.reshape(feat_dim, emb_dim)
     folded = jnp.dot(flat, weight, preferred_element_type=jnp.float32)
     embedded = folded.reshape(rows_dev, views, emb_dim)
     scale = lax.rsqrt(jnp.sum(embedded * embedded, axis=2, keepdims=True) + 1e-06)

time: 466 us -> 443 us (0.951)
  blocking collectives: 47.9 us -> 0 us
  starting transfers between devices: 27.9 us -> 51.6 us
  waiting for transfers between devices: 310 us -> 319 us
  local copies, waits for them, and re-layouts: 42.5 us -> 35.8 us
    all_to_all x0 -> x2, waiting for transfers between devices: none -> 79.5 us  [the longest x1 48.6 us: local(): lax.all_to_all(copies, 'bin', split_axis=0, concat_axis=0, tiled=True)]
    all_gather x2 -> x0, waiting for transfers between devices: 68.9 us -> none  [the longest x1 44.4 us: local(): blocks = lax.all_gather(half, 'bin', axis=0)]
    all_to_all x1 -> x0, blocking collectives: 47.9 us -> none  [local(): lax.all_to_all(planes, ('dx', 'dz'), split_axis=0, concat_axis=0, tiled=T...]
    all_to_all x0 -> x2, starting transfers between devices: none -> 20.9 us  [the longest x1 15.9 us: local(): lax.all_to_all(planes, ('dx', 'dz'), split_axis=0, concat_axis=0, tiled=T...]
    scatter x1, local copies, waits for them, and re-layouts: 10.9 us -> 4.29 us  [local(): outbox = empty.at[target].set(sent)]
where the time goes in v4:
time: 443 us; the launch traced here: 442 us
  waiting for transfers between devices  319 us (72%)
  starting transfers between devices  51.6 us (12%)
  local copies, waits for them, and re-layouts  35.8 us (8%)
  between operations  16 us (4%)
  matrix products  10.7 us (2%)
  other arithmetic  8.78 us (2%)
    all_to_all x1, waiting for transfers between devices, local(): lax.all_to_all(grads.reshape(sources, per_owner, views, emb_dim), DP, spl...  96.7 us
    all_to_all x1, waiting for transfers between devices, local(): lax.all_to_all(outbox.reshape(sources, per_owner, views, emb_dim), DP, sp...  94.2 us
    all_to_all x1, waiting for transfers between devices, local(): lax.all_to_all(copies, 'bin', split_axis=0, concat_axis=0, tiled=True)  48.6 us
    all_to_all x1, waiting for transfers between devices, local(): lax.all_to_all(planes, ('dx', 'dz'), split_axis=0, concat_axis=0, tiled=T...  30.9 us
    all_gather x1, waiting for transfers between devices, local(): outgrad = lax.all_gather(grad_rows, 'bin', axis=0, tiled=True)  28.1 us
    reduce_scatter x1, waiting for transfers between devices, local(): lax.psum_scatter(local_grad.reshape(part_rows, emb_dim), 'dc', scatter_di...  20.3 us
    all_to_all x1, starting transfers between devices, local(): lax.all_to_all(outbox.reshape(sources, per_owner, views, emb_dim), DP, sp...  20 us
    all_to_all x1, starting transfers between devices, local(): lax.all_to_all(planes, ('dx', 'dz'), split_axis=0, concat_axis=0, tiled=T...  15.9 us
  transfers between devices with their start and end apart: 7, of which 6 were waited for; matrix products, arithmetic and copies ran while one was open for 4% of the time, Pallas kernels for 0%

profile of v4, /device:TPU:6, one launch (start us, length us, event | category | flops | bytes accessed | tf_op | source)
XLA Modules:
  0.0 442.4 jit_solution(2915345390227138576)
XLA Ops:
  7.2 3.7 broadcast_in_dim.38
  10.9 5.0 %all-to-all-start = ((bf16[4,512,1024]{2,1,0:T(8,128)(2,1)}), bf16[4,512,1024]{2,1,0:T(8,128)(2,1)}, u32[]{:S(2)}, u32[]{:S(2)}) async-start(bf16[4,512,1024]{2,1,0:T(8,128)(2,1)} %broadcast_in_dim.38), calls=%async_computation | async-start | bytes 8388608 | tf_op jit(solution)/shard_map/all_to_all | solution.py:78
  15.9 0.0 copy-done.7
  15.9 0.2 convert_reduce_fusion.2
  16.1 0.0 copy-done.5
  16.1 0.2 convert_reduce_fusion.1
  16.3 0.1 select_reduce_fusion.1
  16.4 48.6 %all-to-all-done = bf16[4,512,1024]{2,1,0:T(8,128)(2,1)} async-done(((bf16[4,512,1024]{2,1,0:T(8,128)(2,1)}), bf16[4,512,1024]{2,1,0:T(8,128)(2,1)}, u32[]{:S(2)}, u32[]{:S(2)}) %all-to-all-start) | async-done | bytes 4194336 | tf_op jit(solution)/shard_map/all_to_all | solution.py:78
  65.0 0.0 copy-done.2
  65.0 3.6 multiply_reduce_fusion
  68.6 0.0 copy-start.6
  68.6 0.1 multiply_convert_fusion.3
  68.8 0.8 copy-done.3
  69.6 0.5 copy.41
  70.2 0.0 copy-done.6
  70.2 1.1 scatter.12
  71.3 4.3 scatter_fusion
  75.6 1.3 copy-done
  76.9 20.0 %all-to-all-start.1 = ((bf16[128,4,2,1024]{3,2,1,0:T(2,128)(2,1)}), bf16[128,4,2,1024]{3,2,1,0:T(2,128)(2,1)S(1)}, u32[]{:S(2)}, u32[]{:S(2)}) async-start(bf16[128,4,2,1024]{3,2,1,0:T(2,128)(2,1)} %bitcast.50), calls=%async_computation.1 | async-start | bytes 4194304 | tf_op jit(solution)/shard_map/all_to_all | solution.py:96
  97.0 0.6 fusion.32
  99.6 0.1 pad_dynamic-slice_fusion
  99.6 0.6 fusion.36
  100.2 94.2 %all-to-all-done.1 = bf16[128,4,2,1024]{3,2,1,0:T(2,128)(2,1)S(1)} async-done(((bf16[128,4,2,1024]{3,2,1,0:T(2,128)(2,1)}), bf16[128,4,2,1024]{3,2,1,0:T(2,128)(2,1)S(1)}, u32[]{:S(2)}, u32[]{:S(2)}) %all-to-all-start.1) | async-done | bytes 2097184 | tf_op jit(solution)/shard_map/all_to_all | solution.py:96
  194.5 0.6 copy.53
  195.1 0.2 compare_reduce_fusion
  195.2 0.4 broadcast_select_fusion
  195.7 2.7 fusion.37
  198.3 0.7 multiply_convert_fusion
  199.1 0.7 multiply_convert_fusion.1
  199.8 0.4 stack.10
  200.2 0.4 stack.9
  200.7 2.7 pad_maximum_fusion
  203.4 10.5 %all-to-all-start.2 = ((bf16[128,4,2,1024]{3,1,2,0:T(4,128)(2,1)}), bf16[128,4,2,1024]{3,1,2,0:T(4,128)(2,1)S(1)}, u32[]{:S(2)}, u32[]{:S(2)}) async-start(bf16[128,4,2,1024]{3,1,2,0:T(4,128)(2,1)} %pad_maximum_fusion), calls=%async_computation.2 | async-start | bytes 4194304 | tf_op jit(solution)/shard_map/all_to_all | solution.py:109
  213.9 0.0 all-gather.3.cloned.1.call-start
  214.0 0.7 all-gather.3.cloned.1.call-update
  214.7 0.0 all-gather.5.cloned.1.call-start
  214.7 96.7 %all-to-all-done.2 = bf16[128,4,2,1024]{3,1,2,0:T(4,128)(2,1)S(1)} async-done(((bf16[128,4,2,1024]{3,1,2,0:T(4,128)(2,1)}), bf16[128,4,2,1024]{3,1,2,0:T(4,128)(2,1)S(1)}, u32[]{:S(2)}, u32[]{:S(2)}) %all-to-all-start.2) | async-done | bytes 2097184 | tf_op jit(solution)/shard_map/all_to_all | solution.py:109
  311.4 3.7 copy.45
  315.1 3.2 gather_fusion
  318.4 0.0 copy-done.4
  318.4 2.1 fusion.12
  320.5 0.0 all-gather.5.cloned.1.call-update
  320.5 0.0 reduce-scatter.2.cloned.1.call-start
  320.6 0.0 all-gather.3.cloned.1.call-done
  320.6 1.9 constant_dynamic-slice_fusion
  322.5 0.4 reshape.158
  323.0 0.5 copy.47
  323.5 0.4 dot_general.24
  324.0 28.1 %all-gather.5.cloned.1.call-done = bf16[512,2,1024]{2,0,1:T(8,128)(2,1)} async-done(((bf16[128,2,1024]{2,0,1:T(8,128)(2,1)}), bf16[512,2,1024]{2,0,1:T(8,128)(2,1)}) %all-gather.5.cloned.1.call-update) | async-done | bytes 2097168 | tf_op jit(solution)/shard_map/all_gather | solution.py:122
  352.0 3.7 copy.48
  355.8 2.2 reshape.178
  358.0 3.0 fusion.3
  361.1 1.4 copy.50
  362.5 1.8 reshape.160
  364.2 0.0 reduce-scatter.2.cloned.1.call-update
  364.3 0.0 copy-start.1
  364.3 20.3 %reduce-scatter.2.cloned.1.call-done = f32[256,1024]{1,0:T(8,128)} async-done(((f32[512,1024]{1,0:T(8,128)}), f32[256,1024]{1,0:T(8,128)}) %reduce-scatter.2.cloned.1.call-update) | async-done | bytes 1048592 | tf_op jit(solution)/shard_map/reduce_scatter | solution.py:134
  384.6 1.3 convert_element_type.58
  385.9 1.0 convert_element_type.59
  386.9 15.9 %all-to-all-start.3 = ((bf16[64,4,1024]{2,1,0:T(4,128)(2,1)}), bf16[64,4,1024]{2,1,0:T(4,128)(2,1)S(1)}, u32[]{:S(2)}, u32[]{:S(2)}) async-start(bf16[64,4,1024]{2,1,0:T(4,128)(2,1)} %convert_element_type.59), calls=%async_computation.4 | async-start | bytes 1048576 | tf_op jit(solution)/shard_map/all_to_all | solution.py:138
  402.8 1.3 copy.51
  404.1 30.9 %all-to-all-done.3 = bf16[64,4,1024]{2,1,0:T(4,128)(2,1)S(1)} async-done(((bf16[64,4,1024]{2,1,0:T(4,128)(2,1)}), bf16[64,4,1024]{2,1,0:T(4,128)(2,1)S(1)}, u32[]{:S(2)}, u32[]{:S(2)}) %all-to-all-start.3) | async-done | bytes 524320 | tf_op jit(solution)/shard_map/all_to_all | solution.py:138
  435.0 0.2 convert_reduce_fusion
  435.2 0.6 broadcast_multiply_fusion
  (14 shorter events, 0.1 us)
Async XLA Ops:
  10.9 5.0 %copy-start.7 = (s32[128,1]{0,1:T(1,128)S(1)}, s32[128,1]{0,1:T(1,128)}, u32[]{:S(2)}) copy-start(s32[128,1]{0,1:T(1,128)} %param.9) | copy-start | bytes 1540
  10.9 5.2 %copy-start.5 = (s32[192]{0:T(256)S(1)}, s32[192]{0:T(256)}, u32[]{:S(2)}) copy-start(s32[192]{0:T(256)} %param.10) | copy-start | bytes 2308
  10.9 54.1 %copy-start.2 = (bf16[128,2,2048]{2,1,0:T(2,128)(2,1)S(1)}, bf16[128,2,2048]{2,1,0:T(2,128)(2,1)}, u32[]{:S(2)}) copy-start(bf16[128,2,2048]{2,1,0:T(2,128)(2,1)} %param.7) | copy-start | bytes 3145732
  10.9 54.1 %all-to-all-start = ((bf16[4,512,1024]{2,1,0:T(8,128)(2,1)}), bf16[4,512,1024]{2,1,0:T(8,128)(2,1)}, u32[]{:S(2)}, u32[]{:S(2)}) async-start(bf16[4,512,1024]{2,1,0:T(8,128)(2,1)} %broadcast_in_dim.38), calls=%async_computation | async-start | bytes 8388608 | tf_op jit(solution)/shard_map/all_to_all | solution.py:78
  68.6 1.0 copy-start.3
  68.6 1.5 copy-start.6
  75.6 1.4 copy-start
  76.9 22.6 %copy-start.8 = (s32[192]{0:T(256)S(1)}, s32[192]{0:T(256)}, u32[]{:S(2)}) copy-start(s32[192]{0:T(256)} %param.11) | copy-start | bytes 2308
  76.9 117.5 %all-to-all-start.1 = ((bf16[128,4,2,1024]{3,2,1,0:T(2,128)(2,1)}), bf16[128,4,2,1024]{3,2,1,0:T(2,128)(2,1)S(1)}, u32[]{:S(2)}, u32[]{:S(2)}) async-start(bf16[128,4,2,1024]{3,2,1,0:T(2,128)(2,1)} %bitcast.50), calls=%async_computation.1 | async-start | bytes 4194304 | tf_op jit(solution)/shard_map/all_to_all | solution.py:96
  203.4 108.0 %all-to-all-start.2 = ((bf16[128,4,2,1024]{3,1,2,0:T(4,128)(2,1)}), bf16[128,4,2,1024]{3,1,2,0:T(4,128)(2,1)S(1)}, u32[]{:S(2)}, u32[]{:S(2)}) async-start(bf16[128,4,2,1024]{3,1,2,0:T(4,128)(2,1)} %pad_maximum_fusion), calls=%async_computation.2 | async-start | bytes 4194304 | tf_op jit(solution)/shard_map/all_to_all | solution.py:109
  213.9 106.7 %all-gather.3.cloned.1.call-start = ((), (), s32[]{:S(2)}) async-start(), calls=%async_computation.5 | async-start | bytes 5242880 | tf_op jit(solution)/shard_map/all_gather | solution.py:121
  214.7 137.4 %all-gather.5.cloned.1.call-start = ((), (), s32[]{:S(2)}) async-start(), calls=%async_computation.6 | async-start | bytes 2621440 | tf_op jit(solution)/shard_map/all_gather | solution.py:122
  214.7 103.7 %copy-start.4 = (f32[128,2,1024]{2,0,1:T(8,128)S(1)}, f32[128,2,1024]{2,0,1:T(8,128)}, u32[]{:S(2)}) copy-start(f32[128,2,1024]{2,0,1:T(8,128)} %copy-done.3) | copy-start | bytes 3145732
  320.5 64.1 %reduce-scatter.2.cloned.1.call-start = ((), (), s32[]{:S(2)}) async-start(), calls=%async_computation.7 | async-start | bytes 3145728 | tf_op jit(solution)/shard_map/reduce_scatter | solution.py:134
  364.3 38.5 %copy-start.1 = (bf16[128,2,1024]{2,0,1:T(8,128)(2,1)S(1)}, bf16[128,2,1024]{2,0,1:T(8,128)(2,1)}, u32[]{:S(2)}) copy-start(bf16[128,2,1024]{2,0,1:T(8,128)(2,1)} %fusion.12) | copy-start | bytes 1572868
  386.9 48.1 %all-to-all-start.3 = ((bf16[64,4,1024]{2,1,0:T(4,128)(2,1)}), bf16[64,4,1024]{2,1,0:T(4,128)(2,1)S(1)}, u32[]{:S(2)}, u32[]{:S(2)}) async-start(bf16[64,4,1024]{2,1,0:T(4,128)(2,1)} %convert_element_type.59), calls=%async_computation.4 | async-start | bytes 1048576 | tf_op jit(solution)/shard_map/all_to_all | solution.py:138
Sparse Core Ops, SparseCore 0:
  216.9 54.6 all-gather.2
  320.6 31.3 all-gather.4
  364.4 20.1 reduce-scatter.1

commit v5 on v4

--- a/solution.py
+++ b/solution.py
@@ -52,7 +52,7 @@
         )
         / SOFTMAX_TEMP_SCALE
     ).astype(jnp.bfloat16)
-    return jnp.stack([query_gradient, key_gradient_rows], axis=1)
+    return query_gradient, key_gradient_rows
 
 
 def dp_index():
@@ -101,40 +101,45 @@
         tiled=True,
     )
     inbox = inbox.reshape(group_slots, views, emb_dim)
+    trunks = [lax.all_gather(features[:, view], "bin", axis=0, tiled=True) for view in range(views)]
+    inbox, trunks = lax.optimization_barrier((inbox, trunks))
     valid = inbox[:, 0, 0] < 2.0
     inbox = jnp.where(valid[:, None, None], inbox, jnp.zeros_like(inbox))
     first = jnp.sum((bin_owner < dp_index()).astype(jnp.int32))
     allowed = allowed_mask(valid, first, bin_link, group_slots, per_bin)
     grads = contrast(inbox[:, 0], inbox[:, 1], allowed, valid.astype(jnp.float32))
-    returned = lax.all_to_all(
-        grads.reshape(sources, per_owner, views, emb_dim),
-        DP,
-        split_axis=0,
-        concat_axis=0,
-        tiled=True,
-    )
-    row_grads = returned.reshape(group_slots, views, emb_dim)[target].astype(jnp.float32)
-    grad_rows = (
-        scale * (row_grads - unit * jnp.sum(unit * row_grads, axis=2, keepdims=True))
-    ).astype(jnp.bfloat16)
     column_start = lax.axis_index("bin") * part_rows
-    trunk = lax.all_gather(features, "bin", axis=0, tiled=True)
-    outgrad = lax.all_gather(grad_rows, "bin", axis=0, tiled=True)
-    columns = lax.dynamic_slice_in_dim(trunk, column_start, part_rows, 2)
-    count = trunk.shape[0]
-    local_grad = lax.dot_general(
-        columns.reshape(count * views, part_rows),
-        outgrad.reshape(count * views, emb_dim),
-        (((0,), (0,)), ((), ())),
-        preferred_element_type=jnp.float32,
-    )
+    view_rows = []
+    local_grad = None
+    for view, view_grads in enumerate(grads):
+        if view_rows:
+            view_grads, _ = lax.optimization_barrier((view_grads, view_rows[-1]))
+        returned = lax.all_to_all(
+            view_grads.reshape(sources, per_owner, emb_dim),
+            DP,
+            split_axis=0,
+            concat_axis=0,
+            tiled=True,
+        )
+        row_grads = returned.reshape(group_slots, emb_dim)[target].astype(jnp.float32)
+        view_unit = unit[:, view]
+        projected = row_grads - view_unit * jnp.sum(view_unit * row_grads, axis=1, keepdims=True)
+        rows_out = (scale[:, view] * projected).astype(jnp.bfloat16)
+        view_rows.append(rows_out)
+        columns = lax.dynamic_slice_in_dim(trunks[view], column_start, part_rows, 1)
+        outgrad = lax.all_gather(rows_out, "bin", axis=0, tiled=True)
+        term = lax.dot_general(
+            columns, outgrad, (((0,), (0,)), ((), ())), preferred_element_type=jnp.float32
+        )
+        local_grad = term if local_grad is None else local_grad + term
+    grad_rows = jnp.stack(view_rows, axis=1)
     sizes = [size for _, size in DP_PARTS]
     per_dev = part_rows // sources
     local_grad = jnp.transpose(local_grad.reshape(*sizes, per_dev, emb_dim), (2, 0, 1, 3, 4))
     local_grad = lax.psum_scatter(
-        local_grad.reshape(part_rows, emb_dim), "dc", scatter_dimension=0, tiled=True
+        local_grad.reshape(part_rows, emb_dim).astype(jnp.bfloat16), "dc", scatter_dimension=0, tiled=True
     )
-    planes = local_grad.reshape(sizes[0] * sizes[1], per_dev, emb_dim).astype(jnp.bfloat16)
+    planes = local_grad.reshape(sizes[0] * sizes[1], per_dev, emb_dim)
     planes = lax.all_to_all(planes, ("dx", "dz"), split_axis=0, concat_axis=0, tiled=True)
     local_grad = jnp.sum(planes.astype(jnp.float32), axis=0)
     grad_weight = local_grad / rows_dev

time: 443 us -> 455 us (1.027)
  local copies, waits for them, and re-layouts: 35.8 us -> 46 us
  starting transfers between devices: 51.6 us -> 60.5 us
  waiting for transfers between devices: 319 us -> 311 us
    scatter x1, local copies, waits for them, and re-layouts: 4.29 us -> 14.4 us  [local(): outbox = empty.at[target].set(sent)]
    all_to_all x1 -> x2, starting transfers between devices: 10.5 us -> 19.5 us  [local(): lax.all_to_all(view_grads.reshape(sources, per_owner, emb_dim), DP, split...]
    all_to_all x1 -> x2, waiting for transfers between devices: 96.7 us -> 104 us  [local(): lax.all_to_all(view_grads.reshape(sources, per_owner, emb_dim), DP, split...]
    all_to_all x1, waiting for transfers between devices: 94.2 us -> 86.5 us  [local(): lax.all_to_all(outbox.reshape(sources, per_owner, views, emb_dim), DP, sp...]
    all_gather x2 -> x4, waiting for transfers between devices: 28.1 us -> 20.6 us  [the longest x2 20.5 us: local(): outgrad = lax.all_gather(rows_out, 'bin', axis=0, tiled=True)]
  transfers between devices with their start and end apart: 7 -> 10, of which waited for: 6 -> 7; matrix products, arithmetic and copies ran while one was open for 4% -> 5% of each run, Pallas kernels for 0% -> 0%
where the time goes in v5:
time: 455 us; the launch traced here: 454 us
  waiting for transfers between devices  311 us (68%)
  starting transfers between devices  60.5 us (13%)
  local copies, waits for them, and re-layouts  46 us (10%)
  between operations  16 us (4%)
  matrix products  15.2 us (3%)
  other arithmetic  4.82 us (1%)
    all_to_all x2, waiting for transfers between devices, local(): lax.all_to_all(view_grads.reshape(sources, per_owner, emb_dim), DP, split...  104 us
    all_to_all x1, waiting for transfers between devices, local(): lax.all_to_all(outbox.reshape(sources, per_owner, views, emb_dim), DP, sp...  86.5 us
    all_to_all x1, waiting for transfers between devices, local(): lax.all_to_all(copies, 'bin', split_axis=0, concat_axis=0, tiled=True)  48.6 us
    all_to_all x1, waiting for transfers between devices, local(): lax.all_to_all(planes, ('dx', 'dz'), split_axis=0, concat_axis=0, tiled=T...  30.6 us
    all_gather x2, waiting for transfers between devices, local(): outgrad = lax.all_gather(rows_out, 'bin', axis=0, tiled=True)  20.5 us
    all_to_all x1, starting transfers between devices, local(): lax.all_to_all(outbox.reshape(sources, per_owner, views, emb_dim), DP, sp...  20 us
    reduce_scatter x1, waiting for transfers between devices, local(): lax.psum_scatter(local_grad.reshape(part_rows, emb_dim).astype(jnp.bfloat...  19.5 us
    all_to_all x2, starting transfers between devices, local(): lax.all_to_all(view_grads.reshape(sources, per_owner, emb_dim), DP, split...  19.5 us
  transfers between devices with their start and end apart: 10, of which 7 were waited for; matrix products, arithmetic and copies ran while one was open for 5% of the time, Pallas kernels for 0%

profile of v5, /device:TPU:6, one launch (start us, length us, event | category | flops | bytes accessed | tf_op | source)
XLA Modules:
  0.0 453.6 jit_solution(8795842793043173516)
XLA Ops:
  7.2 3.8 broadcast_in_dim.38
  10.9 5.0 %all-to-all-start = ((bf16[4,512,1024]{2,1,0:T(8,128)(2,1)}), bf16[4,512,1024]{2,1,0:T(8,128)(2,1)}, u32[]{:S(2)}, u32[]{:S(2)}) async-start(bf16[4,512,1024]{2,1,0:T(8,128)(2,1)} %broadcast_in_dim.38), calls=%async_computation | async-start | bytes 8388608 | tf_op jit(solution)/shard_map/all_to_all | solution.py:78
  15.9 0.2 convert_reduce_fusion.2
  16.1 0.2 convert_reduce_fusion.1
  16.3 0.1 select_reduce_fusion.1
  16.4 48.6 %all-to-all-done = bf16[4,512,1024]{2,1,0:T(8,128)(2,1)} async-done(((bf16[4,512,1024]{2,1,0:T(8,128)(2,1)}), bf16[4,512,1024]{2,1,0:T(8,128)(2,1)}, u32[]{:S(2)}, u32[]{:S(2)}) %all-to-all-start) | async-done | bytes 4194336 | tf_op jit(solution)/shard_map/all_to_all | solution.py:78
  65.0 3.6 multiply_reduce_fusion
  68.6 0.2 fusion.38
  68.8 0.5 copy.17
  69.4 2.4 scatter.12
  71.8 14.4 %scatter_fusion = bf16[512,2,1024]{2,1,0:T(2,128)(2,1)} fusion(bf16[512,2,1024]{2,1,0:T(2,128)(2,1)} %scatter.12, s32[128]{0:T(128)S(1)} %fusion.31, bf16[128,2,1024]{2,1,0:T(2,128)(2,1)S(1)} %copy.17), kind=kCustom, calls=%fused_computation.2 | custom fusion | bytes 1573376 | tf_op jit(solution)/shard_map/scatter | solution.py:95
  86.2 20.0 %all-to-all-start.1 = ((bf16[128,4,2,1024]{3,2,1,0:T(2,128)(2,1)}), bf16[128,4,2,1024]{3,2,1,0:T(2,128)(2,1)S(1)}, u32[]{:S(2)}, u32[]{:S(2)}) async-start(bf16[128,4,2,1024]{3,2,1,0:T(2,128)(2,1)} %bitcast.9), calls=%async_computation.1 | async-start | bytes 4194304 | tf_op jit(solution)/shard_map/all_to_all | solution.py:96
  106.2 0.0 all-gather.11.cloned.1.call-start
  106.2 4.1 fusion.39
  110.3 1.1 copy.27
  111.5 0.0 all-gather.13.cloned.1.call-start
  111.5 2.3 copy.28
  113.9 0.6 fusion.30
  116.5 0.1 pad_dynamic-slice_fusion
  116.6 0.6 fusion.40
  117.2 86.5 %all-to-all-done.1 = bf16[128,4,2,1024]{3,2,1,0:T(2,128)(2,1)S(1)} async-done(((bf16[128,4,2,1024]{3,2,1,0:T(2,128)(2,1)}), bf16[128,4,2,1024]{3,2,1,0:T(2,128)(2,1)S(1)}, u32[]{:S(2)}, u32[]{:S(2)}) %all-to-all-start.1) | async-done | bytes 2097184 | tf_op jit(solution)/shard_map/all_to_all | solution.py:96
  203.7 1.3 copy-done
  205.0 2.2 copy.23
  207.2 0.0 all-gather.11.cloned.1.call-done
  207.3 0.1 compare_reduce_fusion
  207.4 0.2 broadcast_select_fusion
  207.6 2.7 fusion.41
  210.4 1.0 copy-done.10
  211.4 0.7 multiply_convert_fusion.1
  212.1 1.2 reshape.209
  213.3 10.5 %all-to-all-start.2 = ((bf16[128,4,1024]{2,1,0:T(4,128)(2,1)}), bf16[128,4,1024]{2,1,0:T(4,128)(2,1)S(1)}, u32[]{:S(2)}, u32[]{:S(2)}) async-start(bf16[128,4,1024]{2,1,0:T(4,128)(2,1)} %reshape.209), calls=%async_computation.2 | async-start | bytes 2097152 | tf_op jit(solution)/shard_map/all_to_all | solution.py:117
  223.9 2.9 multiply_convert_fusion
  226.8 51.3 %all-to-all-done.2 = bf16[128,4,1024]{2,1,0:T(4,128)(2,1)S(1)} async-done(((bf16[128,4,1024]{2,1,0:T(4,128)(2,1)}), bf16[128,4,1024]{2,1,0:T(4,128)(2,1)S(1)}, u32[]{:S(2)}, u32[]{:S(2)}) %all-to-all-start.2) | async-done | bytes 1048608 | tf_op jit(solution)/shard_map/all_to_all | solution.py:117
  278.1 0.3 reshape.210
  278.4 0.9 gather_fusion
  279.3 0.1 fusion.11
  279.4 0.9 fusion.13
  280.3 1.2 reshape.211
  281.5 9.0 %all-to-all-start.3 = ((bf16[128,4,1024]{2,1,0:T(4,128)(2,1)}), bf16[128,4,1024]{2,1,0:T(4,128)(2,1)}, u32[]{:S(2)}, u32[]{:S(2)}) async-start(bf16[128,4,1024]{2,1,0:T(4,128)(2,1)} %reshape.211), calls=%async_computation.3 | async-start | bytes 2097152 | tf_op jit(solution)/shard_map/all_to_all | solution.py:117
  290.5 0.0 all-gather.7.cloned.1.call-start
  290.5 0.7 all-gather.7.cloned.1.call-update
  291.2 0.0 all-gather.9.cloned.1.call-start
  291.2 53.2 %all-to-all-done.3 = bf16[128,4,1024]{2,1,0:T(4,128)(2,1)} async-done(((bf16[128,4,1024]{2,1,0:T(4,128)(2,1)}), bf16[128,4,1024]{2,1,0:T(4,128)(2,1)}, u32[]{:S(2)}, u32[]{:S(2)}) %all-to-all-start.3) | async-done | bytes 1048608 | tf_op jit(solution)/shard_map/all_to_all | solution.py:117
  344.4 1.3 reshape.212
  345.8 0.9 gather_fusion.1
  346.6 0.1 fusion.17
  346.8 0.9 fusion.19
  347.7 0.0 reduce-scatter.2.cloned.1.call-start
  347.7 0.0 all-gather.7.cloned.1.call-done
  347.7 2.1 fusion.21
  349.9 20.5 %all-gather.9.cloned.1.call-done = bf16[512,1024]{1,0:T(8,128)(2,1)} async-done(((bf16[128,1024]{1,0:T(8,128)(2,1)}), bf16[512,1024]{1,0:T(8,128)(2,1)}) %all-gather.9.cloned.1.call-update) | async-done | bytes 1048592 | tf_op jit(solution)/shard_map/all_gather | solution.py:130
  370.4 3.1 add_convert_fusion
  373.5 1.5 convert_element_type.109
  375.0 0.4 copy.31
  375.4 1.1 convert_element_type.111
  376.6 19.5 %reduce-scatter.2.cloned.1.call-done = bf16[256,1024]{1,0:T(8,128)(2,1)} async-done(((bf16[512,1024]{1,0:T(8,128)(2,1)}), bf16[256,1024]{1,0:T(8,128)(2,1)}) %reduce-scatter.2.cloned.1.call-update) | async-done | bytes 524304 | tf_op jit(solution)/shard_map/reduce_scatter | solution.py:139
  396.0 2.0 reshape.213
  398.1 15.9 %all-to-all-start.4 = ((bf16[64,4,1024]{2,1,0:T(4,128)(2,1)}), bf16[64,4,1024]{2,1,0:T(4,128)(2,1)S(1)}, u32[]{:S(2)}, u32[]{:S(2)}) async-start(bf16[64,4,1024]{2,1,0:T(4,128)(2,1)} %reshape.213), calls=%async_computation.5 | async-start | bytes 1048576 | tf_op jit(solution)/shard_map/all_to_all | solution.py:143
  414.0 0.2 fusion.10
  414.2 0.1 pad_maximum_fusion
  414.3 1.3 copy.22
  415.6 30.6 %all-to-all-done.4 = bf16[64,4,1024]{2,1,0:T(4,128)(2,1)S(1)} async-done(((bf16[64,4,1024]{2,1,0:T(4,128)(2,1)}), bf16[64,4,1024]{2,1,0:T(4,128)(2,1)S(1)}, u32[]{:S(2)}, u32[]{:S(2)}) %all-to-all-start.4) | async-done | bytes 524320 | tf_op jit(solution)/shard_map/all_to_all | solution.py:143
  446.2 0.2 convert_reduce_fusion
  446.5 0.6 broadcast_multiply_fusion.1
  (33 shorter events, 0.2 us)
Async XLA Ops:
  10.9 5.0 %copy-start.8 = (s32[128,1]{0,1:T(1,128)S(1)}, s32[128,1]{0,1:T(1,128)}, u32[]{:S(2)}) copy-start(s32[128,1]{0,1:T(1,128)} %param.9) | copy-start | bytes 1540
  10.9 5.2 %copy-start.6 = (s32[192]{0:T(256)S(1)}, s32[192]{0:T(256)}, u32[]{:S(2)}) copy-start(s32[192]{0:T(256)} %param.10) | copy-start | bytes 2308
  10.9 54.1 %copy-start.3 = (bf16[128,2,2048]{2,1,0:T(2,128)(2,1)S(1)}, bf16[128,2,2048]{2,1,0:T(2,128)(2,1)}, u32[]{:S(2)}) copy-start(bf16[128,2,2048]{2,1,0:T(2,128)(2,1)} %param.7) | copy-start | bytes 3145732
  10.9 54.1 %all-to-all-start = ((bf16[4,512,1024]{2,1,0:T(8,128)(2,1)}), bf16[4,512,1024]{2,1,0:T(8,128)(2,1)}, u32[]{:S(2)}, u32[]{:S(2)}) async-start(bf16[4,512,1024]{2,1,0:T(8,128)(2,1)} %broadcast_in_dim.38), calls=%async_computation | async-start | bytes 8388608 | tf_op jit(solution)/shard_map/all_to_all | solution.py:78
  68.6 0.8 copy-start.7
  86.2 117.5 %all-to-all-start.1 = ((bf16[128,4,2,1024]{3,2,1,0:T(2,128)(2,1)}), bf16[128,4,2,1024]{3,2,1,0:T(2,128)(2,1)S(1)}, u32[]{:S(2)}, u32[]{:S(2)}) async-start(bf16[128,4,2,1024]{3,2,1,0:T(2,128)(2,1)} %bitcast.9), calls=%async_computation.1 | async-start | bytes 4194304 | tf_op jit(solution)/shard_map/all_to_all | solution.py:96
  106.2 101.0 %all-gather.11.cloned.1.call-start = ((), (), s32[]{:S(2)}) async-start(), calls=%async_computation.9 | async-start | bytes 2621440 | tf_op jit(solution)/shard_map/all_gather | solution.py:104
  110.3 6.1 %copy-start.9 = (s32[192]{0:T(256)S(1)}, s32[192]{0:T(256)}, u32[]{:S(2)}) copy-start(s32[192]{0:T(256)} %param.11) | copy-start | bytes 2308
  111.5 95.8 %all-gather.13.cloned.1.call-start = ((), (), s32[]{:S(2)}) async-start(), calls=%async_computation.10 | async-start | bytes 2621440 | tf_op jit(solution)/shard_map/all_gather | solution.py:104
  203.7 1.3 copy-start
  207.6 2.7 copy-start.4
  210.3 1.0 copy-start.10
  213.3 10.5 %copy-start.11 = (f32[512,512]{0,1:T(8,128)S(1)}, f32[512,512]{0,1:T(8,128)}, u32[]{:S(2)}) copy-start(f32[512,512]{0,1:T(8,128)} %copy-done.10) | copy-start | bytes 3145732
  213.3 64.8 %all-to-all-start.2 = ((bf16[128,4,1024]{2,1,0:T(4,128)(2,1)}), bf16[128,4,1024]{2,1,0:T(4,128)(2,1)S(1)}, u32[]{:S(2)}, u32[]{:S(2)}) async-start(bf16[128,4,1024]{2,1,0:T(4,128)(2,1)} %reshape.209), calls=%async_computation.2 | async-start | bytes 2097152 | tf_op jit(solution)/shard_map/all_to_all | solution.py:117
  278.4 1.9 copy-start.5
  281.5 62.9 %all-to-all-start.3 = ((bf16[128,4,1024]{2,1,0:T(4,128)(2,1)}), bf16[128,4,1024]{2,1,0:T(4,128)(2,1)}, u32[]{:S(2)}, u32[]{:S(2)}) async-start(bf16[128,4,1024]{2,1,0:T(4,128)(2,1)} %reshape.211), calls=%async_computation.3 | async-start | bytes 2097152 | tf_op jit(solution)/shard_map/all_to_all | solution.py:117
  290.5 57.3 %all-gather.7.cloned.1.call-start = ((), (), s32[]{:S(2)}) async-start(), calls=%async_computation.6 | async-start | bytes 1310720 | tf_op jit(solution)/shard_map/all_gather | solution.py:130
  291.2 79.2 %all-gather.9.cloned.1.call-start = ((), (), s32[]{:S(2)}) async-start(), calls=%async_computation.7 | async-start | bytes 1310720 | tf_op jit(solution)/shard_map/all_gather | solution.py:130
  346.6 1.1 copy-start.1
  347.7 48.4 %reduce-scatter.2.cloned.1.call-start = ((), (), s32[]{:S(2)}) async-start(), calls=%async_computation.8 | async-start | bytes 1572864 | tf_op jit(solution)/shard_map/reduce_scatter | solution.py:139
  376.5 37.5 %copy-start.2 = (bf16[128,1024]{1,0:T(8,128)(2,1)S(1)}, bf16[128,1024]{1,0:T(8,128)(2,1)}, u32[]{:S(2)}) copy-start(bf16[128,1024]{1,0:T(8,128)(2,1)} %copy-done.1) | copy-start | bytes 786436
  398.1 48.1 %all-to-all-start.4 = ((bf16[64,4,1024]{2,1,0:T(4,128)(2,1)}), bf16[64,4,1024]{2,1,0:T(4,128)(2,1)S(1)}, u32[]{:S(2)}, u32[]{:S(2)}) async-start(bf16[64,4,1024]{2,1,0:T(4,128)(2,1)} %reshape.213), calls=%async_computation.5 | async-start | bytes 1048576 | tf_op jit(solution)/shard_map/all_to_all | solution.py:143
Sparse Core Ops, SparseCore 0:
  111.6 37.0 all-gather.10
  150.8 38.6 all-gather.12
  293.4 30.2 all-gather.6
  347.8 22.5 all-gather.8
  376.7 19.3 reduce-scatter.1

commit v6 on v4

--- a/solution.py
+++ b/solution.py
@@ -74,9 +74,15 @@
     per_owner = per_bin * MOSTB
     group_slots = sources * per_owner
     flat = features.reshape(rows_dev * views, feat_dim)
-    copies = jnp.broadcast_to(head_weight[None], (bins_n, part_rows, emb_dim))
-    weight = lax.all_to_all(copies, "bin", split_axis=0, concat_axis=0, tiled=True)
-    weight = weight.reshape(feat_dim, emb_dim)
+    core = lax.axis_index("dc")
+    halves = head_weight.reshape(2, part_rows // 2, emb_dim)
+    half = lax.dynamic_index_in_dim(halves, core, 0, keepdims=False)
+    copies = jnp.broadcast_to(half[None], (bins_n, part_rows // 2, emb_dim))
+    mine = lax.all_to_all(copies, "bin", split_axis=0, concat_axis=0, tiled=True)
+    theirs = lax.ppermute(mine, "dc", perm=[(0, 1), (1, 0)])
+    low = jnp.where(core == 0, mine, theirs)
+    high = jnp.where(core == 0, theirs, mine)
+    weight = jnp.stack([low, high], axis=1).reshape(feat_dim, emb_dim)
     folded = jnp.dot(flat, weight, preferred_element_type=jnp.float32)
     embedded = folded.reshape(rows_dev, views, emb_dim)
     scale = lax.rsqrt(jnp.sum(embedded * embedded, axis=2, keepdims=True) + 1e-06)

time: 443 us -> 433 us (0.977)
  blocking collectives: 0 us -> 78.5 us
  waiting for transfers between devices: 319 us -> 241 us
  starting transfers between devices: 51.6 us -> 32.7 us
  local copies, waits for them, and re-layouts: 35.8 us -> 41.1 us
  other arithmetic: 8.78 us -> 13.5 us
    all_to_all x2 -> x0, waiting for transfers between devices: 79.5 us -> none  [the longest x1 48.6 us: local(): lax.all_to_all(copies, 'bin', split_axis=0, concat_axis=0, tiled=True)]
    all_to_all x0 -> x2, blocking collectives: none -> 78.5 us  [the longest x1 47.9 us: local(): lax.all_to_all(planes, ('dx', 'dz'), split_axis=0, concat_axis=0, tiled=T...]
    all_to_all x2 -> x0, starting transfers between devices: 20.9 us -> none  [the longest x1 15.9 us: local(): lax.all_to_all(planes, ('dx', 'dz'), split_axis=0, concat_axis=0, tiled=T...]
    scatter x1, local copies, waits for them, and re-layouts: 4.29 us -> 10.9 us  [local(): outbox = empty.at[target].set(sent)]
  transfers between devices with their start and end apart: 7 -> 6, of which waited for: 6 -> 5; matrix products, arithmetic and copies ran while one was open for 4% -> 5% of each run, Pallas kernels for 0% -> 0%
where the time goes in v6:
time: 433 us; the launch traced here: 432 us
  waiting for transfers between devices  241 us (56%)
  blocking collectives  78.5 us (18%)
  local copies, waits for them, and re-layouts  41.1 us (9%)
  starting transfers between devices  32.7 us (8%)
  between operations  16 us (4%)
  other arithmetic  13.5 us (3%)
  matrix products  9.19 us (2%)
    all_to_all x1, waiting for transfers between devices, local(): lax.all_to_all(grads.reshape(sources, per_owner, views, emb_dim), DP, spl...  96.7 us
    all_to_all x1, waiting for transfers between devices, local(): lax.all_to_all(outbox.reshape(sources, per_owner, views, emb_dim), DP, sp...  94.3 us
    all_to_all x1, blocking collectives, local(): lax.all_to_all(planes, ('dx', 'dz'), split_axis=0, concat_axis=0, tiled=T...  47.9 us
    all_to_all x1, blocking collectives, local(): lax.all_to_all(copies, 'bin', split_axis=0, concat_axis=0, tiled=True)  30.6 us
    all_gather x1, waiting for transfers between devices, local(): outgrad = lax.all_gather(grad_rows, 'bin', axis=0, tiled=True)  27.1 us
    reduce_scatter x1, waiting for transfers between devices, local(): lax.psum_scatter(local_grad.reshape(part_rows, emb_dim), 'dc', scatter_di...  20.3 us
    all_to_all x1, starting transfers between devices, local(): lax.all_to_all(outbox.reshape(sources, per_owner, views, emb_dim), DP, sp...  20 us
    scatter x1, local copies, waits for them, and re-layouts, local(): outbox = empty.at[target].set(sent)  10.9 us
  transfers between devices with their start and end apart: 6, of which 5 were waited for; matrix products, arithmetic and copies ran while one was open for 5% of the time, Pallas kernels for 0%

profile of v6, /device:TPU:6, one launch (start us, length us, event | category | flops | bytes accessed | tf_op | source)
XLA Modules:
  0.0 431.6 jit_solution(1600840469729161802)
XLA Ops:
  7.2 1.2 copy-done
  8.4 0.3 broadcast_in_dim.41
  8.7 30.6 %all_to_all.20 = bf16[4,256,1024]{2,1,0:T(8,128)(2,1)S(1)} all-to-all(bf16[4,256,1024]{2,1,0:T(8,128)(2,1)S(1)} %broadcast_in_dim.41), channel_id=1, replica_groups=mesh['dx'=4,'dz'=16,'dc'=2,'bin'=4] {'bin'}, dimensions={0} | all-to-all | bytes 4194304 | tf_op jit(solution)/shard_map/all_to_all | solution.py:81
  39.3 2.0 collective-permute-start
  41.4 2.3 reshape.174
  43.6 0.2 convert_reduce_fusion.2
  43.8 0.2 convert_reduce_fusion.1
  44.0 0.1 select_reduce_fusion.1
  44.1 1.5 collective-permute-done
  45.6 1.9 select_bitcast_fusion.1
  47.5 0.4 pad_maximum_fusion
  47.9 0.8 copy-done.5
  48.7 1.3 multiply_reduce_fusion.1
  50.1 0.6 reshape.175
  50.7 0.1 rsqrt.13
  50.9 0.2 copy-done.4
  51.0 0.7 copy-done.2
  51.7 1.2 multiply_convert_fusion.4
  52.9 1.1 scatter.12
  54.0 10.9 %scatter_fusion = bf16[512,2,1024]{2,1,0:T(2,128)(2,1)S(1)} fusion(bf16[512,2,1024]{2,1,0:T(2,128)(2,1)S(1)} %scatter.12, s32[128]{0:T(128)S(1)} %fusion.22, bf16[128,2,1024]{2,1,0:T(2,128)(2,1)} %multiply_convert_fusion.4), kind=kCustom, calls=%fused_computation.1 | custom fusion | bytes 1573376 | tf_op jit(solution)/shard_map/scatter | solution.py:101
  64.9 1.3 copy-done.1
  66.2 20.0 %all-to-all-start.1 = ((bf16[128,4,2,1024]{3,2,1,0:T(2,128)(2,1)}), bf16[128,4,2,1024]{3,2,1,0:T(2,128)(2,1)S(1)}, u32[]{:S(2)}, u32[]{:S(2)}) async-start(bf16[128,4,2,1024]{3,2,1,0:T(2,128)(2,1)} %bitcast.61), calls=%async_computation.1 | async-start | bytes 4194304 | tf_op jit(solution)/shard_map/all_to_all | solution.py:102
  86.3 0.6 fusion.21
  88.9 0.1 pad_dynamic-slice_fusion
  89.0 0.6 fusion.25
  89.6 94.3 %all-to-all-done.1 = bf16[128,4,2,1024]{3,2,1,0:T(2,128)(2,1)S(1)} async-done(((bf16[128,4,2,1024]{3,2,1,0:T(2,128)(2,1)}), bf16[128,4,2,1024]{3,2,1,0:T(2,128)(2,1)S(1)}, u32[]{:S(2)}, u32[]{:S(2)}) %all-to-all-start.1) | async-done | bytes 2097184 | tf_op jit(solution)/shard_map/all_to_all | solution.py:102
  183.8 0.6 copy.35
  184.4 0.2 compare_reduce_fusion
  184.6 0.4 broadcast_select_fusion
  185.0 2.7 fusion.26
  187.7 0.8 multiply_convert_fusion.1
  188.5 1.7 multiply_convert_fusion
  190.2 0.4 stack.21
  190.6 1.5 stack.22
  192.1 2.7 pad_maximum_fusion.1
  194.8 10.3 %all-to-all-start.2 = ((bf16[128,4,2,1024]{3,1,2,0:T(4,128)(2,1)}), bf16[128,4,2,1024]{3,1,2,0:T(4,128)(2,1)S(1)}, u32[]{:S(2)}, u32[]{:S(2)}) async-start(bf16[128,4,2,1024]{3,1,2,0:T(4,128)(2,1)} %pad_maximum_fusion.1), calls=%async_computation.2 | async-start | bytes 4194304 | tf_op jit(solution)/shard_map/all_to_all | solution.py:115
  205.1 0.0 all-gather.3.cloned.1.call-start
  205.1 0.7 all-gather.3.cloned.1.call-update
  205.8 0.0 all-gather.5.cloned.1.call-start
  205.9 96.7 %all-to-all-done.2 = bf16[128,4,2,1024]{3,1,2,0:T(4,128)(2,1)S(1)} async-done(((bf16[128,4,2,1024]{3,1,2,0:T(4,128)(2,1)}), bf16[128,4,2,1024]{3,1,2,0:T(4,128)(2,1)S(1)}, u32[]{:S(2)}, u32[]{:S(2)}) %all-to-all-start.2) | async-done | bytes 2097184 | tf_op jit(solution)/shard_map/all_to_all | solution.py:115
  302.6 3.7 copy.30
  306.3 3.2 gather_fusion
  309.6 1.1 reshape.182
  310.7 1.8 multiply_reduce_fusion
  312.5 0.1 mul.96
  312.6 1.7 multiply_convert_fusion.2
  314.3 0.3 reduce-scatter.2.cloned.1.call-start
  314.6 0.0 all-gather.3.cloned.1.call-done
  314.6 1.9 constant_dynamic-slice_fusion
  316.6 0.4 reshape.179
  317.0 0.5 copy.31
  317.6 1.2 dot_general.27
  318.8 27.1 %all-gather.5.cloned.1.call-done = bf16[512,2,1024]{2,1,0:T(2,128)(2,1)} async-done(((bf16[128,2,1024]{2,1,0:T(2,128)(2,1)}), bf16[512,2,1024]{2,1,0:T(2,128)(2,1)}) %all-gather.5.cloned.1.call-update) | async-done | bytes 2097168 | tf_op jit(solution)/shard_map/all_gather | solution.py:128
  345.9 2.7 reshape.199
  348.6 2.7 fusion.2
  351.3 1.4 copy.33
  352.7 1.8 reshape.181
  354.5 0.0 reduce-scatter.2.cloned.1.call-update
  354.5 20.3 %reduce-scatter.2.cloned.1.call-done = f32[256,1024]{1,0:T(8,128)} async-done(((f32[512,1024]{1,0:T(8,128)}), f32[256,1024]{1,0:T(8,128)}) %reduce-scatter.2.cloned.1.call-update) | async-done | bytes 1048592 | tf_op jit(solution)/shard_map/reduce_scatter | solution.py:140
  374.8 1.3 convert_element_type.66
  376.1 0.2 convert_element_type.67
  376.3 47.9 %all_to_all.21 = bf16[64,4,1024]{2,1,0:T(4,128)(2,1)S(1)} all-to-all(bf16[64,4,1024]{2,1,0:T(4,128)(2,1)S(1)} %convert_element_type.67), channel_id=1, replica_groups=mesh['dx'=4,'dz'=16,'dc'=2,'bin'=4] {'dx','dz'}, dimensions={0} | all-to-all | bytes 1048576 | tf_op jit(solution)/shard_map/all_to_all | solution.py:144
  424.2 0.2 convert_reduce_fusion
  424.5 0.6 broadcast_multiply_fusion
  (22 shorter events, 0.1 us)
Async XLA Ops:
  7.2 1.2 copy-start
  39.3 4.3 %copy-start.8 = (s32[128,1]{0,1:T(1,128)S(1)}, s32[128,1]{0,1:T(1,128)}, u32[]{:S(2)}) copy-start(s32[128,1]{0,1:T(1,128)} %param.9) | copy-start | bytes 1540
  39.3 4.5 %copy-start.6 = (s32[192]{0:T(256)S(1)}, s32[192]{0:T(256)}, u32[]{:S(2)}) copy-start(s32[192]{0:T(256)} %param.10) | copy-start | bytes 2308
  39.3 6.3 %collective-permute-start = (bf16[4,256,1024]{2,1,0:T(8,128)(2,1)S(1)}, bf16[4,256,1024]{2,1,0:T(8,128)(2,1)}, u32[]{:S(2)}, u32[]{:S(2)}) collective-permute-start(bf16[4,256,1024]{2,1,0:T(8,128)(2,1)S(1)} %all_to_all.20), channel_id=1, source_target_pairs={{0,4},{4,0},{1,5},{5,1},{2,6},{6,2},{3,7},{7,3},{8,12},{12,8},{9,1... | collective-permute-start | bytes 6291464 | tf_op jit(solution)/shard_map/ppermute | solution.py:82
  47.5 1.2 copy-start.5
  50.0 1.0 copy-start.4
  50.0 2.9 copy-start.7
  50.7 1.0 copy-start.2
  64.9 1.4 copy-start.1
  66.2 22.6 %copy-start.9 = (s32[192]{0:T(256)S(1)}, s32[192]{0:T(256)}, u32[]{:S(2)}) copy-start(s32[192]{0:T(256)} %param.11) | copy-start | bytes 2308
  66.2 117.6 %all-to-all-start.1 = ((bf16[128,4,2,1024]{3,2,1,0:T(2,128)(2,1)}), bf16[128,4,2,1024]{3,2,1,0:T(2,128)(2,1)S(1)}, u32[]{:S(2)}, u32[]{:S(2)}) async-start(bf16[128,4,2,1024]{3,2,1,0:T(2,128)(2,1)} %bitcast.61), calls=%async_computation.1 | async-start | bytes 4194304 | tf_op jit(solution)/shard_map/all_to_all | solution.py:102
  194.8 107.8 %all-to-all-start.2 = ((bf16[128,4,2,1024]{3,1,2,0:T(4,128)(2,1)}), bf16[128,4,2,1024]{3,1,2,0:T(4,128)(2,1)S(1)}, u32[]{:S(2)}, u32[]{:S(2)}) async-start(bf16[128,4,2,1024]{3,1,2,0:T(4,128)(2,1)} %pad_maximum_fusion.1), calls=%async_computation.2 | async-start | bytes 4194304 | tf_op jit(solution)/shard_map/all_to_all | solution.py:115
  205.1 109.5 %all-gather.3.cloned.1.call-start = ((), (), s32[]{:S(2)}) async-start(), calls=%async_computation.5 | async-start | bytes 5242880 | tf_op jit(solution)/shard_map/all_gather | solution.py:127
  205.8 140.0 %all-gather.5.cloned.1.call-start = ((), (), s32[]{:S(2)}) async-start(), calls=%async_computation.6 | async-start | bytes 2621440 | tf_op jit(solution)/shard_map/all_gather | solution.py:128
  309.5 3.1 copy-start.3
  314.3 60.5 %reduce-scatter.2.cloned.1.call-start = ((), (), s32[]{:S(2)}) async-start(), calls=%async_computation.7 | async-start | bytes 3145728 | tf_op jit(solution)/shard_map/reduce_scatter | solution.py:140
Sparse Core Ops, SparseCore 0:
  208.0 54.6 all-gather.2
  314.5 31.3 all-gather.4
  354.6 20.1 reduce-scatter.1

commit v7 on v6

--- a/solution.py
+++ b/solution.py
@@ -97,8 +97,15 @@
     earlier = (row_bins[:, None] == row_bins[None, :]) & (order[None, :] < order[:, None])
     seat = jnp.sum(earlier.astype(jnp.int32), axis=1)
     target = owner * per_owner + local_bin * per_bin + seat
-    empty = jnp.zeros((group_slots, views, emb_dim), jnp.bfloat16).at[:, 0, 0].set(EMPTY_MARK)
-    outbox = empty.at[target].set(sent)
+    picks = target[None, :] == jnp.arange(group_slots, dtype=jnp.int32)[:, None]
+    picked = jnp.dot(
+        picks.astype(jnp.bfloat16),
+        sent.reshape(rows_dev, views * emb_dim),
+        preferred_element_type=jnp.float32,
+    ).reshape(group_slots, views, emb_dim)
+    unfilled = 1.0 - jnp.any(picks, axis=1).astype(jnp.float32)
+    mark = jnp.zeros((views, emb_dim), jnp.float32).at[0, 0].set(EMPTY_MARK)
+    outbox = (picked + unfilled[:, None, None] * mark[None]).astype(jnp.bfloat16)
     inbox = lax.all_to_all(
         outbox.reshape(sources, per_owner, views, emb_dim),
         DP,
@@ -119,13 +126,24 @@
         concat_axis=0,
         tiled=True,
     )
-    row_grads = returned.reshape(group_slots, views, emb_dim)[target].astype(jnp.float32)
+    row_grads = lax.dot_general(
+        picks.astype(jnp.bfloat16),
+        returned.reshape(group_slots, views * emb_dim),
+        (((0,), (0,)), ((), ())),
+        preferred_element_type=jnp.float32,
+    ).reshape(rows_dev, views, emb_dim)
     grad_rows = (
         scale * (row_grads - unit * jnp.sum(unit * row_grads, axis=2, keepdims=True))
     ).astype(jnp.bfloat16)
     column_start = lax.axis_index("bin") * part_rows
     trunk = lax.all_gather(features, "bin", axis=0, tiled=True)
-    outgrad = lax.all_gather(grad_rows, "bin", axis=0, tiled=True)
+    outgrad = lax.all_to_all(
+        jnp.broadcast_to(grad_rows[None], (bins_n, *grad_rows.shape)),
+        "bin",
+        split_axis=0,
+        concat_axis=0,
+        tiled=True,
+    )
     columns = lax.dynamic_slice_in_dim(trunk, column_start, part_rows, 2)
     count = trunk.shape[0]
     local_grad = lax.dot_general(
@@ -137,9 +155,9 @@
     sizes = [size for _, size in DP_PARTS]
     per_dev = part_rows // sources
     local_grad = jnp.transpose(local_grad.reshape(*sizes, per_dev, emb_dim), (2, 0, 1, 3, 4))
-    local_grad = lax.psum_scatter(
-        local_grad.reshape(part_rows, emb_dim), "dc", scatter_dimension=0, tiled=True
-    )
+    kept = lax.dynamic_index_in_dim(local_grad, core, 0, keepdims=False)
+    given = lax.dynamic_index_in_dim(local_grad, 1 - core, 0, keepdims=False)
+    local_grad = kept + lax.ppermute(given, "dc", perm=[(0, 1), (1, 0)])
     planes = local_grad.reshape(sizes[0] * sizes[1], per_dev, emb_dim).astype(jnp.bfloat16)
     planes = lax.all_to_all(planes, ("dx", "dz"), split_axis=0, concat_axis=0, tiled=True)
     local_grad = jnp.sum(planes.astype(jnp.float32), axis=0)

time: 433 us -> 415 us (0.958)
  waiting for transfers between devices: 241 us -> 216 us
  other arithmetic: 13.5 us -> 24.8 us
  blocking collectives: 78.5 us -> 71.5 us
  starting transfers between devices: 32.7 us -> 38 us
    all_gather x1 -> x0, waiting for transfers between devices: 27.1 us -> none  [local(): outgrad = lax.all_gather(grad_rows, 'bin', axis=0, tiled=True)]
    all_to_all x0 -> x1, waiting for transfers between devices: none -> 20.7 us  [local(): lax.all_to_all(jnp.broadcast_to(grad_rows[None], (bins_n, *grad_rows.shap...]
    reduce_scatter x1 -> x0, waiting for transfers between devices: 20.3 us -> none  [local(): lax.psum_scatter(local_grad.reshape(part_rows, emb_dim), 'dc', scatter_di...]
    scatter x2 -> x0, local copies, waits for them, and re-layouts: 11.9 us -> none  [the longest x1 10.9 us: local(): outbox = empty.at[target].set(sent)]
    lt x1, other arithmetic: 0.15 us -> 9.14 us  [local(): valid = inbox[:, 0, 0] < 2.0]
    all_to_all x1, blocking collectives: 47.9 us -> 40.8 us  [local(): lax.all_to_all(planes, ('dx', 'dz'), split_axis=0, concat_axis=0, tiled=T...]
    another operation x2, local copies, waits for them, and re-layouts: 1.87 us -> 6.54 us  [contrast(): return jnp.stack([query_gradient, key_gradient_rows], axis=1)]
where the time goes in v7:
time: 415 us; the launch traced here: 414 us
  waiting for transfers between devices  216 us (52%)
  blocking collectives  71.5 us (17%)
  starting transfers between devices  38 us (9%)
  local copies, waits for them, and re-layouts  36.8 us (9%)
  other arithmetic  24.8 us (6%)
  between operations  16.3 us (4%)
  matrix products  11.4 us (3%)
    all_to_all x1, waiting for transfers between devices, local(): lax.all_to_all(grads.reshape(sources, per_owner, views, emb_dim), DP, spl...  94.9 us
    all_to_all x1, waiting for transfers between devices, local(): lax.all_to_all(outbox.reshape(sources, per_owner, views, emb_dim), DP, sp...  94.3 us
    all_to_all x1, blocking collectives, local(): lax.all_to_all(planes, ('dx', 'dz'), split_axis=0, concat_axis=0, tiled=T...  40.8 us
    all_to_all x1, blocking collectives, local(): lax.all_to_all(copies, 'bin', split_axis=0, concat_axis=0, tiled=True)  30.7 us
    all_to_all x1, waiting for transfers between devices, local(): lax.all_to_all(jnp.broadcast_to(grad_rows[None], (bins_n, *grad_rows.shap...  20.7 us
    all_to_all x1, starting transfers between devices, local(): lax.all_to_all(outbox.reshape(sources, per_owner, views, emb_dim), DP, sp...  20 us
    all_to_all x1, starting transfers between devices, local(): lax.all_to_all(grads.reshape(sources, per_owner, views, emb_dim), DP, spl...  10.3 us
    lt x1, other arithmetic, local(): valid = inbox[:, 0, 0] < 2.0  9.14 us
  transfers between devices with their start and end apart: 6, of which 5 were waited for; matrix products, arithmetic and copies ran while one was open for 5% of the time, Pallas kernels for 0%

profile of v7, /device:TPU:6, one launch (start us, length us, event | category | flops | bytes accessed | tf_op | source)
XLA Modules:
  0.0 414.3 jit_solution(13664411239125979977)
XLA Ops:
  7.2 1.2 copy-done
  8.4 0.3 broadcast_in_dim.45
  8.7 30.7 %all_to_all.25 = bf16[4,256,1024]{2,1,0:T(8,128)(2,1)S(1)} all-to-all(bf16[4,256,1024]{2,1,0:T(8,128)(2,1)S(1)} %broadcast_in_dim.45), channel_id=1, replica_groups=mesh['dx'=4,'dz'=16,'dc'=2,'bin'=4] {'bin'}, dimensions={0} | all-to-all | bytes 4194304 | tf_op jit(solution)/shard_map/all_to_all | solution.py:81
  39.4 2.0 collective-permute-start
  41.5 1.2 reshape.193
  42.7 0.2 convert_reduce_fusion.2
  42.9 0.2 convert_reduce_fusion.1
  43.1 0.1 select_reduce_fusion.1
  43.3 0.1 fusion.28
  43.4 2.3 collective-permute-done
  45.7 1.9 select_bitcast_fusion.1
  47.6 0.4 pad_maximum_fusion
  48.0 0.8 copy-done.5
  48.8 1.3 multiply_reduce_fusion
  50.2 0.3 reshape.194
  50.6 0.3 copy.74
  50.9 0.3 copy-done.3
  51.2 0.1 rsqrt.12
  51.3 0.1 copy.72
  51.4 0.1 fusion.14
  51.5 0.9 add_convert_fusion
  52.4 3.5 copy.90
  55.9 20.0 %all-to-all-start.1 = ((bf16[128,4,2,1024]{3,2,1,0:T(2,128)(2,1)}), bf16[128,4,2,1024]{3,2,1,0:T(2,128)(2,1)S(1)}, u32[]{:S(2)}, u32[]{:S(2)}) async-start(bf16[128,4,2,1024]{3,2,1,0:T(2,128)(2,1)} %bitcast.70), calls=%async_computation.1 | async-start | bytes 4194304 | tf_op jit(solution)/shard_map/all_to_all | solution.py:109
  75.9 0.6 fusion.43
  78.5 0.1 pad_dynamic-slice_fusion
  78.6 0.6 fusion.45
  79.2 94.3 %all-to-all-done.1 = bf16[128,4,2,1024]{3,2,1,0:T(2,128)(2,1)S(1)} async-done(((bf16[128,4,2,1024]{3,2,1,0:T(2,128)(2,1)}), bf16[128,4,2,1024]{3,2,1,0:T(2,128)(2,1)S(1)}, u32[]{:S(2)}, u32[]{:S(2)}) %all-to-all-start.1) | async-done | bytes 2097184 | tf_op jit(solution)/shard_map/all_to_all | solution.py:109
  173.5 9.1 %compare_reduce_fusion = pred[512]{0:T(512)(128)(4,1)S(1)} fusion(bf16[512,2,1024]{2,1,0:T(2,128)(2,1)S(1)} %bitcast.69), kind=kLoop, calls=%fused_computation.44 | loop fusion | flops 512 | bytes 1536 | tf_op jit(solution)/shard_map/lt | solution.py:117
  182.6 3.0 broadcast_select_fusion
  185.6 3.0 fusion.44
  188.6 2.7 fusion.46
  191.4 0.8 multiply_convert_fusion.1
  192.2 1.8 multiply_convert_fusion
  194.0 0.9 stack.24
  194.9 5.7 %stack.25 = bf16[128,4,1,1024]{3,2,1,0:T(2,128)(2,1)} reshape(bf16[512,1024]{1,0:T(8,128)(2,1)} %multiply_convert_fusion) | data formatting | bytes 2097152 | tf_op jit(solution)/shard_map/stack | solution.py:55
  200.6 6.7 %pad_maximum_fusion.1 = bf16[128,4,2,1024]{3,2,1,0:T(2,128)(2,1)} fusion(bf16[128,4,1,1024]{3,2,1,0:T(2,128)(2,1)} %stack.25, bf16[128,4,1,1024]{3,2,1,0:T(2,128)(2,1)S(1)} %stack.24), kind=kLoop, calls=%fused_computation.4 | loop fusion | flops 4194304 | bytes 4194304 | tf_op jit(solution)/shard_map/stack | solution.py:55
  207.2 10.3 %all-to-all-start.2 = ((bf16[128,4,2,1024]{3,2,1,0:T(2,128)(2,1)}), bf16[128,4,2,1024]{3,2,1,0:T(2,128)(2,1)S(1)}, u32[]{:S(2)}, u32[]{:S(2)}) async-start(bf16[128,4,2,1024]{3,2,1,0:T(2,128)(2,1)} %pad_maximum_fusion.1), calls=%async_computation.2 | async-start | bytes 4194304 | tf_op jit(solution)/shard_map/all_to_all | solution.py:122
  217.6 0.0 all-gather.2.cloned.1.call-start
  217.6 0.7 all-gather.2.cloned.1.call-update
  218.3 1.8 reshape.198
  220.1 94.9 %all-to-all-done.2 = bf16[128,4,2,1024]{3,2,1,0:T(2,128)(2,1)S(1)} async-done(((bf16[128,4,2,1024]{3,2,1,0:T(2,128)(2,1)}), bf16[128,4,2,1024]{3,2,1,0:T(2,128)(2,1)S(1)}, u32[]{:S(2)}, u32[]{:S(2)}) %all-to-all-start.2) | async-done | bytes 2097184 | tf_op jit(solution)/shard_map/all_to_all | solution.py:122
  315.1 1.9 copy.95
  317.0 2.9 copy.79
  319.9 0.8 fusion.31
  320.7 1.3 fusion.8
  322.0 0.5 copy.86
  322.6 2.4 broadcast_in_dim.53
  325.0 3.6 all-to-all-start.3
  328.6 0.0 all-gather.2.cloned.1.call-done
  328.6 1.9 constant_dynamic-slice_fusion
  330.6 1.2 reshape.199
  331.8 1.5 copy.81
  333.3 1.2 dot_general.47
  334.6 20.7 %all-to-all-done.3 = bf16[4,128,2,1024]{3,2,1,0:T(2,128)(2,1)S(1)} async-done(((bf16[4,128,2,1024]{3,2,1,0:T(2,128)(2,1)}), bf16[4,128,2,1024]{3,2,1,0:T(2,128)(2,1)S(1)}, u32[]{:S(2)}, u32[]{:S(2)}) %all-to-all-start.3) | async-done | bytes 2097184 | tf_op jit(solution)/shard_map/all_to_all | solution.py:140
  355.2 2.2 reshape.203
  357.4 3.0 fusion.1
  360.5 0.1 dynamic-slice_bitcast_fusion
  360.6 1.9 collective-permute-start.1
  362.5 2.6 collective-permute-done.1
  365.2 0.2 fusion.13
  365.4 0.4 copy.85
  365.8 40.8 %all_to_all.26 = bf16[64,4,1024]{2,1,0:T(4,128)(2,1)S(1)} all-to-all(bf16[64,4,1024]{2,1,0:T(4,128)(2,1)S(1)} %copy.85), channel_id=1, replica_groups=mesh['dx'=4,'dz'=16,'dc'=2,'bin'=4] {'dx','dz'}, dimensions={0} | all-to-all | bytes 1048576 | tf_op jit(solution)/shard_map/all_to_all | solution.py:162
  406.6 0.2 convert_reduce_fusion
  406.8 0.6 broadcast_multiply_fusion
  (26 shorter events, 0.2 us)
Async XLA Ops:
  7.2 1.2 copy-start
  8.7 32.8 %copy-start.2 = (bf16[128,2,2048]{2,1,0:T(2,128)(2,1)S(1)}, bf16[128,2,2048]{2,1,0:T(2,128)(2,1)}, u32[]{:S(2)}) copy-start(bf16[128,2,2048]{2,1,0:T(2,128)(2,1)} %param.7) | copy-start | bytes 3145732
  39.4 3.3 copy-start.8
  39.4 3.5 copy-start.7
  39.4 6.3 %collective-permute-start = (bf16[4,256,1024]{2,1,0:T(8,128)(2,1)S(1)}, bf16[4,256,1024]{2,1,0:T(8,128)(2,1)}, u32[]{:S(2)}, u32[]{:S(2)}) collective-permute-start(bf16[4,256,1024]{2,1,0:T(8,128)(2,1)S(1)} %all_to_all.25), channel_id=1, source_target_pairs={{0,4},{4,0},{1,5},{5,1},{2,6},{6,2},{3,7},{7,3},{8,12},{12,8},{9,1... | collective-permute-start | bytes 6291464 | tf_op jit(solution)/shard_map/ppermute | solution.py:82
  47.6 1.2 copy-start.5
  50.2 1.0 copy-start.3
  50.5 1.0 copy-start.10
  55.9 22.6 %copy-start.9 = (s32[192]{0:T(256)S(1)}, s32[192]{0:T(256)}, u32[]{:S(2)}) copy-start(s32[192]{0:T(256)} %param.11) | copy-start | bytes 2308
  55.9 117.6 %all-to-all-start.1 = ((bf16[128,4,2,1024]{3,2,1,0:T(2,128)(2,1)}), bf16[128,4,2,1024]{3,2,1,0:T(2,128)(2,1)S(1)}, u32[]{:S(2)}, u32[]{:S(2)}) async-start(bf16[128,4,2,1024]{3,2,1,0:T(2,128)(2,1)} %bitcast.70), calls=%async_computation.1 | async-start | bytes 4194304 | tf_op jit(solution)/shard_map/all_to_all | solution.py:109
  207.2 107.8 %all-to-all-start.2 = ((bf16[128,4,2,1024]{3,2,1,0:T(2,128)(2,1)}), bf16[128,4,2,1024]{3,2,1,0:T(2,128)(2,1)S(1)}, u32[]{:S(2)}, u32[]{:S(2)}) async-start(bf16[128,4,2,1024]{3,2,1,0:T(2,128)(2,1)} %pad_maximum_fusion.1), calls=%async_computation.2 | async-start | bytes 4194304 | tf_op jit(solution)/shard_map/all_to_all | solution.py:122
  217.6 111.1 %all-gather.2.cloned.1.call-start = ((), (), s32[]{:S(2)}) async-start(), calls=%async_computation.5 | async-start | bytes 5242880 | tf_op jit(solution)/shard_map/all_gather | solution.py:139
  322.6 2.4 copy-start.4
  325.0 30.2 %all-to-all-start.3 = ((bf16[4,128,2,1024]{3,2,1,0:T(2,128)(2,1)}), bf16[4,128,2,1024]{3,2,1,0:T(2,128)(2,1)S(1)}, u32[]{:S(2)}, u32[]{:S(2)}) async-start(bf16[4,128,2,1024]{3,2,1,0:T(2,128)(2,1)} %broadcast_in_dim.53), calls=%async_computation.3 | async-start | bytes 4194304 | tf_op jit(solution)/shard_map/all_to_all | solution.py:140
  334.6 22.9 %copy-start.6 = (bf16[4,16,2,4,1024]{4,3,2,1,0:T(4,128)(2,1)S(1)}, bf16[4,16,2,4,1024]{4,3,2,1,0:T(4,128)(2,1)}, u32[]{:S(2)}) copy-start(bf16[4,16,2,4,1024]{4,3,2,1,0:T(4,128)(2,1)} %dot_general.47) | copy-start | bytes 3145732
  360.6 4.6 %collective-permute-start.1 = (f32[4,16,4,1024]{3,1,2,0:T(8,128)S(1)}, f32[4,16,4,1024]{3,1,2,0:T(8,128)S(1)}, u32[]{:S(2)}, u32[]{:S(2)}) collective-permute-start(f32[4,16,4,1024]{3,1,2,0:T(8,128)S(1)} %dynamic-slice_bitcast_fusion), channel_id=1, source_target_pairs={{0,4},{4,0},{1,5},{5,1},{2,6},{6,2},{3,7},{7,3},{8,12},{12,8},{9,1... | collective-permute-start | bytes 3145736 | tf_op jit(solution)/shard_map/ppermute | solution.py:160
  365.2 42.3 %copy-start.1 = (bf16[512,1024]{1,0:T(8,128)(2,1)S(1)}, bf16[512,1024]{1,0:T(8,128)(2,1)}, u32[]{:S(2)}) copy-start(bf16[512,1024]{1,0:T(8,128)(2,1)} %param.8) | copy-start | bytes 3145732
Sparse Core Ops, SparseCore 0:
  220.5 54.6 all-gather.1

commit v8 on v7

--- a/solution.py
+++ b/solution.py
@@ -52,7 +52,7 @@
         )
         / SOFTMAX_TEMP_SCALE
     ).astype(jnp.bfloat16)
-    return jnp.stack([query_gradient, key_gradient_rows], axis=1)
+    return query_gradient, key_gradient_rows
 
 
 def dp_index():
@@ -97,38 +97,37 @@
     earlier = (row_bins[:, None] == row_bins[None, :]) & (order[None, :] < order[:, None])
     seat = jnp.sum(earlier.astype(jnp.int32), axis=1)
     target = owner * per_owner + local_bin * per_bin + seat
-    picks = target[None, :] == jnp.arange(group_slots, dtype=jnp.int32)[:, None]
+    block = views * per_owner
+    dest = (
+        (target // per_owner)[:, None] * block
+        + jnp.arange(views, dtype=jnp.int32)[None, :] * per_owner
+        + (target % per_owner)[:, None]
+    )
+    lanes = sources * block
+    picks = (dest.reshape(-1)[None, :] == jnp.arange(lanes, dtype=jnp.int32)[:, None]).astype(jnp.bfloat16)
     picked = jnp.dot(
-        picks.astype(jnp.bfloat16),
-        sent.reshape(rows_dev, views * emb_dim),
-        preferred_element_type=jnp.float32,
-    ).reshape(group_slots, views, emb_dim)
-    unfilled = 1.0 - jnp.any(picks, axis=1).astype(jnp.float32)
-    mark = jnp.zeros((views, emb_dim), jnp.float32).at[0, 0].set(EMPTY_MARK)
-    outbox = (picked + unfilled[:, None, None] * mark[None]).astype(jnp.bfloat16)
+        picks, sent.reshape(rows_dev * views, emb_dim), preferred_element_type=jnp.float32
+    )
+    unfilled = 1.0 - jnp.sum(picks.astype(jnp.float32), axis=1)
+    first_lane = (jnp.arange(emb_dim, dtype=jnp.int32) == 0).astype(jnp.float32)
+    outbox = (picked + (unfilled * EMPTY_MARK)[:, None] * first_lane[None, :]).astype(jnp.bfloat16)
     inbox = lax.all_to_all(
-        outbox.reshape(sources, per_owner, views, emb_dim),
-        DP,
-        split_axis=0,
-        concat_axis=0,
-        tiled=True,
+        outbox.reshape(sources, block, emb_dim), DP, split_axis=0, concat_axis=0, tiled=True
     )
-    inbox = inbox.reshape(group_slots, views, emb_dim)
-    valid = inbox[:, 0, 0] < 2.0
-    inbox = jnp.where(valid[:, None, None], inbox, jnp.zeros_like(inbox))
+    inbox = inbox.reshape(sources, views, per_owner, emb_dim)
+    valid = (inbox[:, 0, :, 0] < 2.0).reshape(group_slots)
+    query = jnp.where(valid[:, None], inbox[:, 0].reshape(group_slots, emb_dim), 0)
+    key = jnp.where(valid[:, None], inbox[:, 1].reshape(group_slots, emb_dim), 0)
     first = jnp.sum((bin_owner < dp_index()).astype(jnp.int32))
     allowed = allowed_mask(valid, first, bin_link, group_slots, per_bin)
-    grads = contrast(inbox[:, 0], inbox[:, 1], allowed, valid.astype(jnp.float32))
+    grads = contrast(query, key, allowed, valid.astype(jnp.float32))
+    back = jnp.stack([g.reshape(sources, per_owner, emb_dim) for g in grads], axis=1)
     returned = lax.all_to_all(
-        grads.reshape(sources, per_owner, views, emb_dim),
-        DP,
-        split_axis=0,
-        concat_axis=0,
-        tiled=True,
+        back.reshape(sources, block, emb_dim), DP, split_axis=0, concat_axis=0, tiled=True
     )
     row_grads = lax.dot_general(
-        picks.astype(jnp.bfloat16),
-        returned.reshape(group_slots, views * emb_dim),
+        picks,
+        returned.reshape(lanes, emb_dim),
         (((0,), (0,)), ((), ())),
         preferred_element_type=jnp.float32,
     ).reshape(rows_dev, views, emb_dim)

time: 415 us -> 400 us (0.964)
  other arithmetic: 24.8 us -> 6.73 us
    lt x1, other arithmetic: 9.14 us -> 0.15 us  [local(): valid = (inbox[:, 0, :, 0] < 2.0).reshape(group_slots)]
    select_n x0 -> x4, local copies, waits for them, and re-layouts: none -> 7.99 us  [the longest x2 4 us: local(): jnp.where(valid[:, None], inbox[:, 0].reshape(group_slots, emb_dim), 0)]
    another operation x1, other arithmetic: 6.68 us -> 0.19 us  [local(): jnp.stack([g.reshape(sources, per_owner, emb_dim) for g in grads], axis=1)]
  transfers between devices with their start and end apart: 6 -> 6, of which waited for: 5 -> 5; matrix products, arithmetic and copies ran while one was open for 5% -> 4% of each run, Pallas kernels for 0% -> 0%
where the time goes in v8:
time: 400 us; the launch traced here: 399 us
  waiting for transfers between devices  215 us (54%)
  blocking collectives  71.5 us (18%)
  starting transfers between devices  38.2 us (10%)
  local copies, waits for them, and re-layouts  36.8 us (9%)
  between operations  16.4 us (4%)
  matrix products  14.1 us (4%)
  other arithmetic  6.73 us (2%)
    all_to_all x1, waiting for transfers between devices, local(): lax.all_to_all(back.reshape(sources, block, emb_dim), DP, split_axis=0, c...  94.7 us
    all_to_all x1, waiting for transfers between devices, local(): lax.all_to_all(outbox.reshape(sources, block, emb_dim), DP, split_axis=0,...  94.3 us
    all_to_all x1, blocking collectives, local(): lax.all_to_all(planes, ('dx', 'dz'), split_axis=0, concat_axis=0, tiled=T...  40.8 us
    all_to_all x1, blocking collectives, local(): lax.all_to_all(copies, 'bin', split_axis=0, concat_axis=0, tiled=True)  30.7 us
    all_to_all x1, waiting for transfers between devices, local(): lax.all_to_all(jnp.broadcast_to(grad_rows[None], (bins_n, *grad_rows.shap...  20.7 us
    all_to_all x1, starting transfers between devices, local(): lax.all_to_all(outbox.reshape(sources, block, emb_dim), DP, split_axis=0,...  20 us
    all_to_all x1, starting transfers between devices, local(): lax.all_to_all(back.reshape(sources, block, emb_dim), DP, split_axis=0, c...  10.5 us
  transfers between devices with their start and end apart: 6, of which 5 were waited for; matrix products, arithmetic and copies ran while one was open for 4% of the time, Pallas kernels for 0%

profile of v8, /device:TPU:6, one launch (start us, length us, event | category | flops | bytes accessed | tf_op | source)
XLA Modules:
  0.0 398.5 jit_solution(14766309185677834837)
XLA Ops:
  7.2 1.2 copy-done
  8.4 0.3 broadcast_in_dim.88
  8.7 30.7 %all_to_all.25 = bf16[4,256,1024]{2,1,0:T(8,128)(2,1)S(1)} all-to-all(bf16[4,256,1024]{2,1,0:T(8,128)(2,1)S(1)} %broadcast_in_dim.88), channel_id=1, replica_groups=mesh['dx'=4,'dz'=16,'dc'=2,'bin'=4] {'bin'}, dimensions={0} | all-to-all | bytes 4194304 | tf_op jit(solution)/shard_map/all_to_all | solution.py:81
  39.4 2.0 collective-permute-start
  41.5 1.2 reshape.221
  42.8 0.2 convert_reduce_fusion.3
  42.9 0.2 convert_reduce_fusion.2
  43.6 0.2 convert_reduce_fusion.1
  43.9 1.9 collective-permute-done
  45.7 1.9 select_bitcast_fusion.1
  47.6 0.4 pad_maximum_fusion
  48.0 0.8 copy-done.5
  48.8 1.3 multiply_reduce_fusion
  50.2 2.2 fusion.5
  52.4 20.0 %all-to-all-start.1 = ((bf16[128,8,1024]{2,1,0:T(8,128)(2,1)}), bf16[128,8,1024]{2,1,0:T(8,128)(2,1)S(1)}, u32[]{:S(2)}, u32[]{:S(2)}) async-start(bf16[128,8,1024]{2,1,0:T(8,128)(2,1)} %fusion.5), calls=%async_computation.1 | async-start | bytes 4194304 | tf_op jit(solution)/shard_map/all_to_all | solution.py:114
  72.4 0.6 fusion.42
  75.1 0.6 fusion.49
  75.7 94.3 %all-to-all-done.1 = bf16[128,8,1024]{2,1,0:T(8,128)(2,1)S(1)} async-done(((bf16[128,8,1024]{2,1,0:T(8,128)(2,1)}), bf16[128,8,1024]{2,1,0:T(8,128)(2,1)S(1)}, u32[]{:S(2)}, u32[]{:S(2)}) %all-to-all-start.1) | async-done | bytes 2097184 | tf_op jit(solution)/shard_map/all_to_all | solution.py:114
  170.0 1.2 copy.80
  171.1 0.1 fusion.48
  171.3 0.3 broadcast_select_fusion
  171.6 1.8 copy.82
  173.4 2.2 select_n.125
  175.6 1.8 copy.83
  177.4 2.2 select_n.127
  179.6 0.9 copy.81
  180.6 0.8 copy.84
  181.4 1.1 reshape_squeeze.6
  182.5 0.5 copy-done.6
  183.0 4.0 fusion.50
  187.0 1.0 copy-done.12
  188.0 0.8 multiply_convert_fusion.1
  188.8 0.4 stack_reshape.6
  189.2 0.3 copy.86
  189.5 0.8 copy.85
  190.3 0.3 reshape_squeeze.7
  190.6 2.0 multiply_convert_fusion
  192.7 0.4 stack_reshape.7
  193.1 0.3 copy.87
  193.4 0.2 pad_maximum_fusion.1
  193.6 2.5 copy.88
  196.1 10.5 %all-to-all-start.2 = ((bf16[128,8,1024]{2,1,0:T(8,128)(2,1)}), bf16[128,8,1024]{2,1,0:T(8,128)(2,1)S(1)}, u32[]{:S(2)}, u32[]{:S(2)}) async-start(bf16[128,8,1024]{2,1,0:T(8,128)(2,1)} %copy.88), calls=%async_computation.2 | async-start | bytes 4194304 | tf_op jit(solution)/shard_map/all_to_all | solution.py:125
  206.7 0.7 all-gather.2.cloned.1.call-update
  207.4 1.8 reshape.226
  209.4 94.7 %all-to-all-done.2 = bf16[128,8,1024]{2,1,0:T(8,128)(2,1)S(1)} async-done(((bf16[128,8,1024]{2,1,0:T(8,128)(2,1)}), bf16[128,8,1024]{2,1,0:T(8,128)(2,1)S(1)}, u32[]{:S(2)}, u32[]{:S(2)}) %all-to-all-start.2) | async-done | bytes 2097184 | tf_op jit(solution)/shard_map/all_to_all | solution.py:125
  304.1 0.8 fusion.1
  304.9 1.3 fusion.11
  306.2 0.5 copy.95
  306.8 2.4 broadcast_in_dim.98
  309.2 3.6 all-to-all-start.3
  312.9 1.9 constant_dynamic-slice_fusion
  314.8 1.2 reshape.227
  316.1 1.5 copy.90
  317.5 1.2 dot_general.35
  318.8 20.7 %all-to-all-done.3 = bf16[4,128,2,1024]{3,2,1,0:T(2,128)(2,1)S(1)} async-done(((bf16[4,128,2,1024]{3,2,1,0:T(2,128)(2,1)}), bf16[4,128,2,1024]{3,2,1,0:T(2,128)(2,1)S(1)}, u32[]{:S(2)}, u32[]{:S(2)}) %all-to-all-start.3) | async-done | bytes 2097184 | tf_op jit(solution)/shard_map/all_to_all | solution.py:139
  339.4 2.2 reshape.230
  341.7 3.0 fusion.3
  344.8 1.9 collective-permute-start.1
  346.8 2.6 collective-permute-done.1
  349.4 0.2 fusion.12
  349.6 0.4 copy.94
  350.0 40.8 %all_to_all.26 = bf16[64,4,1024]{2,1,0:T(4,128)(2,1)S(1)} all-to-all(bf16[64,4,1024]{2,1,0:T(4,128)(2,1)S(1)} %copy.94), channel_id=1, replica_groups=mesh['dx'=4,'dz'=16,'dc'=2,'bin'=4] {'dx','dz'}, dimensions={0} | all-to-all | bytes 1048576 | tf_op jit(solution)/shard_map/all_to_all | solution.py:161
  390.8 0.2 convert_reduce_fusion
  391.1 0.6 broadcast_multiply_fusion
  (43 shorter events, 1.2 us)
Async XLA Ops:
  7.2 1.2 copy-start
  8.7 32.8 %copy-start.2 = (bf16[128,2,2048]{2,1,0:T(2,128)(2,1)S(1)}, bf16[128,2,2048]{2,1,0:T(2,128)(2,1)}, u32[]{:S(2)}) copy-start(bf16[128,2,2048]{2,1,0:T(2,128)(2,1)} %param.5) | copy-start | bytes 3145732
  39.4 3.3 copy-start.10
  39.4 3.5 copy-start.9
  39.4 6.3 %collective-permute-start = (bf16[4,256,1024]{2,1,0:T(8,128)(2,1)S(1)}, bf16[4,256,1024]{2,1,0:T(8,128)(2,1)}, u32[]{:S(2)}, u32[]{:S(2)}) collective-permute-start(bf16[4,256,1024]{2,1,0:T(8,128)(2,1)S(1)} %all_to_all.25), channel_id=1, source_target_pairs={{0,4},{4,0},{1,5},{5,1},{2,6},{6,2},{3,7},{7,3},{8,12},{12,8},{9,1... | collective-permute-start | bytes 6291464 | tf_op jit(solution)/shard_map/ppermute | solution.py:82
  47.6 1.2 copy-start.5
  50.2 2.2 copy-start.4
  52.4 22.6 %copy-start.11 = (s32[192]{0:T(256)S(1)}, s32[192]{0:T(256)}, u32[]{:S(2)}) copy-start(s32[192]{0:T(256)} %param.9) | copy-start | bytes 2308
  52.4 117.6 %all-to-all-start.1 = ((bf16[128,8,1024]{2,1,0:T(8,128)(2,1)}), bf16[128,8,1024]{2,1,0:T(8,128)(2,1)S(1)}, u32[]{:S(2)}, u32[]{:S(2)}) async-start(bf16[128,8,1024]{2,1,0:T(8,128)(2,1)} %fusion.5), calls=%async_computation.1 | async-start | bytes 4194304 | tf_op jit(solution)/shard_map/all_to_all | solution.py:114
  181.4 1.6 copy-start.6
  183.0 5.0 %copy-start.7 = (bf16[512,1024]{1,0:T(8,128)(2,1)S(1)}, bf16[512,1024]{1,0:T(8,128)(2,1)}, u32[]{:S(2)}) copy-start(bf16[512,1024]{1,0:T(8,128)(2,1)} %reshape_squeeze.6) | copy-start | bytes 3145732
  187.0 1.0 copy-start.12
  196.1 108.0 %all-to-all-start.2 = ((bf16[128,8,1024]{2,1,0:T(8,128)(2,1)}), bf16[128,8,1024]{2,1,0:T(8,128)(2,1)S(1)}, u32[]{:S(2)}, u32[]{:S(2)}) async-start(bf16[128,8,1024]{2,1,0:T(8,128)(2,1)} %copy.88), calls=%async_computation.2 | async-start | bytes 4194304 | tf_op jit(solution)/shard_map/all_to_all | solution.py:125
  206.7 106.2 %all-gather.2.cloned.1.call-start = ((), (), s32[]{:S(2)}) async-start(), calls=%async_computation.5 | async-start | bytes 5242880 | tf_op jit(solution)/shard_map/all_gather | solution.py:138
  306.8 2.4 copy-start.3
  309.2 30.2 %all-to-all-start.3 = ((bf16[4,128,2,1024]{3,2,1,0:T(2,128)(2,1)}), bf16[4,128,2,1024]{3,2,1,0:T(2,128)(2,1)S(1)}, u32[]{:S(2)}, u32[]{:S(2)}) async-start(bf16[4,128,2,1024]{3,2,1,0:T(2,128)(2,1)} %broadcast_in_dim.98), calls=%async_computation.3 | async-start | bytes 4194304 | tf_op jit(solution)/shard_map/all_to_all | solution.py:139
  318.8 22.9 %copy-start.8 = (bf16[4,16,2,4,1024]{4,3,2,1,0:T(4,128)(2,1)S(1)}, bf16[4,16,2,4,1024]{4,3,2,1,0:T(4,128)(2,1)}, u32[]{:S(2)}) copy-start(bf16[4,16,2,4,1024]{4,3,2,1,0:T(4,128)(2,1)} %dot_general.35) | copy-start | bytes 3145732
  344.8 4.6 %collective-permute-start.1 = (f32[4,16,4,1024]{3,1,2,0:T(8,128)S(1)}, f32[4,16,4,1024]{3,1,2,0:T(8,128)S(1)}, u32[]{:S(2)}, u32[]{:S(2)}) collective-permute-start(f32[4,16,4,1024]{3,1,2,0:T(8,128)S(1)} %dynamic-slice_bitcast_fusion), channel_id=1, source_target_pairs={{0,4},{4,0},{1,5},{5,1},{2,6},{6,2},{3,7},{7,3},{8,12},{12,8},{9,1... | collective-permute-start | bytes 3145736 | tf_op jit(solution)/shard_map/ppermute | solution.py:159
  349.4 42.3 %copy-start.1 = (bf16[512,1024]{1,0:T(8,128)(2,1)S(1)}, bf16[512,1024]{1,0:T(8,128)(2,1)}, u32[]{:S(2)}) copy-start(bf16[512,1024]{1,0:T(8,128)(2,1)} %param.6) | copy-start | bytes 3145732
Sparse Core Ops, SparseCore 0:
  209.6 54.6 all-gather.1

commit v9 on v8

--- a/solution.py
+++ b/solution.py
@@ -109,15 +109,17 @@
         picks, sent.reshape(rows_dev * views, emb_dim), preferred_element_type=jnp.float32
     )
     unfilled = 1.0 - jnp.sum(picks.astype(jnp.float32), axis=1)
+    lane_view = jnp.arange(lanes, dtype=jnp.int32) % block // per_owner
+    marked = unfilled * (lane_view == 0).astype(jnp.float32) * EMPTY_MARK
     first_lane = (jnp.arange(emb_dim, dtype=jnp.int32) == 0).astype(jnp.float32)
-    outbox = (picked + (unfilled * EMPTY_MARK)[:, None] * first_lane[None, :]).astype(jnp.bfloat16)
+    outbox = (picked + marked[:, None] * first_lane[None, :]).astype(jnp.bfloat16)
     inbox = lax.all_to_all(
         outbox.reshape(sources, block, emb_dim), DP, split_axis=0, concat_axis=0, tiled=True
     )
     inbox = inbox.reshape(sources, views, per_owner, emb_dim)
     valid = (inbox[:, 0, :, 0] < 2.0).reshape(group_slots)
-    query = jnp.where(valid[:, None], inbox[:, 0].reshape(group_slots, emb_dim), 0)
-    key = jnp.where(valid[:, None], inbox[:, 1].reshape(group_slots, emb_dim), 0)
+    query = inbox[:, 0].reshape(group_slots, emb_dim)
+    key = inbox[:, 1].reshape(group_slots, emb_dim)
     first = jnp.sum((bin_owner < dp_index()).astype(jnp.int32))
     allowed = allowed_mask(valid, first, bin_link, group_slots, per_bin)
     grads = contrast(query, key, allowed, valid.astype(jnp.float32))
@@ -157,8 +159,10 @@
     kept = lax.dynamic_index_in_dim(local_grad, core, 0, keepdims=False)
     given = lax.dynamic_index_in_dim(local_grad, 1 - core, 0, keepdims=False)
     local_grad = kept + lax.ppermute(given, "dc", perm=[(0, 1), (1, 0)])
-    planes = local_grad.reshape(sizes[0] * sizes[1], per_dev, emb_dim).astype(jnp.bfloat16)
-    planes = lax.all_to_all(planes, ("dx", "dz"), split_axis=0, concat_axis=0, tiled=True)
+    planes = local_grad.reshape(sizes[0], sizes[1] * per_dev, emb_dim)
+    planes = lax.all_to_all(planes, "dx", split_axis=0, concat_axis=0, tiled=True)
+    planes = jnp.sum(planes, axis=0).reshape(sizes[1], per_dev, emb_dim).astype(jnp.bfloat16)
+    planes = lax.all_to_all(planes, "dz", split_axis=0, concat_axis=0, tiled=True)
     local_grad = jnp.sum(planes.astype(jnp.float32), axis=0)
     grad_weight = local_grad / rows_dev
     return (grad_rows, grad_weight)

time: 400 us -> 386 us (0.965)
  local copies, waits for them, and re-layouts: 36.8 us -> 28 us
    select_n x4 -> x0, local copies, waits for them, and re-layouts: 7.99 us -> none  [the longest x2 4 us: local(): jnp.where(valid[:, None], inbox[:, 0].reshape(group_slots, emb_dim), 0)]
    all_to_all x1 -> x2, blocking collectives: 40.8 us -> 37.1 us  [the longest x1 19.3 us: local(): lax.all_to_all(planes, 'dx', split_axis=0, concat_axis=0, tiled=True)]
where the time goes in v9:
time: 386 us; the launch traced here: 385 us
  waiting for transfers between devices  215 us (56%)
  blocking collectives  67.8 us (18%)
  starting transfers between devices  38.2 us (10%)
  local copies, waits for them, and re-layouts  28 us (7%)
  between operations  16.4 us (4%)
  matrix products  13.5 us (3%)
  other arithmetic  6.23 us (2%)
    all_to_all x1, waiting for transfers between devices, local(): lax.all_to_all(back.reshape(sources, block, emb_dim), DP, split_axis=0, c...  94.7 us
    all_to_all x1, waiting for transfers between devices, local(): lax.all_to_all(outbox.reshape(sources, block, emb_dim), DP, split_axis=0,...  94.3 us
    all_to_all x1, blocking collectives, local(): lax.all_to_all(copies, 'bin', split_axis=0, concat_axis=0, tiled=True)  30.7 us
    all_to_all x1, waiting for transfers between devices, local(): lax.all_to_all(jnp.broadcast_to(grad_rows[None], (bins_n, *grad_rows.shap...  20.7 us
    all_to_all x1, starting transfers between devices, local(): lax.all_to_all(outbox.reshape(sources, block, emb_dim), DP, split_axis=0,...  20 us
    all_to_all x1, blocking collectives, local(): lax.all_to_all(planes, 'dx', split_axis=0, concat_axis=0, tiled=True)  19.3 us
    all_to_all x1, blocking collectives, local(): lax.all_to_all(planes, 'dz', split_axis=0, concat_axis=0, tiled=True)  17.8 us
    all_to_all x1, starting transfers between devices, local(): lax.all_to_all(back.reshape(sources, block, emb_dim), DP, split_axis=0, c...  10.3 us
  transfers between devices with their start and end apart: 6, of which 5 were waited for; matrix products, arithmetic and copies ran while one was open for 4% of the time, Pallas kernels for 0%

profile of v9, /device:TPU:6, one launch (start us, length us, event | category | flops | bytes accessed | tf_op | source)
XLA Modules:
  0.0 384.7 jit_solution(9121876979879127190)
XLA Ops:
  7.2 1.2 copy-done
  8.4 0.3 broadcast_in_dim.35
  8.7 30.7 %all_to_all.30 = bf16[4,256,1024]{2,1,0:T(8,128)(2,1)S(1)} all-to-all(bf16[4,256,1024]{2,1,0:T(8,128)(2,1)S(1)} %broadcast_in_dim.35), channel_id=1, replica_groups=mesh['dx'=4,'dz'=16,'dc'=2,'bin'=4] {'bin'}, dimensions={0} | all-to-all | bytes 4194304 | tf_op jit(solution)/shard_map/all_to_all | solution.py:81
  39.4 2.0 collective-permute-start
  41.5 1.2 reshape.231
  42.8 0.2 convert_reduce_fusion.3
  42.9 0.2 convert_reduce_fusion.2
  43.1 0.1 select_reduce_fusion.1
  43.5 0.1 add.161
  43.6 0.2 convert_reduce_fusion
  43.9 1.9 collective-permute-done
  45.7 1.9 select_bitcast_fusion.1
  47.6 0.4 pad_maximum_fusion
  48.0 0.8 copy-done.5
  48.8 1.3 multiply_reduce_fusion
  50.2 2.2 fusion.5
  52.4 20.0 %all-to-all-start.1 = ((bf16[128,8,1024]{2,1,0:T(8,128)(2,1)}), bf16[128,8,1024]{2,1,0:T(8,128)(2,1)S(1)}, u32[]{:S(2)}, u32[]{:S(2)}) async-start(bf16[128,8,1024]{2,1,0:T(8,128)(2,1)} %fusion.5), calls=%async_computation.1 | async-start | bytes 4194304 | tf_op jit(solution)/shard_map/all_to_all | solution.py:116
  72.4 0.6 fusion.42
  75.1 0.6 fusion.47
  75.7 94.3 %all-to-all-done.1 = bf16[128,8,1024]{2,1,0:T(8,128)(2,1)S(1)} async-done(((bf16[128,8,1024]{2,1,0:T(8,128)(2,1)}), bf16[128,8,1024]{2,1,0:T(8,128)(2,1)S(1)}, u32[]{:S(2)}, u32[]{:S(2)}) %all-to-all-start.1) | async-done | bytes 2097184 | tf_op jit(solution)/shard_map/all_to_all | solution.py:116
  170.0 1.2 copy.110
  171.1 0.2 fusion.46
  171.3 0.8 copy.113
  172.2 0.3 reshape_squeeze.6
  172.5 0.8 copy.114
  173.3 0.3 reshape_squeeze.7
  173.6 0.9 copy.112
  174.4 0.1 lt.103
  174.6 2.7 fusion.48
  177.2 1.8 multiply_convert_fusion.1
  179.0 1.7 multiply_convert_fusion
  180.7 0.4 stack_reshape.6
  181.2 0.3 copy.115
  181.5 0.5 copy-done.6
  182.0 0.4 stack_reshape.7
  182.4 0.3 copy.116
  182.7 0.2 pad_maximum_fusion.1
  182.9 2.5 copy.117
  185.4 10.3 %all-to-all-start.2 = ((bf16[128,8,1024]{2,1,0:T(8,128)(2,1)}), bf16[128,8,1024]{2,1,0:T(8,128)(2,1)S(1)}, u32[]{:S(2)}, u32[]{:S(2)}) async-start(bf16[128,8,1024]{2,1,0:T(8,128)(2,1)} %copy.117), calls=%async_computation.2 | async-start | bytes 4194304 | tf_op jit(solution)/shard_map/all_to_all | solution.py:127
  195.7 0.3 all-gather.2.cloned.1.call-start
  196.0 0.5 all-gather.2.cloned.1.call-update
  196.5 1.8 reshape.236
  198.3 0.1 rsqrt.13
  198.5 94.7 %all-to-all-done.2 = bf16[128,8,1024]{2,1,0:T(8,128)(2,1)S(1)} async-done(((bf16[128,8,1024]{2,1,0:T(8,128)(2,1)}), bf16[128,8,1024]{2,1,0:T(8,128)(2,1)S(1)}, u32[]{:S(2)}, u32[]{:S(2)}) %all-to-all-start.2) | async-done | bytes 2097184 | tf_op jit(solution)/shard_map/all_to_all | solution.py:127
  293.2 0.8 fusion.1
  294.0 1.3 fusion.11
  295.3 0.5 copy.125
  295.9 2.4 broadcast_in_dim.41
  298.3 3.6 all-to-all-start.3
  301.9 1.9 constant_dynamic-slice_fusion
  303.9 1.2 reshape.237
  305.1 1.5 copy.119
  306.6 1.2 dot_general.35
  307.8 20.7 %all-to-all-done.3 = bf16[4,128,2,1024]{3,2,1,0:T(2,128)(2,1)S(1)} async-done(((bf16[4,128,2,1024]{3,2,1,0:T(2,128)(2,1)}), bf16[4,128,2,1024]{3,2,1,0:T(2,128)(2,1)S(1)}, u32[]{:S(2)}, u32[]{:S(2)}) %all-to-all-start.3) | async-done | bytes 2097184 | tf_op jit(solution)/shard_map/all_to_all | solution.py:141
  328.5 2.2 reshape.241
  330.7 3.1 fusion.3
  333.9 1.9 collective-permute-start.1
  335.8 2.6 collective-permute-done.1
  338.5 0.2 bitcast_add_fusion
  338.6 0.7 copy.122
  339.3 0.6 copy.123
  339.9 19.3 %all_to_all.31 = f32[4,64,1024]{2,1,0:T(8,128)S(1)} all-to-all(f32[4,64,1024]{2,1,0:T(8,128)S(1)} %copy.123), channel_id=1, replica_groups=mesh['dx'=4,'dz'=16,'dc'=2,'bin'=4] {'dx'}, dimensions={0} | all-to-all | bytes 2097152 | tf_op jit(solution)/shard_map/all_to_all | solution.py:163
  359.3 17.8 %all_to_all.32 = bf16[16,4,1024]{2,1,0:T(4,128)(2,1)S(1)} all-to-all(bf16[16,4,1024]{2,1,0:T(4,128)(2,1)S(1)} %convert_element_type.77), channel_id=1, replica_groups=mesh['dx'=4,'dz'=16,'dc'=2,'bin'=4] {'dz'}, dimensions={0} | all-to-all | bytes 262144 | tf_op jit(solution)/shard_map/all_to_all | solution.py:165
  377.2 0.6 broadcast_multiply_fusion
  (40 shorter events, 0.9 us)
Async XLA Ops:
  7.2 1.2 copy-start
  8.7 32.8 %copy-start.2 = (bf16[128,2,2048]{2,1,0:T(2,128)(2,1)S(1)}, bf16[128,2,2048]{2,1,0:T(2,128)(2,1)}, u32[]{:S(2)}) copy-start(bf16[128,2,2048]{2,1,0:T(2,128)(2,1)} %param.5) | copy-start | bytes 3145732
  39.4 3.3 copy-start.10
  39.4 3.5 copy-start.9
  39.4 6.3 %collective-permute-start = (bf16[4,256,1024]{2,1,0:T(8,128)(2,1)S(1)}, bf16[4,256,1024]{2,1,0:T(8,128)(2,1)}, u32[]{:S(2)}, u32[]{:S(2)}) collective-permute-start(bf16[4,256,1024]{2,1,0:T(8,128)(2,1)S(1)} %all_to_all.30), channel_id=1, source_target_pairs={{0,4},{4,0},{1,5},{5,1},{2,6},{6,2},{3,7},{7,3},{8,12},{12,8},{9,1... | collective-permute-start | bytes 6291464 | tf_op jit(solution)/shard_map/ppermute | solution.py:82
  47.6 1.2 copy-start.5
  50.2 2.2 copy-start.4
  52.4 22.6 %copy-start.11 = (s32[192]{0:T(256)S(1)}, s32[192]{0:T(256)}, u32[]{:S(2)}) copy-start(s32[192]{0:T(256)} %param.9) | copy-start | bytes 2308
  52.4 117.6 %all-to-all-start.1 = ((bf16[128,8,1024]{2,1,0:T(8,128)(2,1)}), bf16[128,8,1024]{2,1,0:T(8,128)(2,1)S(1)}, u32[]{:S(2)}, u32[]{:S(2)}) async-start(bf16[128,8,1024]{2,1,0:T(8,128)(2,1)} %fusion.5), calls=%async_computation.1 | async-start | bytes 4194304 | tf_op jit(solution)/shard_map/all_to_all | solution.py:116
  179.0 1.7 copy-start.8
  180.7 1.2 copy-start.6
  185.4 107.8 %all-to-all-start.2 = ((bf16[128,8,1024]{2,1,0:T(8,128)(2,1)}), bf16[128,8,1024]{2,1,0:T(8,128)(2,1)S(1)}, u32[]{:S(2)}, u32[]{:S(2)}) async-start(bf16[128,8,1024]{2,1,0:T(8,128)(2,1)} %copy.117), calls=%async_computation.2 | async-start | bytes 4194304 | tf_op jit(solution)/shard_map/all_to_all | solution.py:127
  195.7 106.2 %all-gather.2.cloned.1.call-start = ((), (), s32[]{:S(2)}) async-start(), calls=%async_computation.6 | async-start | bytes 5242880 | tf_op jit(solution)/shard_map/all_gather | solution.py:140
  295.9 2.4 copy-start.3
  298.3 30.2 %all-to-all-start.3 = ((bf16[4,128,2,1024]{3,2,1,0:T(2,128)(2,1)}), bf16[4,128,2,1024]{3,2,1,0:T(2,128)(2,1)S(1)}, u32[]{:S(2)}, u32[]{:S(2)}) async-start(bf16[4,128,2,1024]{3,2,1,0:T(2,128)(2,1)} %broadcast_in_dim.41), calls=%async_computation.3 | async-start | bytes 4194304 | tf_op jit(solution)/shard_map/all_to_all | solution.py:141
  307.8 22.9 %copy-start.7 = (bf16[4,16,2,4,1024]{4,3,2,1,0:T(4,128)(2,1)S(1)}, bf16[4,16,2,4,1024]{4,3,2,1,0:T(4,128)(2,1)}, u32[]{:S(2)}) copy-start(bf16[4,16,2,4,1024]{4,3,2,1,0:T(4,128)(2,1)} %dot_general.35) | copy-start | bytes 3145732
  333.9 4.6 %collective-permute-start.1 = (f32[4,16,4,1024]{3,1,2,0:T(8,128)S(1)}, f32[4,16,4,1024]{3,1,2,0:T(8,128)S(1)}, u32[]{:S(2)}, u32[]{:S(2)}) collective-permute-start(f32[4,16,4,1024]{3,1,2,0:T(8,128)S(1)} %dynamic-slice_bitcast_fusion), channel_id=1, source_target_pairs={{0,4},{4,0},{1,5},{5,1},{2,6},{6,2},{3,7},{7,3},{8,12},{12,8},{9,1... | collective-permute-start | bytes 3145736 | tf_op jit(solution)/shard_map/ppermute | solution.py:161
  339.3 38.5 %copy-start.1 = (bf16[512,1024]{1,0:T(8,128)(2,1)S(1)}, bf16[512,1024]{1,0:T(8,128)(2,1)}, u32[]{:S(2)}) copy-start(bf16[512,1024]{1,0:T(8,128)(2,1)} %param.6) | copy-start | bytes 3145732
Sparse Core Ops, SparseCore 0:
  198.7 54.6 all-gather.1

commit v10 on v9

--- a/solution.py
+++ b/solution.py
@@ -159,9 +159,10 @@
     kept = lax.dynamic_index_in_dim(local_grad, core, 0, keepdims=False)
     given = lax.dynamic_index_in_dim(local_grad, 1 - core, 0, keepdims=False)
     local_grad = kept + lax.ppermute(given, "dc", perm=[(0, 1), (1, 0)])
-    planes = local_grad.reshape(sizes[0], sizes[1] * per_dev, emb_dim)
+    planes = local_grad.reshape(sizes[0], sizes[1] * per_dev, emb_dim).astype(jnp.bfloat16)
     planes = lax.all_to_all(planes, "dx", split_axis=0, concat_axis=0, tiled=True)
-    planes = jnp.sum(planes, axis=0).reshape(sizes[1], per_dev, emb_dim).astype(jnp.bfloat16)
+    planes = jnp.sum(planes.astype(jnp.float32), axis=0)
+    planes = planes.reshape(sizes[1], per_dev, emb_dim).astype(jnp.bfloat16)
     planes = lax.all_to_all(planes, "dz", split_axis=0, concat_axis=0, tiled=True)
     local_grad = jnp.sum(planes.astype(jnp.float32), axis=0)
     grad_weight = local_grad / rows_dev

time: 386 us -> 380 us (0.984)
  blocking collectives: 67.8 us -> 62.2 us
    all_to_all x1, blocking collectives: 19.3 us -> 13.6 us  [local(): lax.all_to_all(planes, 'dx', split_axis=0, concat_axis=0, tiled=True)]
where the time goes in v10:
time: 380 us; the launch traced here: 378 us
  waiting for transfers between devices  215 us (57%)
  blocking collectives  62.2 us (16%)
  starting transfers between devices  38.2 us (10%)
  local copies, waits for them, and re-layouts  27.3 us (7%)
  between operations  16.4 us (4%)
  matrix products  13.5 us (4%)
  other arithmetic  6.24 us (2%)
    all_to_all x1, waiting for transfers between devices, local(): lax.all_to_all(back.reshape(sources, block, emb_dim), DP, split_axis=0, c...  94.7 us
    all_to_all x1, waiting for transfers between devices, local(): lax.all_to_all(outbox.reshape(sources, block, emb_dim), DP, split_axis=0,...  94.3 us
    all_to_all x1, blocking collectives, local(): lax.all_to_all(copies, 'bin', split_axis=0, concat_axis=0, tiled=True)  30.7 us
    all_to_all x1, waiting for transfers between devices, local(): lax.all_to_all(jnp.broadcast_to(grad_rows[None], (bins_n, *grad_rows.shap...  20.7 us
    all_to_all x1, starting transfers between devices, local(): lax.all_to_all(outbox.reshape(sources, block, emb_dim), DP, split_axis=0,...  20 us
    all_to_all x1, blocking collectives, local(): lax.all_to_all(planes, 'dz', split_axis=0, concat_axis=0, tiled=True)  17.9 us
    all_to_all x1, blocking collectives, local(): lax.all_to_all(planes, 'dx', split_axis=0, concat_axis=0, tiled=True)  13.6 us
    all_to_all x1, starting transfers between devices, local(): lax.all_to_all(back.reshape(sources, block, emb_dim), DP, split_axis=0, c...  10.3 us
  transfers between devices with their start and end apart: 6, of which 5 were waited for; matrix products, arithmetic and copies ran while one was open for 4% of the time, Pallas kernels for 0%

profile of v10, /device:TPU:6, one launch (start us, length us, event | category | flops | bytes accessed | tf_op | source)
XLA Modules:
  0.0 378.4 jit_solution(1891222680179501184)
XLA Ops:
  7.2 1.2 copy-done
  8.4 0.3 broadcast_in_dim.35
  8.7 30.7 %all_to_all.30 = bf16[4,256,1024]{2,1,0:T(8,128)(2,1)S(1)} all-to-all(bf16[4,256,1024]{2,1,0:T(8,128)(2,1)S(1)} %broadcast_in_dim.35), channel_id=1, replica_groups=mesh['dx'=4,'dz'=16,'dc'=2,'bin'=4] {'bin'}, dimensions={0} | all-to-all | bytes 4194304 | tf_op jit(solution)/shard_map/all_to_all | solution.py:81
  39.4 2.0 collective-permute-start
  41.5 1.2 reshape.230
  42.8 0.2 convert_reduce_fusion.3
  42.9 0.2 convert_reduce_fusion.2
  43.1 0.1 select_reduce_fusion.1
  43.5 0.1 add.161
  43.6 0.2 convert_reduce_fusion
  43.9 1.9 collective-permute-done
  45.7 1.9 select_bitcast_fusion.1
  47.6 0.4 pad_maximum_fusion
  48.0 0.8 copy-done.5
  48.8 1.3 multiply_reduce_fusion
  50.2 2.2 fusion.5
  52.4 20.0 %all-to-all-start.1 = ((bf16[128,8,1024]{2,1,0:T(8,128)(2,1)}), bf16[128,8,1024]{2,1,0:T(8,128)(2,1)S(1)}, u32[]{:S(2)}, u32[]{:S(2)}) async-start(bf16[128,8,1024]{2,1,0:T(8,128)(2,1)} %fusion.5), calls=%async_computation.1 | async-start | bytes 4194304 | tf_op jit(solution)/shard_map/all_to_all | solution.py:116
  72.4 0.6 fusion.43
  75.1 0.6 fusion.48
  75.7 94.3 %all-to-all-done.1 = bf16[128,8,1024]{2,1,0:T(8,128)(2,1)S(1)} async-done(((bf16[128,8,1024]{2,1,0:T(8,128)(2,1)}), bf16[128,8,1024]{2,1,0:T(8,128)(2,1)S(1)}, u32[]{:S(2)}, u32[]{:S(2)}) %all-to-all-start.1) | async-done | bytes 2097184 | tf_op jit(solution)/shard_map/all_to_all | solution.py:116
  170.0 1.2 copy.110
  171.1 0.2 fusion.47
  171.3 0.8 copy.113
  172.2 0.3 reshape_squeeze.6
  172.5 0.8 copy.114
  173.3 0.3 reshape_squeeze.7
  173.6 0.9 copy.112
  174.4 0.1 lt.103
  174.6 2.7 fusion.49
  177.2 1.8 multiply_convert_fusion.1
  179.0 1.7 multiply_convert_fusion
  180.7 0.4 stack_reshape.6
  181.2 0.3 copy.115
  181.5 0.5 copy-done.6
  182.0 0.4 stack_reshape.7
  182.4 0.3 copy.116
  182.7 0.2 pad_maximum_fusion.1
  182.9 2.5 copy.117
  185.4 10.3 %all-to-all-start.2 = ((bf16[128,8,1024]{2,1,0:T(8,128)(2,1)}), bf16[128,8,1024]{2,1,0:T(8,128)(2,1)S(1)}, u32[]{:S(2)}, u32[]{:S(2)}) async-start(bf16[128,8,1024]{2,1,0:T(8,128)(2,1)} %copy.117), calls=%async_computation.2 | async-start | bytes 4194304 | tf_op jit(solution)/shard_map/all_to_all | solution.py:127
  195.7 0.3 all-gather.2.cloned.1.call-start
  196.0 0.5 all-gather.2.cloned.1.call-update
  196.5 1.8 reshape.235
  198.3 0.1 rsqrt.13
  198.5 94.7 %all-to-all-done.2 = bf16[128,8,1024]{2,1,0:T(8,128)(2,1)S(1)} async-done(((bf16[128,8,1024]{2,1,0:T(8,128)(2,1)}), bf16[128,8,1024]{2,1,0:T(8,128)(2,1)S(1)}, u32[]{:S(2)}, u32[]{:S(2)}) %all-to-all-start.2) | async-done | bytes 2097184 | tf_op jit(solution)/shard_map/all_to_all | solution.py:127
  293.2 0.8 fusion.1
  294.0 1.3 fusion.11
  295.3 0.5 copy.125
  295.9 2.4 broadcast_in_dim.41
  298.3 3.6 all-to-all-start.3
  301.9 1.9 constant_dynamic-slice_fusion
  303.9 1.2 reshape.236
  305.1 1.5 copy.119
  306.6 1.2 dot_general.35
  307.8 20.7 %all-to-all-done.3 = bf16[4,128,2,1024]{3,2,1,0:T(2,128)(2,1)S(1)} async-done(((bf16[4,128,2,1024]{3,2,1,0:T(2,128)(2,1)}), bf16[4,128,2,1024]{3,2,1,0:T(2,128)(2,1)S(1)}, u32[]{:S(2)}, u32[]{:S(2)}) %all-to-all-start.3) | async-done | bytes 2097184 | tf_op jit(solution)/shard_map/all_to_all | solution.py:141
  328.5 2.2 reshape.239
  330.7 3.1 fusion.3
  333.9 1.9 collective-permute-start.1
  335.8 2.6 collective-permute-done.1
  338.5 0.2 fusion.12
  338.6 0.4 copy.122
  339.0 0.2 copy.123
  339.2 13.6 %all_to_all.31 = bf16[4,64,1024]{2,1,0:T(8,128)(2,1)S(1)} all-to-all(bf16[4,64,1024]{2,1,0:T(8,128)(2,1)S(1)} %copy.123), channel_id=1, replica_groups=mesh['dx'=4,'dz'=16,'dc'=2,'bin'=4] {'dx'}, dimensions={0} | all-to-all | bytes 1048576 | tf_op jit(solution)/shard_map/all_to_all | solution.py:163
  353.0 17.9 %all_to_all.32 = bf16[16,4,1024]{2,1,0:T(4,128)(2,1)S(1)} all-to-all(bf16[16,4,1024]{2,1,0:T(4,128)(2,1)S(1)} %convert_element_type.83), channel_id=1, replica_groups=mesh['dx'=4,'dz'=16,'dc'=2,'bin'=4] {'dz'}, dimensions={0} | all-to-all | bytes 262144 | tf_op jit(solution)/shard_map/all_to_all | solution.py:166
  370.9 0.6 broadcast_multiply_fusion
  (40 shorter events, 0.9 us)
Async XLA Ops:
  7.2 1.2 copy-start
  8.7 32.8 %copy-start.2 = (bf16[128,2,2048]{2,1,0:T(2,128)(2,1)S(1)}, bf16[128,2,2048]{2,1,0:T(2,128)(2,1)}, u32[]{:S(2)}) copy-start(bf16[128,2,2048]{2,1,0:T(2,128)(2,1)} %param.5) | copy-start | bytes 3145732
  39.4 3.3 copy-start.10
  39.4 3.5 copy-start.9
  39.4 6.3 %collective-permute-start = (bf16[4,256,1024]{2,1,0:T(8,128)(2,1)S(1)}, bf16[4,256,1024]{2,1,0:T(8,128)(2,1)}, u32[]{:S(2)}, u32[]{:S(2)}) collective-permute-start(bf16[4,256,1024]{2,1,0:T(8,128)(2,1)S(1)} %all_to_all.30), channel_id=1, source_target_pairs={{0,4},{4,0},{1,5},{5,1},{2,6},{6,2},{3,7},{7,3},{8,12},{12,8},{9,1... | collective-permute-start | bytes 6291464 | tf_op jit(solution)/shard_map/ppermute | solution.py:82
  47.6 1.2 copy-start.5
  50.2 2.2 copy-start.4
  52.4 22.6 %copy-start.11 = (s32[192]{0:T(256)S(1)}, s32[192]{0:T(256)}, u32[]{:S(2)}) copy-start(s32[192]{0:T(256)} %param.9) | copy-start | bytes 2308
  52.4 117.6 %all-to-all-start.1 = ((bf16[128,8,1024]{2,1,0:T(8,128)(2,1)}), bf16[128,8,1024]{2,1,0:T(8,128)(2,1)S(1)}, u32[]{:S(2)}, u32[]{:S(2)}) async-start(bf16[128,8,1024]{2,1,0:T(8,128)(2,1)} %fusion.5), calls=%async_computation.1 | async-start | bytes 4194304 | tf_op jit(solution)/shard_map/all_to_all | solution.py:116
  179.0 1.7 copy-start.8
  180.7 1.2 copy-start.6
  185.4 107.8 %all-to-all-start.2 = ((bf16[128,8,1024]{2,1,0:T(8,128)(2,1)}), bf16[128,8,1024]{2,1,0:T(8,128)(2,1)S(1)}, u32[]{:S(2)}, u32[]{:S(2)}) async-start(bf16[128,8,1024]{2,1,0:T(8,128)(2,1)} %copy.117), calls=%async_computation.2 | async-start | bytes 4194304 | tf_op jit(solution)/shard_map/all_to_all | solution.py:127
  195.7 106.2 %all-gather.2.cloned.1.call-start = ((), (), s32[]{:S(2)}) async-start(), calls=%async_computation.6 | async-start | bytes 5242880 | tf_op jit(solution)/shard_map/all_gather | solution.py:140
  295.9 2.4 copy-start.3
  298.3 30.2 %all-to-all-start.3 = ((bf16[4,128,2,1024]{3,2,1,0:T(2,128)(2,1)}), bf16[4,128,2,1024]{3,2,1,0:T(2,128)(2,1)S(1)}, u32[]{:S(2)}, u32[]{:S(2)}) async-start(bf16[4,128,2,1024]{3,2,1,0:T(2,128)(2,1)} %broadcast_in_dim.41), calls=%async_computation.3 | async-start | bytes 4194304 | tf_op jit(solution)/shard_map/all_to_all | solution.py:141
  307.8 22.9 %copy-start.7 = (bf16[4,16,2,4,1024]{4,3,2,1,0:T(4,128)(2,1)S(1)}, bf16[4,16,2,4,1024]{4,3,2,1,0:T(4,128)(2,1)}, u32[]{:S(2)}) copy-start(bf16[4,16,2,4,1024]{4,3,2,1,0:T(4,128)(2,1)} %dot_general.35) | copy-start | bytes 3145732
  333.9 4.6 %collective-permute-start.1 = (f32[4,16,4,1024]{3,1,2,0:T(8,128)S(1)}, f32[4,16,4,1024]{3,1,2,0:T(8,128)S(1)}, u32[]{:S(2)}, u32[]{:S(2)}) collective-permute-start(f32[4,16,4,1024]{3,1,2,0:T(8,128)S(1)} %dynamic-slice_bitcast_fusion), channel_id=1, source_target_pairs={{0,4},{4,0},{1,5},{5,1},{2,6},{6,2},{3,7},{7,3},{8,12},{12,8},{9,1... | collective-permute-start | bytes 3145736 | tf_op jit(solution)/shard_map/ppermute | solution.py:161
  338.5 33.1 %copy-start.1 = (bf16[512,1024]{1,0:T(8,128)(2,1)S(1)}, bf16[512,1024]{1,0:T(8,128)(2,1)}, u32[]{:S(2)}) copy-start(bf16[512,1024]{1,0:T(8,128)(2,1)} %param.6) | copy-start | bytes 3145732
Sparse Core Ops, SparseCore 0:
  198.7 54.6 all-gather.1

commit v11 on v9

--- a/solution.py
+++ b/solution.py
@@ -9,7 +9,7 @@
 
 SOFTMAX_TEMP_SCALE = 0.1
 
-DP_PARTS = (("dx", 4), ("dz", 16), ("dc", 2))
+DP_PARTS = (("dx", 4), ("dzh", 4), ("dzl", 4), ("dc", 2))
 DP = tuple(name for name, _ in DP_PARTS)
 EMPTY_MARK = 4.0
 
@@ -155,15 +155,18 @@
     )
     sizes = [size for _, size in DP_PARTS]
     per_dev = part_rows // sources
-    local_grad = jnp.transpose(local_grad.reshape(*sizes, per_dev, emb_dim), (2, 0, 1, 3, 4))
+    local_grad = jnp.transpose(local_grad.reshape(*sizes, per_dev, emb_dim), (3, 0, 1, 2, 4, 5))
     kept = lax.dynamic_index_in_dim(local_grad, core, 0, keepdims=False)
     given = lax.dynamic_index_in_dim(local_grad, 1 - core, 0, keepdims=False)
     local_grad = kept + lax.ppermute(given, "dc", perm=[(0, 1), (1, 0)])
-    planes = local_grad.reshape(sizes[0], sizes[1] * per_dev, emb_dim)
+    planes = local_grad.reshape(sizes[0], -1, emb_dim).astype(jnp.bfloat16)
     planes = lax.all_to_all(planes, "dx", split_axis=0, concat_axis=0, tiled=True)
-    planes = jnp.sum(planes, axis=0).reshape(sizes[1], per_dev, emb_dim).astype(jnp.bfloat16)
-    planes = lax.all_to_all(planes, "dz", split_axis=0, concat_axis=0, tiled=True)
-    local_grad = jnp.sum(planes.astype(jnp.float32), axis=0)
+    planes = jnp.sum(planes.astype(jnp.float32), axis=0).reshape(sizes[1], sizes[2], per_dev, emb_dim)
+    planes = jnp.transpose(planes, (1, 0, 2, 3)).reshape(sizes[2], -1, emb_dim).astype(jnp.bfloat16)
+    planes = lax.all_to_all(planes, "dzl", split_axis=0, concat_axis=0, tiled=True)
+    planes = jnp.sum(planes.astype(jnp.float32), axis=0).reshape(sizes[1], per_dev, emb_dim)
+    planes = lax.all_to_all(planes, "dzh", split_axis=0, concat_axis=0, tiled=True)
+    local_grad = jnp.sum(planes, axis=0)
     grad_weight = local_grad / rows_dev
     return (grad_rows, grad_weight)
 

time: 386 us -> 390 us (1.010)
    all_to_all x1 -> x2, blocking collectives: 17.8 us -> 26.6 us  [the longest x1 18.3 us: local(): lax.all_to_all(planes, 'dzh', split_axis=0, concat_axis=0, tiled=True)]
    all_to_all x1, blocking collectives: 19.3 us -> 13.6 us  [local(): lax.all_to_all(planes, 'dx', split_axis=0, concat_axis=0, tiled=True)]
where the time goes in v11:
time: 390 us; the launch traced here: 388 us
  waiting for transfers between devices  215 us (55%)
  blocking collectives  71 us (18%)
  starting transfers between devices  38.2 us (10%)
  local copies, waits for them, and re-layouts  27 us (7%)
  between operations  16.4 us (4%)
  matrix products  14 us (4%)
  other arithmetic  6.47 us (2%)
    all_to_all x1, waiting for transfers between devices, local(): lax.all_to_all(back.reshape(sources, block, emb_dim), DP, split_axis=0, c...  94.7 us
    all_to_all x1, waiting for transfers between devices, local(): lax.all_to_all(outbox.reshape(sources, block, emb_dim), DP, split_axis=0,...  94.3 us
    all_to_all x1, blocking collectives, local(): lax.all_to_all(copies, 'bin', split_axis=0, concat_axis=0, tiled=True)  30.7 us
    all_to_all x1, waiting for transfers between devices, local(): lax.all_to_all(jnp.broadcast_to(grad_rows[None], (bins_n, *grad_rows.shap...  20.7 us
    all_to_all x1, starting transfers between devices, local(): lax.all_to_all(outbox.reshape(sources, block, emb_dim), DP, split_axis=0,...  20 us
    all_to_all x1, blocking collectives, local(): lax.all_to_all(planes, 'dzh', split_axis=0, concat_axis=0, tiled=True)  18.3 us
    all_to_all x1, blocking collectives, local(): lax.all_to_all(planes, 'dx', split_axis=0, concat_axis=0, tiled=True)  13.6 us
    all_to_all x1, starting transfers between devices, local(): lax.all_to_all(back.reshape(sources, block, emb_dim), DP, split_axis=0, c...  10.3 us
  transfers between devices with their start and end apart: 6, of which 5 were waited for; matrix products, arithmetic and copies ran while one was open for 4% of the time, Pallas kernels for 0%

profile of v11, /device:TPU:6, one launch (start us, length us, event | category | flops | bytes accessed | tf_op | source)
XLA Modules:
  0.0 387.6 jit_solution(9350709778994012816)
XLA Ops:
  7.2 1.2 copy-done
  8.4 0.3 broadcast_in_dim.35
  8.7 30.7 %all_to_all.35 = bf16[4,256,1024]{2,1,0:T(8,128)(2,1)S(1)} all-to-all(bf16[4,256,1024]{2,1,0:T(8,128)(2,1)S(1)} %broadcast_in_dim.35), channel_id=1, replica_groups=mesh['dx'=4,'dzh'=4,'dzl'=4,'dc'=2,'bin'=4] {'bin'}, dimensions={0} | all-to-all | bytes 4194304 | tf_op jit(solution)/shard_map/all_to_all | solution.py:81
  39.4 2.0 collective-permute-start
  41.5 1.2 reshape.235
  42.8 0.2 convert_reduce_fusion.3
  42.9 0.2 convert_reduce_fusion.2
  43.1 0.1 select_reduce_fusion.1
  43.5 0.1 add.164
  43.6 0.2 convert_reduce_fusion
  43.9 1.9 collective-permute-done
  45.7 1.9 select_bitcast_fusion.1
  47.6 0.4 pad_maximum_fusion
  48.0 0.8 copy-done.5
  48.8 1.3 multiply_reduce_fusion
  50.2 2.2 fusion.5
  52.4 20.0 %all-to-all-start.1 = ((bf16[128,8,1024]{2,1,0:T(8,128)(2,1)}), bf16[128,8,1024]{2,1,0:T(8,128)(2,1)S(1)}, u32[]{:S(2)}, u32[]{:S(2)}) async-start(bf16[128,8,1024]{2,1,0:T(8,128)(2,1)} %fusion.5), calls=%async_computation.1 | async-start | bytes 4194304 | tf_op jit(solution)/shard_map/all_to_all | solution.py:116
  72.4 0.6 fusion.42
  75.1 0.6 fusion.47
  75.7 94.3 %all-to-all-done.1 = bf16[128,8,1024]{2,1,0:T(8,128)(2,1)S(1)} async-done(((bf16[128,8,1024]{2,1,0:T(8,128)(2,1)}), bf16[128,8,1024]{2,1,0:T(8,128)(2,1)S(1)}, u32[]{:S(2)}, u32[]{:S(2)}) %all-to-all-start.1) | async-done | bytes 2097184 | tf_op jit(solution)/shard_map/all_to_all | solution.py:116
  170.0 1.2 copy.70
  171.1 0.2 fusion.46
  171.3 0.8 copy.73
  172.2 0.3 reshape_squeeze.6
  172.5 0.8 copy.74
  173.3 0.3 reshape_squeeze.7
  173.6 0.9 copy.72
  174.4 0.1 lt.103
  174.6 2.7 fusion.48
  177.2 1.8 multiply_convert_fusion.1
  179.0 1.7 multiply_convert_fusion
  180.7 0.4 stack_reshape.6
  181.2 0.3 copy.75
  181.5 0.5 copy-done.6
  182.0 0.4 stack_reshape.7
  182.4 0.3 copy.76
  182.7 0.2 pad_maximum_fusion.1
  182.9 2.5 copy.77
  185.4 10.3 %all-to-all-start.2 = ((bf16[128,8,1024]{2,1,0:T(8,128)(2,1)}), bf16[128,8,1024]{2,1,0:T(8,128)(2,1)S(1)}, u32[]{:S(2)}, u32[]{:S(2)}) async-start(bf16[128,8,1024]{2,1,0:T(8,128)(2,1)} %copy.77), calls=%async_computation.2 | async-start | bytes 4194304 | tf_op jit(solution)/shard_map/all_to_all | solution.py:127
  195.7 0.3 all-gather.2.cloned.1.call-start
  196.0 0.5 all-gather.2.cloned.1.call-update
  196.5 1.8 reshape.240
  198.3 0.1 rsqrt.13
  198.5 94.7 %all-to-all-done.2 = bf16[128,8,1024]{2,1,0:T(8,128)(2,1)S(1)} async-done(((bf16[128,8,1024]{2,1,0:T(8,128)(2,1)}), bf16[128,8,1024]{2,1,0:T(8,128)(2,1)S(1)}, u32[]{:S(2)}, u32[]{:S(2)}) %all-to-all-start.2) | async-done | bytes 2097184 | tf_op jit(solution)/shard_map/all_to_all | solution.py:127
  293.2 0.8 fusion.1
  294.0 1.3 fusion.11
  295.3 0.5 copy.83
  295.9 2.4 broadcast_in_dim.41
  298.3 3.6 all-to-all-start.3
  301.9 1.9 constant_dynamic-slice_fusion
  303.9 1.2 reshape.241
  305.1 1.5 copy.79
  306.6 1.2 dot_general.35
  307.8 20.7 %all-to-all-done.3 = bf16[4,128,2,1024]{3,2,1,0:T(2,128)(2,1)S(1)} async-done(((bf16[4,128,2,1024]{3,2,1,0:T(2,128)(2,1)}), bf16[4,128,2,1024]{3,2,1,0:T(2,128)(2,1)S(1)}, u32[]{:S(2)}, u32[]{:S(2)}) %all-to-all-start.3) | async-done | bytes 2097184 | tf_op jit(solution)/shard_map/all_to_all | solution.py:141
  328.5 2.2 reshape.245
  330.7 3.6 fusion.3
  334.4 1.9 collective-permute-start.1
  336.3 2.6 collective-permute-done.1
  339.0 0.4 fusion.12
  339.4 0.1 convert_element_type.88
  339.5 13.6 %all_to_all.36 = bf16[4,64,1024]{2,1,0:T(8,128)(2,1)S(1)} all-to-all(bf16[4,64,1024]{2,1,0:T(8,128)(2,1)S(1)} %convert_element_type.88), channel_id=1, replica_groups=mesh['dx'=4,'dzh'=4,'dzl'=4,'dc'=2,'bin'=4] {'dx'}, dimensions={0} | all-to-all | bytes 1048576 | tf_op jit(solution)/shard_map/all_to_all | solution.py:163
  353.5 8.3 %all_to_all.37 = bf16[4,16,1024]{2,1,0:T(8,128)(2,1)S(1)} all-to-all(bf16[4,16,1024]{2,1,0:T(8,128)(2,1)S(1)} %copy.82), channel_id=1, replica_groups=mesh['dx'=4,'dzh'=4,'dzl'=4,'dc'=2,'bin'=4] {'dzl'}, dimensions={0} | all-to-all | bytes 262144 | tf_op jit(solution)/shard_map/all_to_all | solution.py:166
  361.8 18.3 %all_to_all.38 = f32[4,4,1024]{2,1,0:T(4,128)S(1)} all-to-all(f32[4,4,1024]{2,1,0:T(4,128)S(1)} %reshape.243), channel_id=1, replica_groups=mesh['dx'=4,'dzh'=4,'dzl'=4,'dc'=2,'bin'=4] {'dzh'}, dimensions={0} | all-to-all | bytes 131072 | tf_op jit(solution)/shard_map/all_to_all | solution.py:168
  380.2 0.6 broadcast_multiply_fusion
  (44 shorter events, 0.9 us)
Async XLA Ops:
  7.2 1.2 copy-start
  8.7 32.8 %copy-start.2 = (bf16[128,2,2048]{2,1,0:T(2,128)(2,1)S(1)}, bf16[128,2,2048]{2,1,0:T(2,128)(2,1)}, u32[]{:S(2)}) copy-start(bf16[128,2,2048]{2,1,0:T(2,128)(2,1)} %param.5) | copy-start | bytes 3145732
  39.4 3.3 copy-start.10
  39.4 3.5 copy-start.9
  39.4 6.3 %collective-permute-start = (bf16[4,256,1024]{2,1,0:T(8,128)(2,1)S(1)}, bf16[4,256,1024]{2,1,0:T(8,128)(2,1)}, u32[]{:S(2)}, u32[]{:S(2)}) collective-permute-start(bf16[4,256,1024]{2,1,0:T(8,128)(2,1)S(1)} %all_to_all.35), channel_id=1, source_target_pairs={{0,4},{4,0},{1,5},{5,1},{2,6},{6,2},{3,7},{7,3},{8,12},{12,8},{9,1... | collective-permute-start | bytes 6291464 | tf_op jit(solution)/shard_map/ppermute | solution.py:82
  47.6 1.2 copy-start.5
  50.2 2.2 copy-start.4
  52.4 22.6 %copy-start.11 = (s32[192]{0:T(256)S(1)}, s32[192]{0:T(256)}, u32[]{:S(2)}) copy-start(s32[192]{0:T(256)} %param.9) | copy-start | bytes 2308
  52.4 117.6 %all-to-all-start.1 = ((bf16[128,8,1024]{2,1,0:T(8,128)(2,1)}), bf16[128,8,1024]{2,1,0:T(8,128)(2,1)S(1)}, u32[]{:S(2)}, u32[]{:S(2)}) async-start(bf16[128,8,1024]{2,1,0:T(8,128)(2,1)} %fusion.5), calls=%async_computation.1 | async-start | bytes 4194304 | tf_op jit(solution)/shard_map/all_to_all | solution.py:116
  179.0 1.7 copy-start.8
  180.7 1.2 copy-start.6
  185.4 107.8 %all-to-all-start.2 = ((bf16[128,8,1024]{2,1,0:T(8,128)(2,1)}), bf16[128,8,1024]{2,1,0:T(8,128)(2,1)S(1)}, u32[]{:S(2)}, u32[]{:S(2)}) async-start(bf16[128,8,1024]{2,1,0:T(8,128)(2,1)} %copy.77), calls=%async_computation.2 | async-start | bytes 4194304 | tf_op jit(solution)/shard_map/all_to_all | solution.py:127
  195.7 106.2 %all-gather.2.cloned.1.call-start = ((), (), s32[]{:S(2)}) async-start(), calls=%async_computation.7 | async-start | bytes 5242880 | tf_op jit(solution)/shard_map/all_gather | solution.py:140
  295.9 2.4 copy-start.3
  298.3 30.2 %all-to-all-start.3 = ((bf16[4,128,2,1024]{3,2,1,0:T(2,128)(2,1)}), bf16[4,128,2,1024]{3,2,1,0:T(2,128)(2,1)S(1)}, u32[]{:S(2)}, u32[]{:S(2)}) async-start(bf16[4,128,2,1024]{3,2,1,0:T(2,128)(2,1)} %broadcast_in_dim.41), calls=%async_computation.3 | async-start | bytes 4194304 | tf_op jit(solution)/shard_map/all_to_all | solution.py:141
  307.8 22.9 %copy-start.7 = (bf16[4,4,4,2,4,1024]{5,4,3,2,1,0:T(4,128)(2,1)S(1)}, bf16[4,4,4,2,4,1024]{5,4,3,2,1,0:T(4,128)(2,1)}, u32[]{:S(2)}) copy-start(bf16[4,4,4,2,4,1024]{5,4,3,2,1,0:T(4,128)(2,1)} %dot_general.35) | copy-start | bytes 3145732
  334.4 4.6 %collective-permute-start.1 = (f32[4,4,4,4,1024]{4,3,2,1,0:T(4,128)S(1)}, f32[4,4,4,4,1024]{4,3,2,1,0:T(4,128)S(1)}, u32[]{:S(2)}, u32[]{:S(2)}) collective-permute-start(f32[4,4,4,4,1024]{4,3,2,1,0:T(4,128)S(1)} %dynamic-slice_bitcast_fusion), channel_id=1, source_target_pairs={{0,4},{4,0},{1,5},{5,1},{2,6},{6,2},{3,7},{7,3},{8,12},{12,8},{9,1... | collective-permute-start | bytes 3145736 | tf_op jit(solution)/shard_map/ppermute | solution.py:161
  339.0 41.8 %copy-start.1 = (bf16[512,1024]{1,0:T(8,128)(2,1)S(1)}, bf16[512,1024]{1,0:T(8,128)(2,1)}, u32[]{:S(2)}) copy-start(bf16[512,1024]{1,0:T(8,128)(2,1)} %param.6) | copy-start | bytes 3145732
Sparse Core Ops, SparseCore 0:
  198.7 54.6 all-gather.1

commit v12 on v10

--- a/solution.py
+++ b/solution.py
@@ -84,9 +84,8 @@
     high = jnp.where(core == 0, theirs, mine)
     weight = jnp.stack([low, high], axis=1).reshape(feat_dim, emb_dim)
     folded = jnp.dot(flat, weight, preferred_element_type=jnp.float32)
-    embedded = folded.reshape(rows_dev, views, emb_dim)
-    scale = lax.rsqrt(jnp.sum(embedded * embedded, axis=2, keepdims=True) + 1e-06)
-    unit = embedded * scale
+    scale = lax.rsqrt(jnp.sum(folded * folded, axis=1, keepdims=True) + 1e-06)
+    unit = folded * scale
     sent = unit.astype(jnp.bfloat16)
     row_bins = bin_of_row[:, 0]
     lookup = row_bins[:, None] == jnp.arange(bin_count, dtype=jnp.int32)[None, :]
@@ -106,7 +105,7 @@
     lanes = sources * block
     picks = (dest.reshape(-1)[None, :] == jnp.arange(lanes, dtype=jnp.int32)[:, None]).astype(jnp.bfloat16)
     picked = jnp.dot(
-        picks, sent.reshape(rows_dev * views, emb_dim), preferred_element_type=jnp.float32
+        picks, sent, preferred_element_type=jnp.float32
     )
     unfilled = 1.0 - jnp.sum(picks.astype(jnp.float32), axis=1)
     lane_view = jnp.arange(lanes, dtype=jnp.int32) % block // per_owner
@@ -132,24 +131,24 @@
         returned.reshape(lanes, emb_dim),
         (((0,), (0,)), ((), ())),
         preferred_element_type=jnp.float32,
-    ).reshape(rows_dev, views, emb_dim)
-    grad_rows = (
-        scale * (row_grads - unit * jnp.sum(unit * row_grads, axis=2, keepdims=True))
+    )
+    flat_grads = (
+        scale * (row_grads - unit * jnp.sum(unit * row_grads, axis=1, keepdims=True))
     ).astype(jnp.bfloat16)
+    grad_rows = flat_grads.reshape(rows_dev, views, emb_dim)
     column_start = lax.axis_index("bin") * part_rows
-    trunk = lax.all_gather(features, "bin", axis=0, tiled=True)
+    trunk = lax.all_gather(flat, "bin", axis=0, tiled=True)
     outgrad = lax.all_to_all(
-        jnp.broadcast_to(grad_rows[None], (bins_n, *grad_rows.shape)),
+        jnp.broadcast_to(flat_grads[None], (bins_n, *flat_grads.shape)),
         "bin",
         split_axis=0,
         concat_axis=0,
         tiled=True,
     )
-    columns = lax.dynamic_slice_in_dim(trunk, column_start, part_rows, 2)
-    count = trunk.shape[0]
+    columns = lax.dynamic_slice_in_dim(trunk, column_start, part_rows, 1)
     local_grad = lax.dot_general(
-        columns.reshape(count * views, part_rows),
-        outgrad.reshape(count * views, emb_dim),
+        columns,
+        outgrad.reshape(-1, emb_dim),
         (((0,), (0,)), ((), ())),
         preferred_element_type=jnp.float32,
     )

time: 380 us -> 384 us (1.011)
  blocking collectives: 62.2 us -> 44.2 us
  waiting for transfers between devices: 215 us -> 230 us
  starting transfers between devices: 38.2 us -> 43.1 us
    all_to_all x1 -> x0, blocking collectives: 17.9 us -> none  [local(): lax.all_to_all(planes, 'dz', split_axis=0, concat_axis=0, tiled=True)]
    all_to_all x1 -> x2, waiting for transfers between devices: 20.7 us -> 37.1 us  [the longest x1 24.1 us: local(): lax.all_to_all(jnp.broadcast_to(flat_grads[None], (bins_n, *flat_grads.sh...]
    all_to_all x1 -> x2, starting transfers between devices: 3.61 us -> 8.52 us  [the longest x1 4.44 us: local(): lax.all_to_all(jnp.broadcast_to(flat_grads[None], (bins_n, *flat_grads.sh...]
    reshape x3 -> x1, local copies, waits for them, and re-layouts: 5.31 us -> 0.99 us  [local(): grad_rows = flat_grads.reshape(rows_dev, views, emb_dim)]
  transfers between devices with their start and end apart: 6 -> 7, of which waited for: 5 -> 6; matrix products, arithmetic and copies ran while one was open for 4% -> 4% of each run, Pallas kernels for 0% -> 0%
where the time goes in v12:
time: 384 us; the launch traced here: 383 us
  waiting for transfers between devices  230 us (60%)
  blocking collectives  44.2 us (12%)
  starting transfers between devices  43.1 us (11%)
  local copies, waits for them, and re-layouts  27.5 us (7%)
  matrix products  16.5 us (4%)
  between operations  16.3 us (4%)
  other arithmetic  5.18 us (1%)
    all_to_all x1, waiting for transfers between devices, local(): lax.all_to_all(back.reshape(sources, block, emb_dim), DP, split_axis=0, c...  94.9 us
    all_to_all x1, waiting for transfers between devices, local(): lax.all_to_all(outbox.reshape(sources, block, emb_dim), DP, split_axis=0,...  94.3 us
    all_to_all x1, blocking collectives, local(): lax.all_to_all(copies, 'bin', split_axis=0, concat_axis=0, tiled=True)  30.6 us
    all_to_all x1, waiting for transfers between devices, local(): lax.all_to_all(jnp.broadcast_to(flat_grads[None], (bins_n, *flat_grads.sh...  24.1 us
    all_to_all x1, starting transfers between devices, local(): lax.all_to_all(outbox.reshape(sources, block, emb_dim), DP, split_axis=0,...  20 us
    all_to_all x1, blocking collectives, local(): lax.all_to_all(planes, 'dx', split_axis=0, concat_axis=0, tiled=True)  13.6 us
    all_to_all x1, waiting for transfers between devices, local(): lax.all_to_all(planes, 'dz', split_axis=0, concat_axis=0, tiled=True)  13 us
    all_to_all x1, starting transfers between devices, local(): lax.all_to_all(back.reshape(sources, block, emb_dim), DP, split_axis=0, c...  10.3 us
  transfers between devices with their start and end apart: 7, of which 6 were waited for; matrix products, arithmetic and copies ran while one was open for 4% of the time, Pallas kernels for 0%

profile of v12, /device:TPU:6, one launch (start us, length us, event | category | flops | bytes accessed | tf_op | source)
XLA Modules:
  0.0 382.7 jit_solution(6498863904490996244)
XLA Ops:
  7.2 1.2 copy-done
  8.4 0.3 broadcast_in_dim.35
  8.7 30.6 %all_to_all.30 = bf16[4,256,1024]{2,1,0:T(8,128)(2,1)S(1)} all-to-all(bf16[4,256,1024]{2,1,0:T(8,128)(2,1)S(1)} %broadcast_in_dim.35), channel_id=1, replica_groups=mesh['dx'=4,'dz'=16,'dc'=2,'bin'=4] {'bin'}, dimensions={0} | all-to-all | bytes 4194304 | tf_op jit(solution)/shard_map/all_to_all | solution.py:81
  39.3 2.0 collective-permute-start
  41.4 2.3 reshape.199
  43.6 0.2 convert_reduce_fusion.3
  43.8 0.2 convert_reduce_fusion.2
  44.0 0.1 select_reduce_fusion.1
  44.2 0.1 add_add_fusion
  44.3 0.1 add.157
  44.4 0.2 convert_reduce_fusion
  44.7 0.9 collective-permute-done
  45.6 1.9 select_bitcast_fusion.1
  47.5 0.4 pad_maximum_fusion
  47.9 0.8 copy-done.3
  48.7 1.3 multiply_reduce_fusion
  50.1 1.0 copy-done.1
  51.1 2.2 fusion.2
  53.2 20.0 %all-to-all-start.1 = ((bf16[128,8,1024]{2,1,0:T(8,128)(2,1)}), bf16[128,8,1024]{2,1,0:T(8,128)(2,1)S(1)}, u32[]{:S(2)}, u32[]{:S(2)}) async-start(bf16[128,8,1024]{2,1,0:T(8,128)(2,1)} %fusion.2), calls=%async_computation.1 | async-start | bytes 4194304 | tf_op jit(solution)/shard_map/all_to_all | solution.py:115
  73.3 0.6 fusion.37
  75.9 0.6 fusion.42
  76.5 94.3 %all-to-all-done.1 = bf16[128,8,1024]{2,1,0:T(8,128)(2,1)S(1)} async-done(((bf16[128,8,1024]{2,1,0:T(8,128)(2,1)}), bf16[128,8,1024]{2,1,0:T(8,128)(2,1)S(1)}, u32[]{:S(2)}, u32[]{:S(2)}) %all-to-all-start.1) | async-done | bytes 2097184 | tf_op jit(solution)/shard_map/all_to_all | solution.py:115
  170.8 1.2 copy.75
  171.9 0.2 fusion.41
  172.2 0.8 copy.78
  173.0 1.1 reshape_squeeze.6
  174.1 0.8 copy.79
  175.0 1.2 reshape_squeeze.7
  176.1 0.9 copy.77
  177.0 0.1 lt.103
  177.2 4.0 %fusion.43 = (f32[512]{0:T(512)S(1)}, f32[512,512]{0,1:T(8,128)S(1)}) fusion(bf16[512,1024]{1,0:T(8,128)(2,1)S(1)} %copy-done.4, bf16[512,1024]{1,0:T(8,128)(2,1)} %reshape_squeeze.7, s32[]{:T(128)} %bitcast.16, s32[]{:T(128)} %bitcast.15, s32[512]{0:T(512)S(1)} %add_select_fusion.2, pred[512]{0:T(512)(128)(4,1)S(1)} %lt.103), kind=kOutput, calls=%fused_computation.105 | convolution fusion | flops 542113280 | bytes 3150344 | tf_op jit(solution)/shard_map/dot_general | solution.py:36
  181.2 1.8 multiply_convert_fusion.1
  183.0 1.7 multiply_convert_fusion
  184.7 1.5 stack_reshape.6
  186.1 0.3 copy.80
  186.5 1.5 stack_reshape.7
  187.9 0.3 copy.81
  188.2 0.2 pad_maximum_fusion.1
  188.4 2.5 copy.82
  190.9 10.3 %all-to-all-start.2 = ((bf16[128,8,1024]{2,1,0:T(8,128)(2,1)}), bf16[128,8,1024]{2,1,0:T(8,128)(2,1)S(1)}, u32[]{:S(2)}, u32[]{:S(2)}) async-start(bf16[128,8,1024]{2,1,0:T(8,128)(2,1)} %copy.82), calls=%async_computation.2 | async-start | bytes 4194304 | tf_op jit(solution)/shard_map/all_to_all | solution.py:126
  201.3 0.3 all-gather.2.cloned.1.call-start
  201.5 2.3 copy.83
  203.9 94.9 %all-to-all-done.2 = bf16[128,8,1024]{2,1,0:T(8,128)(2,1)S(1)} async-done(((bf16[128,8,1024]{2,1,0:T(8,128)(2,1)}), bf16[128,8,1024]{2,1,0:T(8,128)(2,1)S(1)}, u32[]{:S(2)}, u32[]{:S(2)}) %all-to-all-start.2) | async-done | bytes 2097184 | tf_op jit(solution)/shard_map/all_to_all | solution.py:126
  298.7 2.2 fusion.6
  300.9 0.3 fusion.9
  301.2 1.6 broadcast_in_dim.41
  302.8 4.4 %all-to-all-start.3 = ((bf16[4,256,1024]{2,1,0:T(8,128)(2,1)}), bf16[4,256,1024]{2,1,0:T(8,128)(2,1)}, u32[]{:S(2)}, u32[]{:S(2)}) async-start(bf16[4,256,1024]{2,1,0:T(8,128)(2,1)} %broadcast_in_dim.41), calls=%async_computation.3 | async-start | bytes 4194304 | tf_op jit(solution)/shard_map/all_to_all | solution.py:141
  307.3 1.3 dynamic-slice_bitcast_fusion.1
  308.6 1.2 dot_general.32
  309.8 24.1 %all-to-all-done.3 = bf16[4,256,1024]{2,1,0:T(8,128)(2,1)} async-done(((bf16[4,256,1024]{2,1,0:T(8,128)(2,1)}), bf16[4,256,1024]{2,1,0:T(8,128)(2,1)}, u32[]{:S(2)}, u32[]{:S(2)}) %all-to-all-start.3) | async-done | bytes 2097184 | tf_op jit(solution)/shard_map/all_to_all | solution.py:141
  333.9 3.4 fusion.10
  337.3 0.1 dynamic-slice_bitcast_fusion
  337.4 1.9 collective-permute-start.1
  339.3 2.6 collective-permute-done.1
  342.0 0.2 fusion.5
  342.1 0.4 copy.85
  342.6 0.2 copy.86
  342.7 13.6 %all_to_all.31 = bf16[4,64,1024]{2,1,0:T(8,128)(2,1)S(1)} all-to-all(bf16[4,64,1024]{2,1,0:T(8,128)(2,1)S(1)} %copy.86), channel_id=1, replica_groups=mesh['dx'=4,'dz'=16,'dc'=2,'bin'=4] {'dx'}, dimensions={0} | all-to-all | bytes 1048576 | tf_op jit(solution)/shard_map/all_to_all | solution.py:162
  356.4 0.1 reduce_sum.117
  356.4 0.7 convert_element_type.82
  357.1 4.1 %all-to-all-start.5 = ((bf16[16,4,1024]{2,1,0:T(4,128)(2,1)}), bf16[16,4,1024]{2,1,0:T(4,128)(2,1)S(1)}, u32[]{:S(2)}, u32[]{:S(2)}) async-start(bf16[16,4,1024]{2,1,0:T(4,128)(2,1)} %convert_element_type.82), calls=%async_computation.5 | async-start | bytes 262144 | tf_op jit(solution)/shard_map/all_to_all | solution.py:165
  361.2 1.0 reshape.204
  362.2 13.0 %all-to-all-done.5 = bf16[16,4,1024]{2,1,0:T(4,128)(2,1)S(1)} async-done(((bf16[16,4,1024]{2,1,0:T(4,128)(2,1)}), bf16[16,4,1024]{2,1,0:T(4,128)(2,1)S(1)}, u32[]{:S(2)}, u32[]{:S(2)}) %all-to-all-start.5) | async-done | bytes 131104 | tf_op jit(solution)/shard_map/all_to_all | solution.py:165
  375.3 0.6 broadcast_multiply_fusion
  (29 shorter events, 0.4 us)
Async XLA Ops:
  7.2 1.2 copy-start
  39.3 4.3 %copy-start.7 = (s32[128,1]{0,1:T(1,128)S(1)}, s32[128,1]{0,1:T(1,128)}, u32[]{:S(2)}) copy-start(s32[128,1]{0,1:T(1,128)} %param.7) | copy-start | bytes 1540
  39.3 4.5 %copy-start.6 = (s32[192]{0:T(256)S(1)}, s32[192]{0:T(256)}, u32[]{:S(2)}) copy-start(s32[192]{0:T(256)} %param.8) | copy-start | bytes 2308
  39.3 6.3 %collective-permute-start = (bf16[4,256,1024]{2,1,0:T(8,128)(2,1)S(1)}, bf16[4,256,1024]{2,1,0:T(8,128)(2,1)}, u32[]{:S(2)}, u32[]{:S(2)}) collective-permute-start(bf16[4,256,1024]{2,1,0:T(8,128)(2,1)S(1)} %all_to_all.30), channel_id=1, source_target_pairs={{0,4},{4,0},{1,5},{5,1},{2,6},{6,2},{3,7},{7,3},{8,12},{12,8},{9,1... | collective-permute-start | bytes 6291464 | tf_op jit(solution)/shard_map/ppermute | solution.py:82
  47.5 1.2 copy-start.3
  50.0 1.0 copy-start.1
  53.2 22.6 %copy-start.8 = (s32[192]{0:T(256)S(1)}, s32[192]{0:T(256)}, u32[]{:S(2)}) copy-start(s32[192]{0:T(256)} %param.9) | copy-start | bytes 2308
  53.2 117.6 %all-to-all-start.1 = ((bf16[128,8,1024]{2,1,0:T(8,128)(2,1)}), bf16[128,8,1024]{2,1,0:T(8,128)(2,1)S(1)}, u32[]{:S(2)}, u32[]{:S(2)}) async-start(bf16[128,8,1024]{2,1,0:T(8,128)(2,1)} %fusion.2), calls=%async_computation.1 | async-start | bytes 4194304 | tf_op jit(solution)/shard_map/all_to_all | solution.py:115
  174.9 2.2 copy-start.4
  177.2 4.0 %copy-start.5 = (bf16[512,1024]{1,0:T(8,128)(2,1)S(1)}, bf16[512,1024]{1,0:T(8,128)(2,1)}, u32[]{:S(2)}) copy-start(bf16[512,1024]{1,0:T(8,128)(2,1)} %reshape_squeeze.7) | copy-start | bytes 3145732
  190.9 107.8 %all-to-all-start.2 = ((bf16[128,8,1024]{2,1,0:T(8,128)(2,1)}), bf16[128,8,1024]{2,1,0:T(8,128)(2,1)S(1)}, u32[]{:S(2)}, u32[]{:S(2)}) async-start(bf16[128,8,1024]{2,1,0:T(8,128)(2,1)} %copy.82), calls=%async_computation.2 | async-start | bytes 4194304 | tf_op jit(solution)/shard_map/all_to_all | solution.py:126
  201.3 106.0 %all-gather.2.cloned.1.call-start = ((), (), s32[]{:S(2)}) async-start(), calls=%async_computation.6 | async-start | bytes 5242880 | tf_op jit(solution)/shard_map/all_gather | solution.py:140
  298.7 2.2 copy-start.2
  302.8 31.1 %all-to-all-start.3 = ((bf16[4,256,1024]{2,1,0:T(8,128)(2,1)}), bf16[4,256,1024]{2,1,0:T(8,128)(2,1)}, u32[]{:S(2)}, u32[]{:S(2)}) async-start(bf16[4,256,1024]{2,1,0:T(8,128)(2,1)} %broadcast_in_dim.41), calls=%async_computation.3 | async-start | bytes 4194304 | tf_op jit(solution)/shard_map/all_to_all | solution.py:141
  337.4 4.6 %collective-permute-start.1 = (f32[4,16,4,1024]{3,1,2,0:T(8,128)S(1)}, f32[4,16,4,1024]{3,1,2,0:T(8,128)S(1)}, u32[]{:S(2)}, u32[]{:S(2)}) collective-permute-start(f32[4,16,4,1024]{3,1,2,0:T(8,128)S(1)} %dynamic-slice_bitcast_fusion), channel_id=1, source_target_pairs={{0,4},{4,0},{1,5},{5,1},{2,6},{6,2},{3,7},{7,3},{8,12},{12,8},{9,1... | collective-permute-start | bytes 3145736 | tf_op jit(solution)/shard_map/ppermute | solution.py:160
  357.1 18.1 %all-to-all-start.5 = ((bf16[16,4,1024]{2,1,0:T(4,128)(2,1)}), bf16[16,4,1024]{2,1,0:T(4,128)(2,1)S(1)}, u32[]{:S(2)}, u32[]{:S(2)}) async-start(bf16[16,4,1024]{2,1,0:T(4,128)(2,1)} %convert_element_type.82), calls=%async_computation.5 | async-start | bytes 262144 | tf_op jit(solution)/shard_map/all_to_all | solution.py:165
Sparse Core Ops, SparseCore 0:
  204.2 58.3 all-gather.1

commit v13 on v10

--- a/solution.py
+++ b/solution.py
@@ -117,6 +117,10 @@
         outbox.reshape(sources, block, emb_dim), DP, split_axis=0, concat_axis=0, tiled=True
     )
     inbox = inbox.reshape(sources, views, per_owner, emb_dim)
+    columns = lax.all_to_all(
+        flat.reshape(rows_dev * views, bins_n, part_rows), "bin", split_axis=1, concat_axis=0, tiled=True
+    ).reshape(bins_n * rows_dev * views, part_rows)
+    inbox, columns = lax.optimization_barrier((inbox, columns))
     valid = (inbox[:, 0, :, 0] < 2.0).reshape(group_slots)
     query = inbox[:, 0].reshape(group_slots, emb_dim)
     key = inbox[:, 1].reshape(group_slots, emb_dim)
@@ -136,8 +140,6 @@
     grad_rows = (
         scale * (row_grads - unit * jnp.sum(unit * row_grads, axis=2, keepdims=True))
     ).astype(jnp.bfloat16)
-    column_start = lax.axis_index("bin") * part_rows
-    trunk = lax.all_gather(features, "bin", axis=0, tiled=True)
     outgrad = lax.all_to_all(
         jnp.broadcast_to(grad_rows[None], (bins_n, *grad_rows.shape)),
         "bin",
@@ -145,11 +147,9 @@
         concat_axis=0,
         tiled=True,
     )
-    columns = lax.dynamic_slice_in_dim(trunk, column_start, part_rows, 2)
-    count = trunk.shape[0]
     local_grad = lax.dot_general(
-        columns.reshape(count * views, part_rows),
-        outgrad.reshape(count * views, emb_dim),
+        columns,
+        outgrad.reshape(-1, emb_dim),
         (((0,), (0,)), ((), ())),
         preferred_element_type=jnp.float32,
     )

time: 380 us -> 391 us (1.029)
  between operations: 16.4 us -> 2.96 us
  waiting for transfers between devices: 215 us -> 226 us
  local copies, waits for them, and re-layouts: 27.3 us -> 36.2 us
    all_to_all x0 -> x1, waiting for transfers between devices: none -> 9.17 us  [local(): lax.all_to_all(flat.reshape(rows_dev * views, bins_n, part_rows), 'bin',...]
    another operation x0 -> x2, local copies, waits for them, and re-layouts: none -> 3.93 us  [local(): flat.reshape(rows_dev * views, bins_n, part_rows)]
  transfers between devices with their start and end apart: 6 -> 6, of which waited for: 5 -> 6; matrix products, arithmetic and copies ran while one was open for 4% -> 4% of each run, Pallas kernels for 0% -> 0%
where the time goes in v13:
time: 391 us; the launch traced here: 390 us
  waiting for transfers between devices  226 us (58%)
  blocking collectives  62.2 us (16%)
  starting transfers between devices  41.5 us (11%)
  local copies, waits for them, and re-layouts  36.2 us (9%)
  matrix products  13.5 us (3%)
  other arithmetic  6.88 us (2%)
    all_to_all x1, waiting for transfers between devices, local(): lax.all_to_all(back.reshape(sources, block, emb_dim), DP, split_axis=0, c...  95.5 us
    all_to_all x1, waiting for transfers between devices, local(): lax.all_to_all(outbox.reshape(sources, block, emb_dim), DP, split_axis=0,...  93.6 us
    all_to_all x1, blocking collectives, local(): lax.all_to_all(copies, 'bin', split_axis=0, concat_axis=0, tiled=True)  30.7 us
    all_to_all x1, waiting for transfers between devices, local(): lax.all_to_all(jnp.broadcast_to(grad_rows[None], (bins_n, *grad_rows.shap...  23.8 us
    all_to_all x1, starting transfers between devices, local(): lax.all_to_all(outbox.reshape(sources, block, emb_dim), DP, split_axis=0,...  19.9 us
    all_to_all x1, blocking collectives, local(): lax.all_to_all(planes, 'dz', split_axis=0, concat_axis=0, tiled=True)  17.8 us
    all_to_all x1, blocking collectives, local(): lax.all_to_all(planes, 'dx', split_axis=0, concat_axis=0, tiled=True)  13.6 us
    all_to_all x1, starting transfers between devices, local(): lax.all_to_all(back.reshape(sources, block, emb_dim), DP, split_axis=0, c...  10.2 us
  transfers between devices with their start and end apart: 6, of which 6 were waited for; matrix products, arithmetic and copies ran while one was open for 4% of the time, Pallas kernels for 0%

profile of v13, /device:TPU:6, one launch (start us, length us, event | category | flops | bytes accessed | tf_op | source)
XLA Modules:
  0.0 389.6 jit_solution(1221963766249308315)
XLA Ops:
  0.7 1.2 copy-done
  1.9 0.3 broadcast_in_dim.35
  2.2 30.7 %all_to_all.45 = bf16[4,256,1024]{2,1,0:T(8,128)(2,1)S(1)} all-to-all(bf16[4,256,1024]{2,1,0:T(8,128)(2,1)S(1)} %broadcast_in_dim.35), channel_id=1, replica_groups=mesh['dx'=4,'dz'=16,'dc'=2,'bin'=4] {'bin'}, dimensions={0} | all-to-all | bytes 4194304 | tf_op jit(solution)/shard_map/all_to_all | solution.py:81
  32.9 2.0 collective-permute-start
  35.0 1.2 reshape.231
  36.2 0.2 convert_reduce_fusion.3
  36.4 0.2 convert_reduce_fusion.2
  37.1 0.2 convert_reduce_fusion
  37.3 1.9 collective-permute-done
  39.2 1.9 select_bitcast_fusion.1
  41.1 0.4 pad_maximum_fusion
  41.5 0.8 copy-done.9
  42.3 1.3 multiply_reduce_fusion
  43.7 1.0 copy-done.8
  44.6 2.2 fusion.5
  46.8 19.9 %all-to-all-start.1 = ((bf16[128,8,1024]{2,1,0:T(8,128)(2,1)}), bf16[128,8,1024]{2,1,0:T(8,128)(2,1)S(1)}, u32[]{:S(2)}, u32[]{:S(2)}) async-start(bf16[128,8,1024]{2,1,0:T(8,128)(2,1)} %fusion.5), calls=%async_computation.1 | async-start | bytes 4194304 | tf_op jit(solution)/shard_map/all_to_all | solution.py:116
  66.7 1.5 reshape_reshape.3
  68.2 2.4 copy.117
  70.6 93.6 %all-to-all-done.1 = bf16[128,8,1024]{2,1,0:T(8,128)(2,1)S(1)} async-done(((bf16[128,8,1024]{2,1,0:T(8,128)(2,1)}), bf16[128,8,1024]{2,1,0:T(8,128)(2,1)S(1)}, u32[]{:S(2)}, u32[]{:S(2)}) %all-to-all-start.1) | async-done | bytes 2097184 | tf_op jit(solution)/shard_map/all_to_all | solution.py:116
  164.2 3.7 all-to-all-start.2
  167.9 0.6 fusion.43
  170.6 0.6 fusion.48
  171.2 2.7 copy.116
  173.9 9.2 %all-to-all-done.2 = bf16[256,4,512]{2,0,1:T(8,128)(2,1)S(1)} async-done(((bf16[256,4,512]{2,0,1:T(8,128)(2,1)}), bf16[256,4,512]{2,0,1:T(8,128)(2,1)S(1)}, u32[]{:S(2)}, u32[]{:S(2)}) %all-to-all-start.2) | async-done | bytes 1048608 | tf_op jit(solution)/shard_map/all_to_all | solution.py:120
  183.1 1.7 fusion.47
  184.8 2.6 copy.118
  187.4 2.1 copy.120
  189.5 0.3 reshape_squeeze.6
  189.8 0.8 copy.121
  190.6 0.3 reshape_squeeze.7
  190.9 0.7 slice_compare_fusion
  191.6 0.1 copy.119
  191.8 2.7 fusion.49
  194.5 1.8 multiply_convert_fusion.1
  196.3 1.7 multiply_convert_fusion
  198.0 0.4 stack_reshape.6
  198.5 0.3 copy.122
  198.8 0.5 copy-done.10
  199.3 0.4 stack_reshape.7
  199.7 0.3 copy.123
  200.0 0.2 pad_maximum_fusion.1
  200.2 2.5 copy.124
  202.7 10.2 %all-to-all-start.3 = ((bf16[128,8,1024]{2,1,0:T(8,128)(2,1)}), bf16[128,8,1024]{2,1,0:T(8,128)(2,1)S(1)}, u32[]{:S(2)}, u32[]{:S(2)}) async-start(bf16[128,8,1024]{2,1,0:T(8,128)(2,1)} %copy.124), calls=%async_computation.3 | async-start | bytes 4194304 | tf_op jit(solution)/shard_map/all_to_all | solution.py:131
  212.9 1.8 reshape.237
  214.9 95.5 %all-to-all-done.3 = bf16[128,8,1024]{2,1,0:T(8,128)(2,1)S(1)} async-done(((bf16[128,8,1024]{2,1,0:T(8,128)(2,1)}), bf16[128,8,1024]{2,1,0:T(8,128)(2,1)S(1)}, u32[]{:S(2)}, u32[]{:S(2)}) %all-to-all-start.3) | async-done | bytes 2097184 | tf_op jit(solution)/shard_map/all_to_all | solution.py:131
  310.4 0.8 fusion.1
  311.2 1.3 fusion.11
  312.5 0.5 copy.132
  313.1 0.8 copy-done.7
  313.8 2.4 broadcast_in_dim.41
  316.3 3.7 all-to-all-start.4
  320.0 1.3 copy.126
  321.4 1.5 dot_general.35
  322.8 23.8 %all-to-all-done.4 = bf16[4,128,2,1024]{3,2,1,0:T(2,128)(2,1)S(1)} async-done(((bf16[4,128,2,1024]{3,2,1,0:T(2,128)(2,1)}), bf16[4,128,2,1024]{3,2,1,0:T(2,128)(2,1)S(1)}, u32[]{:S(2)}, u32[]{:S(2)}) %all-to-all-start.4) | async-done | bytes 2097184 | tf_op jit(solution)/shard_map/all_to_all | solution.py:143
  346.6 2.2 reshape.240
  348.8 3.0 fusion.3
  352.0 1.9 collective-permute-start.1
  353.9 2.6 collective-permute-done.1
  356.6 0.2 fusion.12
  356.7 0.4 copy.129
  357.1 0.2 copy.130
  357.3 13.6 %all_to_all.46 = bf16[4,64,1024]{2,1,0:T(8,128)(2,1)S(1)} all-to-all(bf16[4,64,1024]{2,1,0:T(8,128)(2,1)S(1)} %copy.130), channel_id=1, replica_groups=mesh['dx'=4,'dz'=16,'dc'=2,'bin'=4] {'dx'}, dimensions={0} | all-to-all | bytes 1048576 | tf_op jit(solution)/shard_map/all_to_all | solution.py:163
  371.1 17.8 %all_to_all.47 = bf16[16,4,1024]{2,1,0:T(4,128)(2,1)S(1)} all-to-all(bf16[16,4,1024]{2,1,0:T(4,128)(2,1)S(1)} %convert_element_type.83), channel_id=1, replica_groups=mesh['dx'=4,'dz'=16,'dc'=2,'bin'=4] {'dz'}, dimensions={0} | all-to-all | bytes 262144 | tf_op jit(solution)/shard_map/all_to_all | solution.py:166
  389.0 0.6 broadcast_multiply_fusion
  (46 shorter events, 1.3 us)
Async XLA Ops:
  0.6 1.2 copy-start
  2.2 32.8 %copy-start.3 = (bf16[128,2,2048]{2,1,0:T(2,128)(2,1)S(1)}, bf16[128,2,2048]{2,1,0:T(2,128)(2,1)}, u32[]{:S(2)}) copy-start(bf16[128,2,2048]{2,1,0:T(2,128)(2,1)} %param.5) | copy-start | bytes 3145732
  32.9 3.3 copy-start.13
  32.9 3.5 copy-start.12
  32.9 6.3 %collective-permute-start = (bf16[4,256,1024]{2,1,0:T(8,128)(2,1)S(1)}, bf16[4,256,1024]{2,1,0:T(8,128)(2,1)}, u32[]{:S(2)}, u32[]{:S(2)}) collective-permute-start(bf16[4,256,1024]{2,1,0:T(8,128)(2,1)S(1)} %all_to_all.45), channel_id=1, source_target_pairs={{0,4},{4,0},{1,5},{5,1},{2,6},{6,2},{3,7},{7,3},{8,12},{12,8},{9,1... | collective-permute-start | bytes 6291464 | tf_op jit(solution)/shard_map/ppermute | solution.py:82
  41.1 1.2 copy-start.9
  43.6 1.0 copy-start.8
  46.8 117.4 %all-to-all-start.1 = ((bf16[128,8,1024]{2,1,0:T(8,128)(2,1)}), bf16[128,8,1024]{2,1,0:T(8,128)(2,1)S(1)}, u32[]{:S(2)}, u32[]{:S(2)}) async-start(bf16[128,8,1024]{2,1,0:T(8,128)(2,1)} %fusion.5), calls=%async_computation.1 | async-start | bytes 4194304 | tf_op jit(solution)/shard_map/all_to_all | solution.py:116
  68.2 102.3 %copy-start.14 = (s32[192]{0:T(256)S(1)}, s32[192]{0:T(256)}, u32[]{:S(2)}) copy-start(s32[192]{0:T(256)} %param.9) | copy-start | bytes 2308
  164.2 6.4 %copy-start.2 = (bf16[128,8,1024]{2,1,0:T(8,128)(2,1)}, bf16[128,8,1024]{2,1,0:T(8,128)(2,1)S(1)}, u32[]{:S(2)}) copy-start(bf16[128,8,1024]{2,1,0:T(8,128)(2,1)S(1)} %all-to-all-done.1) | copy-start | bytes 6291460
  164.2 18.9 %all-to-all-start.2 = ((bf16[256,4,512]{2,0,1:T(8,128)(2,1)}), bf16[256,4,512]{2,0,1:T(8,128)(2,1)S(1)}, u32[]{:S(2)}, u32[]{:S(2)}) async-start(bf16[256,4,512]{2,0,1:T(8,128)(2,1)} %copy.117), calls=%async_computation.2 | async-start | bytes 2097152 | tf_op jit(solution)/shard_map/all_to_all | solution.py:120
  183.1 1.7 copy-start.4
  187.4 2.4 copy-start.6
  196.3 1.7 copy-start.11
  198.0 1.2 copy-start.10
  202.7 107.7 %all-to-all-start.3 = ((bf16[128,8,1024]{2,1,0:T(8,128)(2,1)}), bf16[128,8,1024]{2,1,0:T(8,128)(2,1)S(1)}, u32[]{:S(2)}, u32[]{:S(2)}) async-start(bf16[128,8,1024]{2,1,0:T(8,128)(2,1)} %copy.124), calls=%async_computation.3 | async-start | bytes 4194304 | tf_op jit(solution)/shard_map/all_to_all | solution.py:131
  313.0 0.8 copy-start.7
  316.3 3.8 copy-start.5
  316.3 30.3 %all-to-all-start.4 = ((bf16[4,128,2,1024]{3,2,1,0:T(2,128)(2,1)}), bf16[4,128,2,1024]{3,2,1,0:T(2,128)(2,1)S(1)}, u32[]{:S(2)}, u32[]{:S(2)}) async-start(bf16[4,128,2,1024]{3,2,1,0:T(2,128)(2,1)} %broadcast_in_dim.41), calls=%async_computation.4 | async-start | bytes 4194304 | tf_op jit(solution)/shard_map/all_to_all | solution.py:143
  352.0 4.6 %collective-permute-start.1 = (f32[4,16,4,1024]{3,1,2,0:T(8,128)S(1)}, f32[4,16,4,1024]{3,1,2,0:T(8,128)S(1)}, u32[]{:S(2)}, u32[]{:S(2)}) collective-permute-start(f32[4,16,4,1024]{3,1,2,0:T(8,128)S(1)} %dynamic-slice_bitcast_fusion), channel_id=1, source_target_pairs={{0,4},{4,0},{1,5},{5,1},{2,6},{6,2},{3,7},{7,3},{8,12},{12,8},{9,1... | collective-permute-start | bytes 3145736 | tf_op jit(solution)/shard_map/ppermute | solution.py:161
  356.6 33.0 %copy-start.1 = (bf16[512,1024]{1,0:T(8,128)(2,1)S(1)}, bf16[512,1024]{1,0:T(8,128)(2,1)}, u32[]{:S(2)}) copy-start(bf16[512,1024]{1,0:T(8,128)(2,1)} %param.6) | copy-start | bytes 3145732

commit v14 on v13

--- a/solution.py
+++ b/solution.py
@@ -120,7 +120,6 @@
     columns = lax.all_to_all(
         flat.reshape(rows_dev * views, bins_n, part_rows), "bin", split_axis=1, concat_axis=0, tiled=True
     ).reshape(bins_n * rows_dev * views, part_rows)
-    inbox, columns = lax.optimization_barrier((inbox, columns))
     valid = (inbox[:, 0, :, 0] < 2.0).reshape(group_slots)
     query = inbox[:, 0].reshape(group_slots, emb_dim)
     key = inbox[:, 1].reshape(group_slots, emb_dim)
@@ -128,6 +127,7 @@
     allowed = allowed_mask(valid, first, bin_link, group_slots, per_bin)
     grads = contrast(query, key, allowed, valid.astype(jnp.float32))
     back = jnp.stack([g.reshape(sources, per_owner, emb_dim) for g in grads], axis=1)
+    back, columns = lax.optimization_barrier((back, columns))
     returned = lax.all_to_all(
         back.reshape(sources, block, emb_dim), DP, split_axis=0, concat_axis=0, tiled=True
     )

time: 391 us -> 382 us (0.977)
  waiting for transfers between devices: 226 us -> 215 us
    all_to_all x1, waiting for transfers between devices: 9.17 us -> 0.01 us  [local(): lax.all_to_all(flat.reshape(rows_dev * views, bins_n, part_rows), 'bin',...]
  transfers between devices with their start and end apart: 6 -> 6, of which waited for: 6 -> 5; matrix products, arithmetic and copies ran while one was open for 4% -> 8% of each run, Pallas kernels for 0% -> 0%
where the time goes in v14:
time: 382 us; the launch traced here: 380 us
  waiting for transfers between devices  215 us (56%)
  blocking collectives  62.2 us (16%)
  starting transfers between devices  43.1 us (11%)
  local copies, waits for them, and re-layouts  34.9 us (9%)
  matrix products  16.4 us (4%)
  other arithmetic  6.24 us (2%)
    all_to_all x1, waiting for transfers between devices, local(): lax.all_to_all(back.reshape(sources, block, emb_dim), DP, split_axis=0, c...  96.3 us
    all_to_all x1, waiting for transfers between devices, local(): lax.all_to_all(outbox.reshape(sources, block, emb_dim), DP, split_axis=0,...  90.3 us
    all_to_all x1, blocking collectives, local(): lax.all_to_all(copies, 'bin', split_axis=0, concat_axis=0, tiled=True)  30.7 us
    all_to_all x1, waiting for transfers between devices, local(): lax.all_to_all(jnp.broadcast_to(grad_rows[None], (bins_n, *grad_rows.shap...  23.5 us
    all_to_all x1, starting transfers between devices, local(): lax.all_to_all(outbox.reshape(sources, block, emb_dim), DP, split_axis=0,...  19.9 us
    all_to_all x1, blocking collectives, local(): lax.all_to_all(planes, 'dz', split_axis=0, concat_axis=0, tiled=True)  17.8 us
    all_to_all x1, blocking collectives, local(): lax.all_to_all(planes, 'dx', split_axis=0, concat_axis=0, tiled=True)  13.6 us
    all_to_all x1, starting transfers between devices, local(): lax.all_to_all(back.reshape(sources, block, emb_dim), DP, split_axis=0, c...  11 us
  transfers between devices with their start and end apart: 6, of which 5 were waited for; matrix products, arithmetic and copies ran while one was open for 8% of the time, Pallas kernels for 0%

profile of v14, /device:TPU:6, one launch (start us, length us, event | category | flops | bytes accessed | tf_op | source)
XLA Modules:
  0.0 380.5 jit_solution(13408095489413617713)
XLA Ops:
  0.7 1.2 copy-done
  1.9 0.3 broadcast_in_dim.35
  2.2 30.7 %all_to_all.45 = bf16[4,256,1024]{2,1,0:T(8,128)(2,1)S(1)} all-to-all(bf16[4,256,1024]{2,1,0:T(8,128)(2,1)S(1)} %broadcast_in_dim.35), channel_id=1, replica_groups=mesh['dx'=4,'dz'=16,'dc'=2,'bin'=4] {'bin'}, dimensions={0} | all-to-all | bytes 4194304 | tf_op jit(solution)/shard_map/all_to_all | solution.py:81
  32.9 2.0 collective-permute-start
  35.0 1.2 reshape.231
  36.2 0.2 convert_reduce_fusion.3
  36.4 0.2 convert_reduce_fusion.2
  36.6 0.1 select_reduce_fusion.1
  37.0 0.1 add.158
  37.1 0.2 convert_reduce_fusion
  37.3 1.9 collective-permute-done
  39.2 1.9 select_bitcast_fusion.1
  41.1 0.4 pad_maximum_fusion
  41.5 0.8 copy-done.7
  42.3 1.3 multiply_reduce_fusion
  43.7 1.0 copy-done.5
  44.6 2.1 fusion.5
  46.8 19.9 %all-to-all-start.1 = ((bf16[128,8,1024]{2,1,0:T(8,128)(2,1)}), bf16[128,8,1024]{2,1,0:T(8,128)(2,1)S(1)}, u32[]{:S(2)}, u32[]{:S(2)}) async-start(bf16[128,8,1024]{2,1,0:T(8,128)(2,1)} %fusion.5), calls=%async_computation.1 | async-start | bytes 4194304 | tf_op jit(solution)/shard_map/all_to_all | solution.py:116
  66.7 1.5 reshape_reshape.3
  68.2 0.6 fusion.43
  70.1 2.4 copy.123
  73.3 0.6 fusion.48
  73.9 90.3 %all-to-all-done.1 = bf16[128,8,1024]{2,1,0:T(8,128)(2,1)S(1)} async-done(((bf16[128,8,1024]{2,1,0:T(8,128)(2,1)}), bf16[128,8,1024]{2,1,0:T(8,128)(2,1)S(1)}, u32[]{:S(2)}, u32[]{:S(2)}) %all-to-all-start.1) | async-done | bytes 2097184 | tf_op jit(solution)/shard_map/all_to_all | solution.py:116
  164.2 3.7 all-to-all-start.2
  167.9 1.2 copy.116
  169.0 0.2 fusion.47
  169.3 0.8 copy.119
  170.1 1.1 reshape_squeeze.6
  171.2 0.8 copy.120
  172.0 1.2 reshape_squeeze.7
  173.2 0.9 copy.118
  174.2 4.0 %fusion.49 = (f32[512]{0:T(512)S(1)}, f32[512,512]{0,1:T(8,128)S(1)}) fusion(bf16[512,1024]{1,0:T(8,128)(2,1)S(1)} %copy-done.8, bf16[512,1024]{1,0:T(8,128)(2,1)} %reshape_squeeze.7, s32[]{:T(128)} %bitcast.17, s32[]{:T(128)} %bitcast.16, s32[512]{0:T(512)S(1)} %add_select_fusion.2, pred[512]{0:T(512)(128)(4,1)S(1)} %lt.100), kind=kOutput, calls=%fused_computation.111 | convolution fusion | flops 542113280 | bytes 3150344 | tf_op jit(solution)/shard_map/dot_general | solution.py:36
  178.2 1.0 copy-done.14
  179.2 1.8 multiply_convert_fusion.1
  181.0 1.5 stack_reshape.6
  182.6 1.3 copy.121
  183.9 1.7 multiply_convert_fusion
  185.6 1.5 stack_reshape.7
  187.1 0.3 copy.122
  187.4 0.9 copy-done.3
  188.3 0.2 pad_maximum_fusion.1
  188.5 2.5 copy.124
  191.0 11.0 %all-to-all-start.3 = ((bf16[128,8,1024]{2,1,0:T(8,128)(2,1)}), bf16[128,8,1024]{2,1,0:T(8,128)(2,1)}, u32[]{:S(2)}, u32[]{:S(2)}) async-start(bf16[128,8,1024]{2,1,0:T(8,128)(2,1)} %copy.124), calls=%async_computation.3 | async-start | bytes 4194304 | tf_op jit(solution)/shard_map/all_to_all | solution.py:131
  202.0 0.6 reshape.237
  202.8 96.3 %all-to-all-done.3 = bf16[128,8,1024]{2,1,0:T(8,128)(2,1)} async-done(((bf16[128,8,1024]{2,1,0:T(8,128)(2,1)}), bf16[128,8,1024]{2,1,0:T(8,128)(2,1)}, u32[]{:S(2)}, u32[]{:S(2)}) %all-to-all-start.3) | async-done | bytes 2097184 | tf_op jit(solution)/shard_map/all_to_all | solution.py:131
  299.1 2.3 fusion.1
  301.5 1.3 fusion.11
  302.8 0.5 copy.132
  303.4 0.8 copy-done.4
  304.2 2.4 broadcast_in_dim.41
  306.6 4.6 %all-to-all-start.4 = ((bf16[4,128,2,1024]{3,2,1,0:T(2,128)(2,1)}), bf16[4,128,2,1024]{3,2,1,0:T(2,128)(2,1)S(1)}, u32[]{:S(2)}, u32[]{:S(2)}) async-start(bf16[4,128,2,1024]{3,2,1,0:T(2,128)(2,1)} %broadcast_in_dim.41), calls=%async_computation.4 | async-start | bytes 4194304 | tf_op jit(solution)/shard_map/all_to_all | solution.py:143
  311.2 1.3 copy.126
  312.5 1.5 dot_general.35
  314.0 23.5 %all-to-all-done.4 = bf16[4,128,2,1024]{3,2,1,0:T(2,128)(2,1)S(1)} async-done(((bf16[4,128,2,1024]{3,2,1,0:T(2,128)(2,1)}), bf16[4,128,2,1024]{3,2,1,0:T(2,128)(2,1)S(1)}, u32[]{:S(2)}, u32[]{:S(2)}) %all-to-all-start.4) | async-done | bytes 2097184 | tf_op jit(solution)/shard_map/all_to_all | solution.py:143
  337.5 2.2 reshape.240
  339.7 3.1 fusion.3
  342.9 1.9 collective-permute-start.1
  344.8 2.6 collective-permute-done.1
  347.5 0.2 fusion.12
  347.6 0.4 copy.129
  348.0 0.2 copy.130
  348.2 13.6 %all_to_all.46 = bf16[4,64,1024]{2,1,0:T(8,128)(2,1)S(1)} all-to-all(bf16[4,64,1024]{2,1,0:T(8,128)(2,1)S(1)} %copy.130), channel_id=1, replica_groups=mesh['dx'=4,'dz'=16,'dc'=2,'bin'=4] {'dx'}, dimensions={0} | all-to-all | bytes 1048576 | tf_op jit(solution)/shard_map/all_to_all | solution.py:163
  362.0 17.8 %all_to_all.47 = bf16[16,4,1024]{2,1,0:T(4,128)(2,1)S(1)} all-to-all(bf16[16,4,1024]{2,1,0:T(4,128)(2,1)S(1)} %convert_element_type.83), channel_id=1, replica_groups=mesh['dx'=4,'dz'=16,'dc'=2,'bin'=4] {'dz'}, dimensions={0} | all-to-all | bytes 262144 | tf_op jit(solution)/shard_map/all_to_all | solution.py:166
  379.9 0.6 broadcast_multiply_fusion
  (47 shorter events, 1.1 us)
Async XLA Ops:
  0.6 1.2 copy-start
  2.2 32.8 %copy-start.2 = (bf16[128,2,2048]{2,1,0:T(2,128)(2,1)S(1)}, bf16[128,2,2048]{2,1,0:T(2,128)(2,1)}, u32[]{:S(2)}) copy-start(bf16[128,2,2048]{2,1,0:T(2,128)(2,1)} %param.5) | copy-start | bytes 3145732
  32.9 3.3 copy-start.12
  32.9 3.5 copy-start.11
  32.9 6.3 %collective-permute-start = (bf16[4,256,1024]{2,1,0:T(8,128)(2,1)S(1)}, bf16[4,256,1024]{2,1,0:T(8,128)(2,1)}, u32[]{:S(2)}, u32[]{:S(2)}) collective-permute-start(bf16[4,256,1024]{2,1,0:T(8,128)(2,1)S(1)} %all_to_all.45), channel_id=1, source_target_pairs={{0,4},{4,0},{1,5},{5,1},{2,6},{6,2},{3,7},{7,3},{8,12},{12,8},{9,1... | collective-permute-start | bytes 6291464 | tf_op jit(solution)/shard_map/ppermute | solution.py:82
  41.1 1.2 copy-start.7
  43.6 1.0 copy-start.5
  46.8 117.4 %all-to-all-start.1 = ((bf16[128,8,1024]{2,1,0:T(8,128)(2,1)}), bf16[128,8,1024]{2,1,0:T(8,128)(2,1)S(1)}, u32[]{:S(2)}, u32[]{:S(2)}) async-start(bf16[128,8,1024]{2,1,0:T(8,128)(2,1)} %fusion.5), calls=%async_computation.1 | async-start | bytes 4194304 | tf_op jit(solution)/shard_map/all_to_all | solution.py:116
  66.7 6.5 %copy-start.13 = (s32[192]{0:T(256)S(1)}, s32[192]{0:T(256)}, u32[]{:S(2)}) copy-start(s32[192]{0:T(256)} %param.9) | copy-start | bytes 2308
  164.2 24.3 %all-to-all-start.2 = ((bf16[256,4,512]{2,0,1:T(8,128)(2,1)}), bf16[256,4,512]{2,0,1:T(8,128)(2,1)S(1)}, u32[]{:S(2)}, u32[]{:S(2)}) async-start(bf16[256,4,512]{2,0,1:T(8,128)(2,1)} %copy.123), calls=%async_computation.2 | async-start | bytes 2097152 | tf_op jit(solution)/shard_map/all_to_all | solution.py:120
  172.0 2.2 copy-start.8
  174.2 5.0 %copy-start.10 = (bf16[512,1024]{1,0:T(8,128)(2,1)S(1)}, bf16[512,1024]{1,0:T(8,128)(2,1)}, u32[]{:S(2)}) copy-start(bf16[512,1024]{1,0:T(8,128)(2,1)} %reshape_squeeze.7) | copy-start | bytes 3145732
  178.2 1.0 copy-start.14
  181.0 2.9 copy-start.9
  182.6 1.4 copy-start.15
  187.1 1.2 copy-start.3
  191.0 11.0 %copy-start.6 = (f32[256,1024]{1,0:T(8,128)S(1)}, f32[256,1024]{1,0:T(8,128)}, u32[]{:S(2)}) copy-start(f32[256,1024]{1,0:T(8,128)} %copy-done.5) | copy-start | bytes 3145732
  191.0 108.2 %all-to-all-start.3 = ((bf16[128,8,1024]{2,1,0:T(8,128)(2,1)}), bf16[128,8,1024]{2,1,0:T(8,128)(2,1)}, u32[]{:S(2)}, u32[]{:S(2)}) async-start(bf16[128,8,1024]{2,1,0:T(8,128)(2,1)} %copy.124), calls=%async_computation.3 | async-start | bytes 4194304 | tf_op jit(solution)/shard_map/all_to_all | solution.py:131
  303.4 0.8 copy-start.4
  306.6 30.9 %all-to-all-start.4 = ((bf16[4,128,2,1024]{3,2,1,0:T(2,128)(2,1)}), bf16[4,128,2,1024]{3,2,1,0:T(2,128)(2,1)S(1)}, u32[]{:S(2)}, u32[]{:S(2)}) async-start(bf16[4,128,2,1024]{3,2,1,0:T(2,128)(2,1)} %broadcast_in_dim.41), calls=%async_computation.4 | async-start | bytes 4194304 | tf_op jit(solution)/shard_map/all_to_all | solution.py:143
  342.9 4.6 %collective-permute-start.1 = (f32[4,16,4,1024]{3,1,2,0:T(8,128)S(1)}, f32[4,16,4,1024]{3,1,2,0:T(8,128)S(1)}, u32[]{:S(2)}, u32[]{:S(2)}) collective-permute-start(f32[4,16,4,1024]{3,1,2,0:T(8,128)S(1)} %dynamic-slice_bitcast_fusion), channel_id=1, source_target_pairs={{0,4},{4,0},{1,5},{5,1},{2,6},{6,2},{3,7},{7,3},{8,12},{12,8},{9,1... | collective-permute-start | bytes 3145736 | tf_op jit(solution)/shard_map/ppermute | solution.py:161
  347.5 33.0 %copy-start.1 = (bf16[512,1024]{1,0:T(8,128)(2,1)S(1)}, bf16[512,1024]{1,0:T(8,128)(2,1)}, u32[]{:S(2)}) copy-start(bf16[512,1024]{1,0:T(8,128)(2,1)} %param.6) | copy-start | bytes 3145732

commit v15 on v10

--- a/solution.py
+++ b/solution.py
@@ -80,10 +80,12 @@
     copies = jnp.broadcast_to(half[None], (bins_n, part_rows // 2, emb_dim))
     mine = lax.all_to_all(copies, "bin", split_axis=0, concat_axis=0, tiled=True)
     theirs = lax.ppermute(mine, "dc", perm=[(0, 1), (1, 0)])
-    low = jnp.where(core == 0, mine, theirs)
-    high = jnp.where(core == 0, theirs, mine)
-    weight = jnp.stack([low, high], axis=1).reshape(feat_dim, emb_dim)
-    folded = jnp.dot(flat, weight, preferred_element_type=jnp.float32)
+    quarters = flat.reshape(rows_dev * views, bins_n, 2, part_rows // 2)
+    own_cols = lax.dynamic_index_in_dim(quarters, core, 2, keepdims=False)
+    other_cols = lax.dynamic_index_in_dim(quarters, 1 - core, 2, keepdims=False)
+    contract = (((1, 2), (0, 1)), ((), ()))
+    folded = lax.dot_general(own_cols, mine, contract, preferred_element_type=jnp.float32)
+    folded = folded + lax.dot_general(other_cols, theirs, contract, preferred_element_type=jnp.float32)
     embedded = folded.reshape(rows_dev, views, emb_dim)
     scale = lax.rsqrt(jnp.sum(embedded * embedded, axis=2, keepdims=True) + 1e-06)
     unit = embedded * scale

time: 380 us -> 389 us (1.024)
  local copies, waits for them, and re-layouts: 27.3 us -> 37.6 us
  matrix products: 13.5 us -> 19 us
  waiting for transfers between devices: 215 us -> 210 us
  transfers between devices with their start and end apart: 6 -> 6, of which waited for: 5 -> 4; matrix products, arithmetic and copies ran while one was open for 4% -> 6% of each run, Pallas kernels for 0% -> 0%
where the time goes in v15:
time: 389 us; the launch traced here: 388 us
  waiting for transfers between devices  210 us (54%)
  blocking collectives  62.3 us (16%)
  starting transfers between devices  38.8 us (10%)
  local copies, waits for them, and re-layouts  37.6 us (10%)
  matrix products  19 us (5%)
  between operations  16.4 us (4%)
  other arithmetic  3.99 us (1%)
    all_to_all x1, waiting for transfers between devices, local(): lax.all_to_all(back.reshape(sources, block, emb_dim), DP, split_axis=0, c...  95.6 us
    all_to_all x1, waiting for transfers between devices, local(): lax.all_to_all(outbox.reshape(sources, block, emb_dim), DP, split_axis=0,...  94.3 us
    all_to_all x1, blocking collectives, local(): lax.all_to_all(copies, 'bin', split_axis=0, concat_axis=0, tiled=True)  30.8 us
    all_to_all x1, starting transfers between devices, local(): lax.all_to_all(outbox.reshape(sources, block, emb_dim), DP, split_axis=0,...  20.1 us
    all_to_all x1, blocking collectives, local(): lax.all_to_all(planes, 'dz', split_axis=0, concat_axis=0, tiled=True)  17.8 us
    all_to_all x1, waiting for transfers between devices, local(): lax.all_to_all(jnp.broadcast_to(grad_rows[None], (bins_n, *grad_rows.shap...  16.8 us
    all_to_all x1, blocking collectives, local(): lax.all_to_all(planes, 'dx', split_axis=0, concat_axis=0, tiled=True)  13.6 us
    all_to_all x1, starting transfers between devices, local(): lax.all_to_all(back.reshape(sources, block, emb_dim), DP, split_axis=0, c...  10.9 us
  transfers between devices with their start and end apart: 6, of which 4 were waited for; matrix products, arithmetic and copies ran while one was open for 6% of the time, Pallas kernels for 0%

profile of v15, /device:TPU:6, one launch (start us, length us, event | category | flops | bytes accessed | tf_op | source)
XLA Modules:
  0.0 387.8 jit_solution(7844718841462663807)
XLA Ops:
  7.2 1.2 copy-done
  8.4 0.3 broadcast_in_dim.35
  8.7 30.8 %all_to_all.30 = bf16[4,256,1024]{2,1,0:T(8,128)(2,1)} all-to-all(bf16[4,256,1024]{2,1,0:T(8,128)(2,1)S(1)} %broadcast_in_dim.35), channel_id=1, replica_groups=mesh['dx'=4,'dz'=16,'dc'=2,'bin'=4] {'bin'}, dimensions={0} | all-to-all | bytes 4194304 | tf_op jit(solution)/shard_map/all_to_all | solution.py:81
  39.6 1.9 collective-permute-start
  41.5 0.2 convert_reduce_fusion.3
  41.7 0.2 convert_reduce_fusion.2
  41.9 0.1 select_reduce_fusion.1
  42.2 0.1 add.169
  42.4 0.7 reshape_reshape.3
  43.1 0.2 convert_reduce_fusion
  43.3 2.2 constant_dynamic-slice_fusion.1
  45.5 2.3 convolution_bitcast_fusion.1
  47.8 2.4 multiply_reduce_fusion
  50.3 1.1 copy-done.1
  51.3 2.2 fusion.5
  53.5 20.1 %all-to-all-start.1 = ((bf16[128,8,1024]{2,1,0:T(8,128)(2,1)}), bf16[128,8,1024]{2,1,0:T(8,128)(2,1)S(1)}, u32[]{:S(2)}, u32[]{:S(2)}) async-start(bf16[128,8,1024]{2,1,0:T(8,128)(2,1)} %fusion.5), calls=%async_computation.1 | async-start | bytes 4194304 | tf_op jit(solution)/shard_map/all_to_all | solution.py:118
  73.7 0.6 fusion.44
  76.3 0.6 fusion.49
  76.9 94.3 %all-to-all-done.1 = bf16[128,8,1024]{2,1,0:T(8,128)(2,1)S(1)} async-done(((bf16[128,8,1024]{2,1,0:T(8,128)(2,1)}), bf16[128,8,1024]{2,1,0:T(8,128)(2,1)S(1)}, u32[]{:S(2)}, u32[]{:S(2)}) %all-to-all-start.1) | async-done | bytes 2097184 | tf_op jit(solution)/shard_map/all_to_all | solution.py:118
  171.2 1.2 copy.119
  172.4 1.2 fusion.48
  173.6 0.9 copy.121
  174.4 0.1 lt.107
  174.6 2.0 copy.123
  176.6 1.2 reshape_squeeze.7
  177.8 0.8 copy.122
  178.6 1.1 reshape_squeeze.6
  179.7 0.5 copy-done.5
  180.2 4.0 %fusion.50 = (f32[512]{0:T(512)S(1)}, f32[512,512]{0,1:T(8,128)S(1)}) fusion(bf16[512,1024]{1,0:T(8,128)(2,1)} %reshape_squeeze.6, bf16[512,1024]{1,0:T(8,128)(2,1)S(1)} %copy-done.5, s32[]{:T(128)} %bitcast.16, s32[]{:T(128)} %bitcast.15, s32[512]{0:T(512)S(1)} %add_select_fusion.2, pred[512]{0:T(512)(128)(4,1)S(1)} %lt.107), kind=kOutput, calls=%fused_computation.115 | convolution fusion | flops 542113280 | bytes 3150344 | tf_op jit(solution)/shard_map/dot_general | solution.py:36
  184.2 1.7 multiply_convert_fusion
  185.9 0.7 multiply_convert_fusion.1
  186.6 0.4 stack_reshape.6
  187.1 0.3 copy.124
  187.4 1.5 stack_reshape.7
  188.9 0.3 copy.125
  189.2 0.2 pad_maximum_fusion
  189.4 2.5 copy.126
  191.9 10.9 %all-to-all-start.2 = ((bf16[128,8,1024]{2,1,0:T(8,128)(2,1)}), bf16[128,8,1024]{2,1,0:T(8,128)(2,1)}, u32[]{:S(2)}, u32[]{:S(2)}) async-start(bf16[128,8,1024]{2,1,0:T(8,128)(2,1)} %copy.126), calls=%async_computation.2 | async-start | bytes 4194304 | tf_op jit(solution)/shard_map/all_to_all | solution.py:129
  202.8 0.3 all-gather.2.cloned.1.call-start
  203.1 0.5 all-gather.2.cloned.1.call-update
  203.5 0.1 rsqrt.13
  203.7 0.6 reshape.227
  204.4 95.6 %all-to-all-done.2 = bf16[128,8,1024]{2,1,0:T(8,128)(2,1)} async-done(((bf16[128,8,1024]{2,1,0:T(8,128)(2,1)}), bf16[128,8,1024]{2,1,0:T(8,128)(2,1)}, u32[]{:S(2)}, u32[]{:S(2)}) %all-to-all-start.2) | async-done | bytes 2097184 | tf_op jit(solution)/shard_map/all_to_all | solution.py:129
  299.9 2.3 fusion.1
  302.3 1.3 fusion.12
  303.6 0.5 copy.134
  304.2 0.8 copy-done.4
  305.0 2.4 broadcast_in_dim.41
  307.4 3.6 all-to-all-start.3
  311.0 3.0 constant_dynamic-slice_fusion
  314.0 2.3 reshape.228
  316.2 2.3 copy.128
  318.5 2.3 dot_general.36
  320.8 16.8 %all-to-all-done.3 = bf16[4,128,2,1024]{3,2,1,0:T(2,128)(2,1)S(1)} async-done(((bf16[4,128,2,1024]{3,2,1,0:T(2,128)(2,1)}), bf16[4,128,2,1024]{3,2,1,0:T(2,128)(2,1)S(1)}, u32[]{:S(2)}, u32[]{:S(2)}) %all-to-all-start.3) | async-done | bytes 2097184 | tf_op jit(solution)/shard_map/all_to_all | solution.py:143
  337.6 2.2 reshape.233
  339.8 3.4 fusion.3
  343.3 1.9 collective-permute-start.1
  345.3 2.6 collective-permute-done.1
  347.9 0.2 fusion.13
  348.0 0.4 copy.131
  348.5 0.2 copy.132
  348.6 13.6 %all_to_all.31 = bf16[4,64,1024]{2,1,0:T(8,128)(2,1)S(1)} all-to-all(bf16[4,64,1024]{2,1,0:T(8,128)(2,1)S(1)} %copy.132), channel_id=1, replica_groups=mesh['dx'=4,'dz'=16,'dc'=2,'bin'=4] {'dx'}, dimensions={0} | all-to-all | bytes 1048576 | tf_op jit(solution)/shard_map/all_to_all | solution.py:165
  362.4 17.8 %all_to_all.32 = bf16[16,4,1024]{2,1,0:T(4,128)(2,1)S(1)} all-to-all(bf16[16,4,1024]{2,1,0:T(4,128)(2,1)S(1)} %convert_element_type.83), channel_id=1, replica_groups=mesh['dx'=4,'dz'=16,'dc'=2,'bin'=4] {'dz'}, dimensions={0} | all-to-all | bytes 262144 | tf_op jit(solution)/shard_map/all_to_all | solution.py:168
  380.3 0.6 broadcast_multiply_fusion
  (36 shorter events, 0.9 us)
Async XLA Ops:
  7.2 1.2 copy-start
  8.7 32.8 %copy-start.8 = (s32[128,1]{0,1:T(1,128)S(1)}, s32[128,1]{0,1:T(1,128)}, u32[]{:S(2)}) copy-start(s32[128,1]{0,1:T(1,128)} %param.7) | copy-start | bytes 1540
  8.7 33.0 %copy-start.7 = (s32[192]{0:T(256)S(1)}, s32[192]{0:T(256)}, u32[]{:S(2)}) copy-start(s32[192]{0:T(256)} %param.8) | copy-start | bytes 2308
  8.7 33.7 %copy-start.3 = (bf16[128,2,2048]{2,1,0:T(2,128)(2,1)S(1)}, bf16[128,2,2048]{2,1,0:T(2,128)(2,1)}, u32[]{:S(2)}) copy-start(bf16[128,2,2048]{2,1,0:T(2,128)(2,1)} %param.5) | copy-start | bytes 3145732
  39.6 8.3 %collective-permute-start = (bf16[4,256,1024]{2,1,0:T(8,128)(2,1)}, bf16[4,256,1024]{2,1,0:T(8,128)(2,1)}, u32[]{:S(2)}, u32[]{:S(2)}) collective-permute-start(bf16[4,256,1024]{2,1,0:T(8,128)(2,1)} %all_to_all.30), channel_id=1, source_target_pairs={{0,4},{4,0},{1,5},{5,1},{2,6},{6,2},{3,7},{7,3},{8,12},{12,8},{9,1... | collective-permute-start | bytes 6291464 | tf_op jit(solution)/shard_map/ppermute | solution.py:82
  50.3 1.1 copy-start.1
  53.5 22.7 %copy-start.9 = (s32[192]{0:T(256)S(1)}, s32[192]{0:T(256)}, u32[]{:S(2)}) copy-start(s32[192]{0:T(256)} %param.9) | copy-start | bytes 2308
  53.5 117.7 %all-to-all-start.1 = ((bf16[128,8,1024]{2,1,0:T(8,128)(2,1)}), bf16[128,8,1024]{2,1,0:T(8,128)(2,1)S(1)}, u32[]{:S(2)}, u32[]{:S(2)}) async-start(bf16[128,8,1024]{2,1,0:T(8,128)(2,1)} %fusion.5), calls=%async_computation.1 | async-start | bytes 4194304 | tf_op jit(solution)/shard_map/all_to_all | solution.py:118
  178.6 1.6 copy-start.5
  180.2 4.0 %copy-start.6 = (bf16[512,1024]{1,0:T(8,128)(2,1)S(1)}, bf16[512,1024]{1,0:T(8,128)(2,1)}, u32[]{:S(2)}) copy-start(bf16[512,1024]{1,0:T(8,128)(2,1)} %reshape_squeeze.6) | copy-start | bytes 3145732
  191.9 11.8 %copy-start.2 = (f32[256,1024]{1,0:T(8,128)S(1)}, f32[256,1024]{1,0:T(8,128)}, u32[]{:S(2)}) copy-start(f32[256,1024]{1,0:T(8,128)} %copy-done.1) | copy-start | bytes 3145732
  191.9 108.1 %all-to-all-start.2 = ((bf16[128,8,1024]{2,1,0:T(8,128)(2,1)}), bf16[128,8,1024]{2,1,0:T(8,128)(2,1)}, u32[]{:S(2)}, u32[]{:S(2)}) async-start(bf16[128,8,1024]{2,1,0:T(8,128)(2,1)} %copy.126), calls=%async_computation.2 | async-start | bytes 4194304 | tf_op jit(solution)/shard_map/all_to_all | solution.py:129
  202.8 108.2 %all-gather.2.cloned.1.call-start = ((), (), s32[]{:S(2)}) async-start(), calls=%async_computation.6 | async-start | bytes 5242880 | tf_op jit(solution)/shard_map/all_gather | solution.py:142
  304.2 0.8 copy-start.4
  307.4 30.2 %all-to-all-start.3 = ((bf16[4,128,2,1024]{3,2,1,0:T(2,128)(2,1)}), bf16[4,128,2,1024]{3,2,1,0:T(2,128)(2,1)S(1)}, u32[]{:S(2)}, u32[]{:S(2)}) async-start(bf16[4,128,2,1024]{3,2,1,0:T(2,128)(2,1)} %broadcast_in_dim.41), calls=%async_computation.3 | async-start | bytes 4194304 | tf_op jit(solution)/shard_map/all_to_all | solution.py:143
  343.3 4.6 %collective-permute-start.1 = (f32[4,16,4,1024]{3,1,2,0:T(8,128)S(1)}, f32[4,16,4,1024]{3,1,2,0:T(8,128)S(1)}, u32[]{:S(2)}, u32[]{:S(2)}) collective-permute-start(f32[4,16,4,1024]{3,1,2,0:T(8,128)S(1)} %dynamic-slice_bitcast_fusion), channel_id=1, source_target_pairs={{0,4},{4,0},{1,5},{5,1},{2,6},{6,2},{3,7},{7,3},{8,12},{12,8},{9,1... | collective-permute-start | bytes 3145736 | tf_op jit(solution)/shard_map/ppermute | solution.py:163
Sparse Core Ops, SparseCore 0:
  205.7 54.6 all-gather.1

commit v16 on v14

--- a/solution.py
+++ b/solution.py
@@ -117,9 +117,6 @@
         outbox.reshape(sources, block, emb_dim), DP, split_axis=0, concat_axis=0, tiled=True
     )
     inbox = inbox.reshape(sources, views, per_owner, emb_dim)
-    columns = lax.all_to_all(
-        flat.reshape(rows_dev * views, bins_n, part_rows), "bin", split_axis=1, concat_axis=0, tiled=True
-    ).reshape(bins_n * rows_dev * views, part_rows)
     valid = (inbox[:, 0, :, 0] < 2.0).reshape(group_slots)
     query = inbox[:, 0].reshape(group_slots, emb_dim)
     key = inbox[:, 1].reshape(group_slots, emb_dim)
@@ -127,10 +124,23 @@
     allowed = allowed_mask(valid, first, bin_link, group_slots, per_bin)
     grads = contrast(query, key, allowed, valid.astype(jnp.float32))
     back = jnp.stack([g.reshape(sources, per_owner, emb_dim) for g in grads], axis=1)
-    back, columns = lax.optimization_barrier((back, columns))
+    own_bin = lax.axis_index("bin")
+    chunks = flat.reshape(rows_dev * views, bins_n, part_rows)
+    sends = [
+        lax.dynamic_index_in_dim(chunks, (own_bin + shift) % bins_n, 1, keepdims=False)
+        for shift in range(bins_n)
+    ]
+    back, sends = lax.optimization_barrier((back, sends))
     returned = lax.all_to_all(
         back.reshape(sources, block, emb_dim), DP, split_axis=0, concat_axis=0, tiled=True
     )
+    arrived = [sends[0]] + [
+        lax.ppermute(sends[shift], "bin", perm=[(j, (j + shift) % bins_n) for j in range(bins_n)])
+        for shift in range(1, bins_n)
+    ]
+    returned, arrived = lax.optimization_barrier((returned, arrived))
+    by_source = (own_bin - jnp.arange(bins_n, dtype=jnp.int32)) % bins_n
+    columns = jnp.take(jnp.stack(arrived), by_source, axis=0).reshape(-1, part_rows)
     row_grads = lax.dot_general(
         picks,
         returned.reshape(lanes, emb_dim),

time: 382 us -> 367 us (0.961)
  waiting for transfers between devices: 215 us -> 199 us
  starting transfers between devices: 43.1 us -> 47 us
    all_to_all x1, waiting for transfers between devices: 96.3 us -> 77.6 us  [local(): lax.all_to_all(back.reshape(sources, block, emb_dim), DP, split_axis=0, c...]
    ppermute x0 -> x3, starting transfers between devices: none -> 9.17 us  [local(): lax.ppermute(sends[shift], 'bin', perm=[(j, (j + shift) % bins_n) for j i...]
    ppermute x0 -> x3, waiting for transfers between devices: none -> 8.69 us  [local(): lax.ppermute(sends[shift], 'bin', perm=[(j, (j + shift) % bins_n) for j i...]
    all_to_all x1, waiting for transfers between devices: 23.5 us -> 19.6 us  [local(): lax.all_to_all(jnp.broadcast_to(grad_rows[None], (bins_n, *grad_rows.shap...]
  transfers between devices with their start and end apart: 6 -> 8, of which waited for: 5 -> 7; matrix products, arithmetic and copies ran while one was open for 8% -> 5% of each run, Pallas kernels for 0% -> 0%
where the time goes in v16:
time: 367 us; the launch traced here: 365 us
  waiting for transfers between devices  199 us (54%)
  blocking collectives  62.2 us (17%)
  starting transfers between devices  47 us (13%)
  local copies, waits for them, and re-layouts  31.9 us (9%)
  matrix products  13.4 us (4%)
  other arithmetic  8.61 us (2%)
    all_to_all x1, waiting for transfers between devices, local(): lax.all_to_all(outbox.reshape(sources, block, emb_dim), DP, split_axis=0,...  88.5 us
    all_to_all x1, waiting for transfers between devices, local(): lax.all_to_all(back.reshape(sources, block, emb_dim), DP, split_axis=0, c...  77.6 us
    all_to_all x1, blocking collectives, local(): lax.all_to_all(copies, 'bin', split_axis=0, concat_axis=0, tiled=True)  30.7 us
    all_to_all x1, starting transfers between devices, local(): lax.all_to_all(outbox.reshape(sources, block, emb_dim), DP, split_axis=0,...  19.9 us
    all_to_all x1, waiting for transfers between devices, local(): lax.all_to_all(jnp.broadcast_to(grad_rows[None], (bins_n, *grad_rows.shap...  19.6 us
    all_to_all x1, blocking collectives, local(): lax.all_to_all(planes, 'dz', split_axis=0, concat_axis=0, tiled=True)  17.8 us
    all_to_all x1, blocking collectives, local(): lax.all_to_all(planes, 'dx', split_axis=0, concat_axis=0, tiled=True)  13.6 us
    all_to_all x1, starting transfers between devices, local(): lax.all_to_all(back.reshape(sources, block, emb_dim), DP, split_axis=0, c...  10.3 us
  transfers between devices with their start and end apart: 8, of which 7 were waited for; matrix products, arithmetic and copies ran while one was open for 5% of the time, Pallas kernels for 0%

profile of v16, /device:TPU:6, one launch (start us, length us, event | category | flops | bytes accessed | tf_op | source)
XLA Modules:
  0.0 365.0 jit_solution(12185791640820434982)
XLA Ops:
  0.7 1.2 copy-done
  1.9 0.3 broadcast_in_dim.49
  2.2 30.7 %all_to_all.30 = bf16[4,256,1024]{2,1,0:T(8,128)(2,1)S(1)} all-to-all(bf16[4,256,1024]{2,1,0:T(8,128)(2,1)S(1)} %broadcast_in_dim.49), channel_id=1, replica_groups=mesh['dx'=4,'dz'=16,'dc'=2,'bin'=4] {'bin'}, dimensions={0} | all-to-all | bytes 4194304 | tf_op jit(solution)/shard_map/all_to_all | solution.py:81
  32.9 2.0 collective-permute-start
  35.0 1.2 reshape.284
  36.4 0.2 convert_reduce_fusion.2
  37.1 0.2 convert_reduce_fusion
  37.3 1.9 collective-permute-done
  39.2 1.9 select_bitcast_fusion.1
  41.1 0.4 pad_maximum_fusion
  41.5 0.8 copy-done.5
  42.3 1.3 multiply_reduce_fusion
  43.7 2.2 fusion.5
  45.8 19.9 %all-to-all-start.1 = ((bf16[128,8,1024]{2,1,0:T(8,128)(2,1)}), bf16[128,8,1024]{2,1,0:T(8,128)(2,1)S(1)}, u32[]{:S(2)}, u32[]{:S(2)}) async-start(bf16[128,8,1024]{2,1,0:T(8,128)(2,1)} %fusion.5), calls=%async_computation.1 | async-start | bytes 4194304 | tf_op jit(solution)/shard_map/all_to_all | solution.py:116
  65.8 1.7 reshape_reshape.3
  67.6 0.6 fusion.43
  70.3 0.6 fusion.51
  70.9 2.2 constant_dynamic-slice_fusion
  73.0 0.9 copy_bitcast_fusion
  73.9 0.8 copy_bitcast_fusion.2
  74.8 88.5 %all-to-all-done.1 = bf16[128,8,1024]{2,1,0:T(8,128)(2,1)S(1)} async-done(((bf16[128,8,1024]{2,1,0:T(8,128)(2,1)}), bf16[128,8,1024]{2,1,0:T(8,128)(2,1)S(1)}, u32[]{:S(2)}, u32[]{:S(2)}) %all-to-all-start.1) | async-done | bytes 2097184 | tf_op jit(solution)/shard_map/all_to_all | solution.py:116
  163.3 1.2 copy.110
  164.7 0.8 copy.113
  165.5 0.3 reshape_squeeze.6
  165.8 0.8 copy.114
  166.6 0.3 reshape_squeeze.7
  166.9 0.9 copy.112
  167.9 2.6 fusion.52
  170.5 1.8 multiply_convert_fusion.1
  172.3 1.7 multiply_convert_fusion
  174.0 0.4 stack_reshape.6
  174.4 0.3 copy.115
  174.7 0.5 copy-done.6
  175.2 0.6 stack_reshape.7
  175.9 0.3 copy.116
  176.2 0.2 pad_maximum_fusion.1
  176.4 2.5 copy.117
  178.9 10.3 %all-to-all-start.2 = ((bf16[128,8,1024]{2,1,0:T(8,128)(2,1)}), bf16[128,8,1024]{2,1,0:T(8,128)(2,1)S(1)}, u32[]{:S(2)}, u32[]{:S(2)}) async-start(bf16[128,8,1024]{2,1,0:T(8,128)(2,1)} %copy.117), calls=%async_computation.2 | async-start | bytes 4194304 | tf_op jit(solution)/shard_map/all_to_all | solution.py:134
  189.2 2.5 collective-permute-start.1
  191.7 4.0 %collective-permute-start.2 = (bf16[256,512]{1,0:T(8,128)(2,1)}, bf16[256,512]{1,0:T(8,128)(2,1)}, u32[]{:S(2)}, u32[]{:S(2)}) collective-permute-start(bf16[256,512]{1,0:T(8,128)(2,1)} %get-tuple-element.15), channel_id=1, source_target_pairs={{0,2},{1,3},{2,0},{3,1},{4,6},{5,7},{6,4},{7,5},{8,10},{9,11},{10,... | collective-permute-start | bytes 786440 | tf_op jit(solution)/shard_map/ppermute | solution.py:138
  195.7 2.7 collective-permute-start.3
  198.4 1.8 reshape.289
  200.4 6.2 %collective-permute-done.1 = bf16[256,512]{1,0:T(8,128)(2,1)} collective-permute-done((bf16[256,512]{1,0:T(8,128)(2,1)}, bf16[256,512]{1,0:T(8,128)(2,1)}, u32[]{:S(2)}, u32[]{:S(2)}) %collective-permute-start.1) | collective-permute-done | bytes 262176 | tf_op jit(solution)/shard_map/ppermute | solution.py:138
  206.6 2.5 collective-permute-done.3
  209.1 77.6 %all-to-all-done.2 = bf16[128,8,1024]{2,1,0:T(8,128)(2,1)S(1)} async-done(((bf16[128,8,1024]{2,1,0:T(8,128)(2,1)}), bf16[128,8,1024]{2,1,0:T(8,128)(2,1)S(1)}, u32[]{:S(2)}, u32[]{:S(2)}) %all-to-all-start.2) | async-done | bytes 2097184 | tf_op jit(solution)/shard_map/all_to_all | solution.py:134
  286.7 0.8 fusion.1
  287.4 1.3 fusion.11
  288.8 0.5 copy.125
  289.3 2.4 broadcast_in_dim.92
  291.8 3.6 all-to-all-start.3
  295.5 1.2 pad_maximum_fusion.2
  296.8 1.6 gather_fusion
  298.4 1.5 copy.119
  299.9 1.1 select_bitcast_fusion.2
  301.0 1.5 dot_general.35
  302.4 19.6 %all-to-all-done.3 = bf16[4,128,2,1024]{3,2,1,0:T(2,128)(2,1)S(1)} async-done(((bf16[4,128,2,1024]{3,2,1,0:T(2,128)(2,1)}), bf16[4,128,2,1024]{3,2,1,0:T(2,128)(2,1)S(1)}, u32[]{:S(2)}, u32[]{:S(2)}) %all-to-all-start.3) | async-done | bytes 2097184 | tf_op jit(solution)/shard_map/all_to_all | solution.py:153
  322.0 2.2 reshape.300
  324.2 3.0 fusion.3
  327.4 1.9 collective-permute-start.4
  329.3 2.6 collective-permute-done.4
  332.1 0.4 copy.122
  332.7 13.6 %all_to_all.31 = bf16[4,64,1024]{2,1,0:T(8,128)(2,1)S(1)} all-to-all(bf16[4,64,1024]{2,1,0:T(8,128)(2,1)S(1)} %copy.123), channel_id=1, replica_groups=mesh['dx'=4,'dz'=16,'dc'=2,'bin'=4] {'dx'}, dimensions={0} | all-to-all | bytes 1048576 | tf_op jit(solution)/shard_map/all_to_all | solution.py:173
  346.5 17.8 %all_to_all.32 = bf16[16,4,1024]{2,1,0:T(4,128)(2,1)S(1)} all-to-all(bf16[16,4,1024]{2,1,0:T(4,128)(2,1)S(1)} %convert_element_type.83), channel_id=1, replica_groups=mesh['dx'=4,'dz'=16,'dc'=2,'bin'=4] {'dz'}, dimensions={0} | all-to-all | bytes 262144 | tf_op jit(solution)/shard_map/all_to_all | solution.py:176
  364.4 0.6 broadcast_multiply_fusion
  (51 shorter events, 2.2 us)
Async XLA Ops:
  0.6 1.2 copy-start
  2.2 32.8 %copy-start.2 = (bf16[128,2,2048]{2,1,0:T(2,128)(2,1)S(1)}, bf16[128,2,2048]{2,1,0:T(2,128)(2,1)}, u32[]{:S(2)}) copy-start(bf16[128,2,2048]{2,1,0:T(2,128)(2,1)} %param.5) | copy-start | bytes 3145732
  32.9 3.3 copy-start.9
  32.9 3.5 copy-start.8
  32.9 6.3 %collective-permute-start = (bf16[4,256,1024]{2,1,0:T(8,128)(2,1)S(1)}, bf16[4,256,1024]{2,1,0:T(8,128)(2,1)}, u32[]{:S(2)}, u32[]{:S(2)}) collective-permute-start(bf16[4,256,1024]{2,1,0:T(8,128)(2,1)S(1)} %all_to_all.30), channel_id=1, source_target_pairs={{0,4},{4,0},{1,5},{5,1},{2,6},{6,2},{3,7},{7,3},{8,12},{12,8},{9,1... | collective-permute-start | bytes 6291464 | tf_op jit(solution)/shard_map/ppermute | solution.py:82
  41.1 1.2 copy-start.5
  43.6 2.2 copy-start.4
  45.8 117.5 %all-to-all-start.1 = ((bf16[128,8,1024]{2,1,0:T(8,128)(2,1)}), bf16[128,8,1024]{2,1,0:T(8,128)(2,1)S(1)}, u32[]{:S(2)}, u32[]{:S(2)}) async-start(bf16[128,8,1024]{2,1,0:T(8,128)(2,1)} %fusion.5), calls=%async_computation.1 | async-start | bytes 4194304 | tf_op jit(solution)/shard_map/all_to_all | solution.py:116
  65.8 4.4 %copy-start.10 = (s32[192]{0:T(256)S(1)}, s32[192]{0:T(256)}, u32[]{:S(2)}) copy-start(s32[192]{0:T(256)} %param.9) | copy-start | bytes 2308
  172.3 1.7 copy-start.7
  174.0 1.2 copy-start.6
  178.9 107.8 %all-to-all-start.2 = ((bf16[128,8,1024]{2,1,0:T(8,128)(2,1)}), bf16[128,8,1024]{2,1,0:T(8,128)(2,1)S(1)}, u32[]{:S(2)}, u32[]{:S(2)}) async-start(bf16[128,8,1024]{2,1,0:T(8,128)(2,1)} %copy.117), calls=%async_computation.2 | async-start | bytes 4194304 | tf_op jit(solution)/shard_map/all_to_all | solution.py:134
  189.2 17.4 %collective-permute-start.1 = (bf16[256,512]{1,0:T(8,128)(2,1)}, bf16[256,512]{1,0:T(8,128)(2,1)}, u32[]{:S(2)}, u32[]{:S(2)}) collective-permute-start(bf16[256,512]{1,0:T(8,128)(2,1)} %get-tuple-element.14), channel_id=1, source_target_pairs={{0,1},{1,2},{2,3},{3,0},{4,5},{5,6},{6,7},{7,4},{8,9},{9,10},{10,1... | collective-permute-start | bytes 786440 | tf_op jit(solution)/shard_map/ppermute | solution.py:138
  191.7 14.9 %collective-permute-start.2 = (bf16[256,512]{1,0:T(8,128)(2,1)}, bf16[256,512]{1,0:T(8,128)(2,1)}, u32[]{:S(2)}, u32[]{:S(2)}) collective-permute-start(bf16[256,512]{1,0:T(8,128)(2,1)} %get-tuple-element.15), channel_id=1, source_target_pairs={{0,2},{1,3},{2,0},{3,1},{4,6},{5,7},{6,4},{7,5},{8,10},{9,11},{10,... | collective-permute-start | bytes 786440 | tf_op jit(solution)/shard_map/ppermute | solution.py:138
  195.7 13.5 %collective-permute-start.3 = (bf16[256,512]{1,0:T(8,128)(2,1)}, bf16[256,512]{1,0:T(8,128)(2,1)}, u32[]{:S(2)}, u32[]{:S(2)}) collective-permute-start(bf16[256,512]{1,0:T(8,128)(2,1)} %get-tuple-element.16), channel_id=1, source_target_pairs={{0,3},{1,0},{2,1},{3,2},{4,7},{5,4},{6,5},{7,6},{8,11},{9,8},{10,9... | collective-permute-start | bytes 786440 | tf_op jit(solution)/shard_map/ppermute | solution.py:138
  289.3 2.4 copy-start.3
  291.8 30.2 %all-to-all-start.3 = ((bf16[4,128,2,1024]{3,2,1,0:T(2,128)(2,1)}), bf16[4,128,2,1024]{3,2,1,0:T(2,128)(2,1)S(1)}, u32[]{:S(2)}, u32[]{:S(2)}) async-start(bf16[4,128,2,1024]{3,2,1,0:T(2,128)(2,1)} %broadcast_in_dim.92), calls=%async_computation.3 | async-start | bytes 4194304 | tf_op jit(solution)/shard_map/all_to_all | solution.py:153
  327.4 4.6 %collective-permute-start.4 = (f32[4,16,4,1024]{3,1,2,0:T(8,128)S(1)}, f32[4,16,4,1024]{3,1,2,0:T(8,128)S(1)}, u32[]{:S(2)}, u32[]{:S(2)}) collective-permute-start(f32[4,16,4,1024]{3,1,2,0:T(8,128)S(1)} %dynamic-slice_bitcast_fusion), channel_id=1, source_target_pairs={{0,4},{4,0},{1,5},{5,1},{2,6},{6,2},{3,7},{7,3},{8,12},{12,8},{9,1... | collective-permute-start | bytes 3145736 | tf_op jit(solution)/shard_map/ppermute | solution.py:171
  331.9 33.1 %copy-start.1 = (bf16[512,1024]{1,0:T(8,128)(2,1)S(1)}, bf16[512,1024]{1,0:T(8,128)(2,1)}, u32[]{:S(2)}) copy-start(bf16[512,1024]{1,0:T(8,128)(2,1)} %param.6) | copy-start | bytes 3145732

commit v17 on v16

--- a/solution.py
+++ b/solution.py
@@ -150,13 +150,11 @@
     grad_rows = (
         scale * (row_grads - unit * jnp.sum(unit * row_grads, axis=2, keepdims=True))
     ).astype(jnp.bfloat16)
-    outgrad = lax.all_to_all(
-        jnp.broadcast_to(grad_rows[None], (bins_n, *grad_rows.shape)),
-        "bin",
-        split_axis=0,
-        concat_axis=0,
-        tiled=True,
-    )
+    given_rows = [grad_rows] + [
+        lax.ppermute(grad_rows, "bin", perm=[(j, (j + shift) % bins_n) for j in range(bins_n)])
+        for shift in range(1, bins_n)
+    ]
+    outgrad = jnp.take(jnp.stack(given_rows), by_source, axis=0)
     local_grad = lax.dot_general(
         columns,
         outgrad.reshape(-1, emb_dim),

time: 367 us -> 375 us (1.022)
  blocking collectives: 62.2 us -> 44.5 us
  waiting for transfers between devices: 199 us -> 210 us
  starting transfers between devices: 47 us -> 57.2 us
    all_to_all x1 -> x0, blocking collectives: 17.8 us -> none  [local(): lax.all_to_all(planes, 'dz', split_axis=0, concat_axis=0, tiled=True)]
    ppermute x0 -> x3, waiting for transfers between devices: none -> 17.7 us  [local(): lax.ppermute(grad_rows, 'bin', perm=[(j, (j + shift) % bins_n) for j in r...]
    ppermute x0 -> x3, starting transfers between devices: none -> 9.17 us  [local(): lax.ppermute(grad_rows, 'bin', perm=[(j, (j + shift) % bins_n) for j in r...]
    all_to_all x1, waiting for transfers between devices: 19.6 us -> 12.6 us  [local(): lax.all_to_all(planes, 'dz', split_axis=0, concat_axis=0, tiled=True)]
    select_n x0 -> x2, local copies, waits for them, and re-layouts: none -> 4.39 us  [local(): outgrad = jnp.take(jnp.stack(given_rows), by_source, axis=0)]
  transfers between devices with their start and end apart: 8 -> 11, of which waited for: 7 -> 9; matrix products, arithmetic and copies ran while one was open for 5% -> 4% of each run, Pallas kernels for 0% -> 0%
where the time goes in v17:
time: 375 us; the launch traced here: 373 us
  waiting for transfers between devices  210 us (56%)
  starting transfers between devices  57.2 us (15%)
  blocking collectives  44.5 us (12%)
  local copies, waits for them, and re-layouts  31.8 us (8%)
  matrix products  15 us (4%)
  other arithmetic  10.9 us (3%)
    all_to_all x1, waiting for transfers between devices, local(): lax.all_to_all(outbox.reshape(sources, block, emb_dim), DP, split_axis=0,...  88.5 us
    all_to_all x1, waiting for transfers between devices, local(): lax.all_to_all(back.reshape(sources, block, emb_dim), DP, split_axis=0, c...  77.4 us
    all_to_all x1, blocking collectives, local(): lax.all_to_all(copies, 'bin', split_axis=0, concat_axis=0, tiled=True)  30.7 us
    all_to_all x1, starting transfers between devices, local(): lax.all_to_all(outbox.reshape(sources, block, emb_dim), DP, split_axis=0,...  19.9 us
    ppermute x3, waiting for transfers between devices, local(): lax.ppermute(grad_rows, 'bin', perm=[(j, (j + shift) % bins_n) for j in r...  17.7 us
    all_to_all x1, blocking collectives, local(): lax.all_to_all(planes, 'dx', split_axis=0, concat_axis=0, tiled=True)  13.8 us
    all_to_all x1, waiting for transfers between devices, local(): lax.all_to_all(planes, 'dz', split_axis=0, concat_axis=0, tiled=True)  12.6 us
    all_to_all x1, starting transfers between devices, local(): lax.all_to_all(back.reshape(sources, block, emb_dim), DP, split_axis=0, c...  10.9 us
  transfers between devices with their start and end apart: 11, of which 9 were waited for; matrix products, arithmetic and copies ran while one was open for 4% of the time, Pallas kernels for 0%

profile of v17, /device:TPU:6, one launch (start us, length us, event | category | flops | bytes accessed | tf_op | source)
XLA Modules:
  0.0 372.9 jit_solution(15712280739030972557)
XLA Ops:
  0.7 1.2 copy-done
  2.2 30.7 %all_to_all.25 = bf16[4,256,1024]{2,1,0:T(8,128)(2,1)S(1)} all-to-all(bf16[4,256,1024]{2,1,0:T(8,128)(2,1)S(1)} %broadcast_in_dim.86), channel_id=1, replica_groups=mesh['dx'=4,'dz'=16,'dc'=2,'bin'=4] {'bin'}, dimensions={0} | all-to-all | bytes 4194304 | tf_op jit(solution)/shard_map/all_to_all | solution.py:81
  32.9 2.0 collective-permute-start
  35.0 1.2 reshape.313
  37.3 1.9 collective-permute-done
  39.2 1.9 select_bitcast_fusion.1
  41.1 0.4 pad_maximum_fusion
  41.5 0.8 copy-done.7
  42.3 1.3 multiply_reduce_fusion
  43.7 2.1 fusion.5
  45.8 19.9 %all-to-all-start.1 = ((bf16[128,8,1024]{2,1,0:T(8,128)(2,1)}), bf16[128,8,1024]{2,1,0:T(8,128)(2,1)S(1)}, u32[]{:S(2)}, u32[]{:S(2)}) async-start(bf16[128,8,1024]{2,1,0:T(8,128)(2,1)} %fusion.5), calls=%async_computation.1 | async-start | bytes 4194304 | tf_op jit(solution)/shard_map/all_to_all | solution.py:116
  65.8 1.7 reshape_reshape.3
  67.6 0.6 fusion.43
  70.3 0.6 fusion.51
  70.9 2.2 constant_dynamic-slice_fusion
  73.1 0.9 copy_bitcast_fusion
  74.0 0.8 copy_bitcast_fusion.2
  74.8 88.5 %all-to-all-done.1 = bf16[128,8,1024]{2,1,0:T(8,128)(2,1)S(1)} async-done(((bf16[128,8,1024]{2,1,0:T(8,128)(2,1)}), bf16[128,8,1024]{2,1,0:T(8,128)(2,1)S(1)}, u32[]{:S(2)}, u32[]{:S(2)}) %all-to-all-start.1) | async-done | bytes 2097184 | tf_op jit(solution)/shard_map/all_to_all | solution.py:116
  163.3 1.2 copy.109
  164.7 0.8 copy.112
  165.8 0.8 copy.113
  166.9 0.9 copy.111
  167.9 2.6 fusion.52
  170.5 1.8 multiply_convert_fusion.1
  172.3 1.7 multiply_convert_fusion
  174.0 0.4 stack_reshape.6
  174.7 0.5 copy-done.9
  175.2 0.6 stack_reshape.7
  175.9 0.3 copy.115
  176.4 2.5 copy.116
  178.9 10.9 %all-to-all-start.2 = ((bf16[128,8,1024]{2,1,0:T(8,128)(2,1)}), bf16[128,8,1024]{2,1,0:T(8,128)(2,1)}, u32[]{:S(2)}, u32[]{:S(2)}) async-start(bf16[128,8,1024]{2,1,0:T(8,128)(2,1)} %copy.116), calls=%async_computation.2 | async-start | bytes 4194304 | tf_op jit(solution)/shard_map/all_to_all | solution.py:134
  189.8 2.5 collective-permute-start.1
  192.3 4.0 %collective-permute-start.2 = (bf16[256,512]{1,0:T(8,128)(2,1)S(1)}, bf16[256,512]{1,0:T(8,128)(2,1)}, u32[]{:S(2)}, u32[]{:S(2)}) collective-permute-start(bf16[256,512]{1,0:T(8,128)(2,1)S(1)} %copy-done.12), channel_id=1, source_target_pairs={{0,2},{1,3},{2,0},{3,1},{4,6},{5,7},{6,4},{7,5},{8,10},{9,11},{10,... | collective-permute-start | bytes 786440 | tf_op jit(solution)/shard_map/ppermute | solution.py:138
  196.3 2.7 collective-permute-start.3
  199.1 0.6 reshape.318
  200.0 6.9 %collective-permute-done.1 = bf16[256,512]{1,0:T(8,128)(2,1)S(1)} collective-permute-done((bf16[256,512]{1,0:T(8,128)(2,1)S(1)}, bf16[256,512]{1,0:T(8,128)(2,1)S(1)}, u32[]{:S(2)}, u32[]{:S(2)}) %collective-permute-start.1) | collective-permute-done | bytes 262176 | tf_op jit(solution)/shard_map/ppermute | solution.py:138
  206.9 2.6 collective-permute-done.3
  209.5 77.4 %all-to-all-done.2 = bf16[128,8,1024]{2,1,0:T(8,128)(2,1)} async-done(((bf16[128,8,1024]{2,1,0:T(8,128)(2,1)}), bf16[128,8,1024]{2,1,0:T(8,128)(2,1)}, u32[]{:S(2)}, u32[]{:S(2)}) %all-to-all-start.2) | async-done | bytes 2097184 | tf_op jit(solution)/shard_map/all_to_all | solution.py:134
  286.9 2.3 fusion.1
  289.3 1.3 fusion.11
  290.6 2.5 collective-permute-start.4
  293.1 4.0 %collective-permute-start.5 = (bf16[128,2,1024]{2,0,1:T(8,128)(2,1)S(1)}, bf16[128,2,1024]{2,0,1:T(8,128)(2,1)}, u32[]{:S(2)}, u32[]{:S(2)}) collective-permute-start(bf16[128,2,1024]{2,0,1:T(8,128)(2,1)S(1)} %fusion.11), channel_id=1, source_target_pairs={{0,2},{1,3},{2,0},{3,1},{4,6},{5,7},{6,4},{7,5},{8,10},{9,11},{10,... | collective-permute-start | bytes 1572872 | tf_op jit(solution)/shard_map/ppermute | solution.py:154
  297.1 2.7 collective-permute-start.6
  299.8 1.2 pad_maximum_fusion.3
  301.1 0.6 gather_fusion
  301.7 0.5 copy.118
  302.4 1.2 dot_general.35
  303.6 15.1 %collective-permute-done.4 = bf16[128,2,1024]{2,0,1:T(8,128)(2,1)S(1)} collective-permute-done((bf16[128,2,1024]{2,0,1:T(8,128)(2,1)S(1)}, bf16[128,2,1024]{2,0,1:T(8,128)(2,1)S(1)}, u32[]{:S(2)}, u32[]{:S(2)}) %collective-permute-start.4) | collective-permute-done | bytes 524320 | tf_op jit(solution)/shard_map/ppermute | solution.py:154
  318.7 2.6 collective-permute-done.6
  321.3 1.5 pad_maximum_fusion.2
  322.8 2.0 gather_fusion.1
  324.8 1.9 broadcast_select_fusion
  326.7 2.2 copy.119
  328.8 2.2 reshape.336
  331.1 3.0 fusion.3
  334.2 1.9 collective-permute-start.7
  336.2 2.6 collective-permute-done.7
  339.0 0.4 copy.121
  339.6 13.8 %all_to_all.26 = bf16[4,64,1024]{2,1,0:T(8,128)(2,1)S(1)} all-to-all(bf16[4,64,1024]{2,1,0:T(8,128)(2,1)S(1)} %copy.122), channel_id=1, replica_groups=mesh['dx'=4,'dz'=16,'dc'=2,'bin'=4] {'dx'}, dimensions={0} | all-to-all | bytes 1048576 | tf_op jit(solution)/shard_map/all_to_all | solution.py:171
  353.4 0.7 convert_element_type.83
  354.1 4.1 %all-to-all-start.4 = ((bf16[16,4,1024]{2,1,0:T(4,128)(2,1)}), bf16[16,4,1024]{2,1,0:T(4,128)(2,1)S(1)}, u32[]{:S(2)}, u32[]{:S(2)}) async-start(bf16[16,4,1024]{2,1,0:T(4,128)(2,1)} %convert_element_type.83), calls=%async_computation.4 | async-start | bytes 262144 | tf_op jit(solution)/shard_map/all_to_all | solution.py:174
  358.2 1.3 copy.124
  359.6 12.6 %all-to-all-done.4 = bf16[16,4,1024]{2,1,0:T(4,128)(2,1)S(1)} async-done(((bf16[16,4,1024]{2,1,0:T(4,128)(2,1)}), bf16[16,4,1024]{2,1,0:T(4,128)(2,1)S(1)}, u32[]{:S(2)}, u32[]{:S(2)}) %all-to-all-start.4) | async-done | bytes 131104 | tf_op jit(solution)/shard_map/all_to_all | solution.py:174
  372.3 0.6 broadcast_multiply_fusion
  (73 shorter events, 4.0 us)
Async XLA Ops:
  0.6 1.2 copy-start
  2.2 32.8 %copy-start.4 = (bf16[128,2,2048]{2,1,0:T(2,128)(2,1)S(1)}, bf16[128,2,2048]{2,1,0:T(2,128)(2,1)}, u32[]{:S(2)}) copy-start(bf16[128,2,2048]{2,1,0:T(2,128)(2,1)} %param.5) | copy-start | bytes 3145732
  32.9 3.3 copy-start.16
  32.9 3.5 copy-start.15
  32.9 6.3 %collective-permute-start = (bf16[4,256,1024]{2,1,0:T(8,128)(2,1)S(1)}, bf16[4,256,1024]{2,1,0:T(8,128)(2,1)}, u32[]{:S(2)}, u32[]{:S(2)}) collective-permute-start(bf16[4,256,1024]{2,1,0:T(8,128)(2,1)S(1)} %all_to_all.25), channel_id=1, source_target_pairs={{0,4},{4,0},{1,5},{5,1},{2,6},{6,2},{3,7},{7,3},{8,12},{12,8},{9,1... | collective-permute-start | bytes 6291464 | tf_op jit(solution)/shard_map/ppermute | solution.py:82
  41.1 1.2 copy-start.7
  43.6 2.2 copy-start.5
  45.8 117.5 %all-to-all-start.1 = ((bf16[128,8,1024]{2,1,0:T(8,128)(2,1)}), bf16[128,8,1024]{2,1,0:T(8,128)(2,1)S(1)}, u32[]{:S(2)}, u32[]{:S(2)}) async-start(bf16[128,8,1024]{2,1,0:T(8,128)(2,1)} %fusion.5), calls=%async_computation.1 | async-start | bytes 4194304 | tf_op jit(solution)/shard_map/all_to_all | solution.py:116
  65.7 4.4 %copy-start.17 = (s32[192]{0:T(256)S(1)}, s32[192]{0:T(256)}, u32[]{:S(2)}) copy-start(s32[192]{0:T(256)} %param.9) | copy-start | bytes 2308
  172.3 1.7 copy-start.10
  174.0 1.2 copy-start.9
  178.9 10.9 %copy-start.13 = (bf16[256,512]{1,0:T(8,128)(2,1)S(1)}, bf16[256,512]{1,0:T(8,128)(2,1)}, u32[]{:S(2)}) copy-start(bf16[256,512]{1,0:T(8,128)(2,1)} %get-tuple-element.14) | copy-start | bytes 786436
  178.9 13.4 %copy-start.12 = (bf16[256,512]{1,0:T(8,128)(2,1)S(1)}, bf16[256,512]{1,0:T(8,128)(2,1)}, u32[]{:S(2)}) copy-start(bf16[256,512]{1,0:T(8,128)(2,1)} %get-tuple-element.15) | copy-start | bytes 786436
  178.9 17.4 %copy-start.11 = (bf16[256,512]{1,0:T(8,128)(2,1)S(1)}, bf16[256,512]{1,0:T(8,128)(2,1)}, u32[]{:S(2)}) copy-start(bf16[256,512]{1,0:T(8,128)(2,1)} %get-tuple-element.16) | copy-start | bytes 786436
  178.9 20.3 %copy-start.6 = (f32[256,1024]{1,0:T(8,128)S(1)}, f32[256,1024]{1,0:T(8,128)}, u32[]{:S(2)}) copy-start(f32[256,1024]{1,0:T(8,128)} %copy-done.5) | copy-start | bytes 3145732
  178.9 108.1 %all-to-all-start.2 = ((bf16[128,8,1024]{2,1,0:T(8,128)(2,1)}), bf16[128,8,1024]{2,1,0:T(8,128)(2,1)}, u32[]{:S(2)}, u32[]{:S(2)}) async-start(bf16[128,8,1024]{2,1,0:T(8,128)(2,1)} %copy.116), calls=%async_computation.2 | async-start | bytes 4194304 | tf_op jit(solution)/shard_map/all_to_all | solution.py:134
  189.8 17.1 %collective-permute-start.1 = (bf16[256,512]{1,0:T(8,128)(2,1)S(1)}, bf16[256,512]{1,0:T(8,128)(2,1)S(1)}, u32[]{:S(2)}, u32[]{:S(2)}) collective-permute-start(bf16[256,512]{1,0:T(8,128)(2,1)S(1)} %copy-done.13), channel_id=1, source_target_pairs={{0,1},{1,2},{2,3},{3,0},{4,5},{5,6},{6,7},{7,4},{8,9},{9,10},{10,1... | collective-permute-start | bytes 786440 | tf_op jit(solution)/shard_map/ppermute | solution.py:138
  192.3 14.6 %collective-permute-start.2 = (bf16[256,512]{1,0:T(8,128)(2,1)S(1)}, bf16[256,512]{1,0:T(8,128)(2,1)}, u32[]{:S(2)}, u32[]{:S(2)}) collective-permute-start(bf16[256,512]{1,0:T(8,128)(2,1)S(1)} %copy-done.12), channel_id=1, source_target_pairs={{0,2},{1,3},{2,0},{3,1},{4,6},{5,7},{6,4},{7,5},{8,10},{9,11},{10,... | collective-permute-start | bytes 786440 | tf_op jit(solution)/shard_map/ppermute | solution.py:138
  196.3 13.3 %collective-permute-start.3 = (bf16[256,512]{1,0:T(8,128)(2,1)S(1)}, bf16[256,512]{1,0:T(8,128)(2,1)}, u32[]{:S(2)}, u32[]{:S(2)}) collective-permute-start(bf16[256,512]{1,0:T(8,128)(2,1)S(1)} %copy-done.11), channel_id=1, source_target_pairs={{0,3},{1,0},{2,1},{3,2},{4,7},{5,4},{6,5},{7,6},{8,11},{9,8},{10,9... | collective-permute-start | bytes 786440 | tf_op jit(solution)/shard_map/ppermute | solution.py:138
  206.9 83.7 %copy-start.14 = (bf16[256,512]{1,0:T(8,128)(2,1)}, bf16[256,512]{1,0:T(8,128)(2,1)S(1)}, u32[]{:S(2)}) copy-start(bf16[256,512]{1,0:T(8,128)(2,1)S(1)} %collective-permute-done.1) | copy-start | bytes 786436
  290.6 30.7 %copy-start.2 = (bf16[128,2,1024]{2,0,1:T(8,128)(2,1)}, bf16[128,2,1024]{2,0,1:T(8,128)(2,1)S(1)}, u32[]{:S(2)}) copy-start(bf16[128,2,1024]{2,0,1:T(8,128)(2,1)S(1)} %fusion.11) | copy-start | bytes 1572868
  290.6 28.0 %collective-permute-start.4 = (bf16[128,2,1024]{2,0,1:T(8,128)(2,1)S(1)}, bf16[128,2,1024]{2,0,1:T(8,128)(2,1)S(1)}, u32[]{:S(2)}, u32[]{:S(2)}) collective-permute-start(bf16[128,2,1024]{2,0,1:T(8,128)(2,1)S(1)} %fusion.11), channel_id=1, source_target_pairs={{0,1},{1,2},{2,3},{3,0},{4,5},{5,6},{6,7},{7,4},{8,9},{9,10},{10,1... | collective-permute-start | bytes 1572872 | tf_op jit(solution)/shard_map/ppermute | solution.py:154
  293.1 25.6 %collective-permute-start.5 = (bf16[128,2,1024]{2,0,1:T(8,128)(2,1)S(1)}, bf16[128,2,1024]{2,0,1:T(8,128)(2,1)}, u32[]{:S(2)}, u32[]{:S(2)}) collective-permute-start(bf16[128,2,1024]{2,0,1:T(8,128)(2,1)S(1)} %fusion.11), channel_id=1, source_target_pairs={{0,2},{1,3},{2,0},{3,1},{4,6},{5,7},{6,4},{7,5},{8,10},{9,11},{10,... | collective-permute-start | bytes 1572872 | tf_op jit(solution)/shard_map/ppermute | solution.py:154
  297.1 24.2 %collective-permute-start.6 = (bf16[128,2,1024]{2,0,1:T(8,128)(2,1)S(1)}, bf16[128,2,1024]{2,0,1:T(8,128)(2,1)}, u32[]{:S(2)}, u32[]{:S(2)}) collective-permute-start(bf16[128,2,1024]{2,0,1:T(8,128)(2,1)S(1)} %fusion.11), channel_id=1, source_target_pairs={{0,3},{1,0},{2,1},{3,2},{4,7},{5,4},{6,5},{7,6},{8,11},{9,8},{10,9... | collective-permute-start | bytes 1572872 | tf_op jit(solution)/shard_map/ppermute | solution.py:154
  328.8 2.2 copy-start.8
  334.2 4.6 %collective-permute-start.7 = (f32[4,16,4,1024]{3,1,2,0:T(8,128)S(1)}, f32[4,16,4,1024]{3,1,2,0:T(8,128)S(1)}, u32[]{:S(2)}, u32[]{:S(2)}) collective-permute-start(f32[4,16,4,1024]{3,1,2,0:T(8,128)S(1)} %dynamic-slice_bitcast_fusion), channel_id=1, source_target_pairs={{0,4},{4,0},{1,5},{5,1},{2,6},{6,2},{3,7},{7,3},{8,12},{12,8},{9,1... | collective-permute-start | bytes 3145736 | tf_op jit(solution)/shard_map/ppermute | solution.py:169
  339.0 19.3 %copy-start.3 = (bf16[128,2,1024]{2,0,1:T(8,128)(2,1)S(1)}, bf16[128,2,1024]{2,0,1:T(8,128)(2,1)}, u32[]{:S(2)}) copy-start(bf16[128,2,1024]{2,0,1:T(8,128)(2,1)} %copy-done.2) | copy-start | bytes 1572868
  339.4 33.5 %copy-start.1 = (bf16[512,1024]{1,0:T(8,128)(2,1)S(1)}, bf16[512,1024]{1,0:T(8,128)(2,1)}, u32[]{:S(2)}) copy-start(bf16[512,1024]{1,0:T(8,128)(2,1)} %param.6) | copy-start | bytes 3145732
  354.1 18.1 %all-to-all-start.4 = ((bf16[16,4,1024]{2,1,0:T(4,128)(2,1)}), bf16[16,4,1024]{2,1,0:T(4,128)(2,1)S(1)}, u32[]{:S(2)}, u32[]{:S(2)}) async-start(bf16[16,4,1024]{2,1,0:T(4,128)(2,1)} %convert_element_type.83), calls=%async_computation.4 | async-start | bytes 262144 | tf_op jit(solution)/shard_map/all_to_all | solution.py:174

commit v18 on v16

--- a/solution.py
+++ b/solution.py
@@ -168,7 +168,8 @@
     local_grad = jnp.transpose(local_grad.reshape(*sizes, per_dev, emb_dim), (2, 0, 1, 3, 4))
     kept = lax.dynamic_index_in_dim(local_grad, core, 0, keepdims=False)
     given = lax.dynamic_index_in_dim(local_grad, 1 - core, 0, keepdims=False)
-    local_grad = kept + lax.ppermute(given, "dc", perm=[(0, 1), (1, 0)])
+    swapped = lax.ppermute(given.astype(jnp.bfloat16), "dc", perm=[(0, 1), (1, 0)])
+    local_grad = kept + swapped.astype(jnp.float32)
     planes = local_grad.reshape(sizes[0], sizes[1] * per_dev, emb_dim).astype(jnp.bfloat16)
     planes = lax.all_to_all(planes, "dx", split_axis=0, concat_axis=0, tiled=True)
     planes = jnp.sum(planes.astype(jnp.float32), axis=0)

time: 367 us -> 366 us (level)
  no operation moved by 1% of the time
where the time goes in v18:
time: 366 us; the launch traced here: 364 us
  waiting for transfers between devices  198 us (54%)
  blocking collectives  62.2 us (17%)
  starting transfers between devices  47 us (13%)
  local copies, waits for them, and re-layouts  31.9 us (9%)
  matrix products  13.4 us (4%)
  other arithmetic  8.6 us (2%)
    all_to_all x1, waiting for transfers between devices, local(): lax.all_to_all(outbox.reshape(sources, block, emb_dim), DP, split_axis=0,...  88.5 us
    all_to_all x1, waiting for transfers between devices, local(): lax.all_to_all(back.reshape(sources, block, emb_dim), DP, split_axis=0, c...  77.6 us
    all_to_all x1, blocking collectives, local(): lax.all_to_all(copies, 'bin', split_axis=0, concat_axis=0, tiled=True)  30.7 us
    all_to_all x1, starting transfers between devices, local(): lax.all_to_all(outbox.reshape(sources, block, emb_dim), DP, split_axis=0,...  19.9 us
    all_to_all x1, waiting for transfers between devices, local(): lax.all_to_all(jnp.broadcast_to(grad_rows[None], (bins_n, *grad_rows.shap...  19.6 us
    all_to_all x1, blocking collectives, local(): lax.all_to_all(planes, 'dz', split_axis=0, concat_axis=0, tiled=True)  17.8 us
    all_to_all x1, blocking collectives, local(): lax.all_to_all(planes, 'dx', split_axis=0, concat_axis=0, tiled=True)  13.6 us
    all_to_all x1, starting transfers between devices, local(): lax.all_to_all(back.reshape(sources, block, emb_dim), DP, split_axis=0, c...  10.3 us
  transfers between devices with their start and end apart: 8, of which 7 were waited for; matrix products, arithmetic and copies ran while one was open for 5% of the time, Pallas kernels for 0%

profile of v18, /device:TPU:6, one launch (start us, length us, event | category | flops | bytes accessed | tf_op | source)
XLA Modules:
  0.0 364.2 jit_solution(10685380645247799537)
XLA Ops:
  0.7 1.2 copy-done
  1.9 0.3 broadcast_in_dim.49
  2.2 30.7 %all_to_all.30 = bf16[4,256,1024]{2,1,0:T(8,128)(2,1)S(1)} all-to-all(bf16[4,256,1024]{2,1,0:T(8,128)(2,1)S(1)} %broadcast_in_dim.49), channel_id=1, replica_groups=mesh['dx'=4,'dz'=16,'dc'=2,'bin'=4] {'bin'}, dimensions={0} | all-to-all | bytes 4194304 | tf_op jit(solution)/shard_map/all_to_all | solution.py:81
  32.9 2.0 collective-permute-start
  35.0 1.2 reshape.285
  36.4 0.2 convert_reduce_fusion.2
  37.1 0.2 convert_reduce_fusion
  37.3 1.9 collective-permute-done
  39.2 1.9 select_bitcast_fusion.1
  41.1 0.4 pad_maximum_fusion
  41.5 0.8 copy-done.5
  42.3 1.3 multiply_reduce_fusion
  43.7 2.2 fusion.5
  45.8 19.9 %all-to-all-start.1 = ((bf16[128,8,1024]{2,1,0:T(8,128)(2,1)}), bf16[128,8,1024]{2,1,0:T(8,128)(2,1)S(1)}, u32[]{:S(2)}, u32[]{:S(2)}) async-start(bf16[128,8,1024]{2,1,0:T(8,128)(2,1)} %fusion.5), calls=%async_computation.1 | async-start | bytes 4194304 | tf_op jit(solution)/shard_map/all_to_all | solution.py:116
  65.8 1.7 reshape_reshape.3
  67.6 0.6 fusion.44
  70.3 0.6 fusion.52
  70.9 2.2 constant_dynamic-slice_fusion
  73.0 0.9 copy_bitcast_fusion
  73.9 0.8 copy_bitcast_fusion.2
  74.8 88.5 %all-to-all-done.1 = bf16[128,8,1024]{2,1,0:T(8,128)(2,1)S(1)} async-done(((bf16[128,8,1024]{2,1,0:T(8,128)(2,1)}), bf16[128,8,1024]{2,1,0:T(8,128)(2,1)S(1)}, u32[]{:S(2)}, u32[]{:S(2)}) %all-to-all-start.1) | async-done | bytes 2097184 | tf_op jit(solution)/shard_map/all_to_all | solution.py:116
  163.3 1.2 copy.111
  164.7 0.8 copy.114
  165.5 0.3 reshape_squeeze.6
  165.8 0.8 copy.115
  166.6 0.3 reshape_squeeze.7
  166.9 0.9 copy.113
  167.9 2.6 fusion.53
  170.5 1.8 multiply_convert_fusion.1
  172.3 1.7 multiply_convert_fusion
  174.0 0.4 stack_reshape.6
  174.4 0.3 copy.116
  174.7 0.5 copy-done.6
  175.2 0.6 stack_reshape.7
  175.9 0.3 copy.117
  176.2 0.2 pad_maximum_fusion.1
  176.4 2.5 copy.118
  178.9 10.3 %all-to-all-start.2 = ((bf16[128,8,1024]{2,1,0:T(8,128)(2,1)}), bf16[128,8,1024]{2,1,0:T(8,128)(2,1)S(1)}, u32[]{:S(2)}, u32[]{:S(2)}) async-start(bf16[128,8,1024]{2,1,0:T(8,128)(2,1)} %copy.118), calls=%async_computation.2 | async-start | bytes 4194304 | tf_op jit(solution)/shard_map/all_to_all | solution.py:134
  189.2 2.5 collective-permute-start.1
  191.7 4.0 %collective-permute-start.2 = (bf16[256,512]{1,0:T(8,128)(2,1)}, bf16[256,512]{1,0:T(8,128)(2,1)}, u32[]{:S(2)}, u32[]{:S(2)}) collective-permute-start(bf16[256,512]{1,0:T(8,128)(2,1)} %get-tuple-element.15), channel_id=1, source_target_pairs={{0,2},{1,3},{2,0},{3,1},{4,6},{5,7},{6,4},{7,5},{8,10},{9,11},{10,... | collective-permute-start | bytes 786440 | tf_op jit(solution)/shard_map/ppermute | solution.py:138
  195.7 2.7 collective-permute-start.3
  198.4 1.8 reshape.290
  200.4 6.2 %collective-permute-done.1 = bf16[256,512]{1,0:T(8,128)(2,1)} collective-permute-done((bf16[256,512]{1,0:T(8,128)(2,1)}, bf16[256,512]{1,0:T(8,128)(2,1)}, u32[]{:S(2)}, u32[]{:S(2)}) %collective-permute-start.1) | collective-permute-done | bytes 262176 | tf_op jit(solution)/shard_map/ppermute | solution.py:138
  206.6 2.5 collective-permute-done.3
  209.1 77.6 %all-to-all-done.2 = bf16[128,8,1024]{2,1,0:T(8,128)(2,1)S(1)} async-done(((bf16[128,8,1024]{2,1,0:T(8,128)(2,1)}), bf16[128,8,1024]{2,1,0:T(8,128)(2,1)S(1)}, u32[]{:S(2)}, u32[]{:S(2)}) %all-to-all-start.2) | async-done | bytes 2097184 | tf_op jit(solution)/shard_map/all_to_all | solution.py:134
  286.7 0.8 fusion.1
  287.4 1.3 fusion.11
  288.8 0.5 copy.126
  289.3 2.4 broadcast_in_dim.92
  291.8 3.6 all-to-all-start.3
  295.5 1.2 pad_maximum_fusion.2
  296.8 1.6 gather_fusion
  298.4 1.5 copy.120
  299.9 1.1 select_bitcast_fusion.2
  301.0 1.5 dot_general.35
  302.4 19.6 %all-to-all-done.3 = bf16[4,128,2,1024]{3,2,1,0:T(2,128)(2,1)S(1)} async-done(((bf16[4,128,2,1024]{3,2,1,0:T(2,128)(2,1)}), bf16[4,128,2,1024]{3,2,1,0:T(2,128)(2,1)S(1)}, u32[]{:S(2)}, u32[]{:S(2)}) %all-to-all-start.3) | async-done | bytes 2097184 | tf_op jit(solution)/shard_map/all_to_all | solution.py:153
  322.0 2.2 reshape.301
  324.2 3.0 fusion.3
  327.4 1.9 collective-permute-start.4
  329.3 1.9 collective-permute-done.4
  331.3 0.4 copy.123
  331.9 13.6 %all_to_all.31 = bf16[4,64,1024]{2,1,0:T(8,128)(2,1)S(1)} all-to-all(bf16[4,64,1024]{2,1,0:T(8,128)(2,1)S(1)} %copy.124), channel_id=1, replica_groups=mesh['dx'=4,'dz'=16,'dc'=2,'bin'=4] {'dx'}, dimensions={0} | all-to-all | bytes 1048576 | tf_op jit(solution)/shard_map/all_to_all | solution.py:174
  345.7 17.8 %all_to_all.32 = bf16[16,4,1024]{2,1,0:T(4,128)(2,1)S(1)} all-to-all(bf16[16,4,1024]{2,1,0:T(4,128)(2,1)S(1)} %convert_element_type.95), channel_id=1, replica_groups=mesh['dx'=4,'dz'=16,'dc'=2,'bin'=4] {'dz'}, dimensions={0} | all-to-all | bytes 262144 | tf_op jit(solution)/shard_map/all_to_all | solution.py:177
  363.6 0.6 broadcast_multiply_fusion
  (51 shorter events, 2.1 us)
Async XLA Ops:
  0.6 1.2 copy-start
  2.2 32.8 %copy-start.2 = (bf16[128,2,2048]{2,1,0:T(2,128)(2,1)S(1)}, bf16[128,2,2048]{2,1,0:T(2,128)(2,1)}, u32[]{:S(2)}) copy-start(bf16[128,2,2048]{2,1,0:T(2,128)(2,1)} %param.5) | copy-start | bytes 3145732
  32.9 3.3 copy-start.9
  32.9 3.5 copy-start.8
  32.9 6.3 %collective-permute-start = (bf16[4,256,1024]{2,1,0:T(8,128)(2,1)S(1)}, bf16[4,256,1024]{2,1,0:T(8,128)(2,1)}, u32[]{:S(2)}, u32[]{:S(2)}) collective-permute-start(bf16[4,256,1024]{2,1,0:T(8,128)(2,1)S(1)} %all_to_all.30), channel_id=1, source_target_pairs={{0,4},{4,0},{1,5},{5,1},{2,6},{6,2},{3,7},{7,3},{8,12},{12,8},{9,1... | collective-permute-start | bytes 6291464 | tf_op jit(solution)/shard_map/ppermute | solution.py:82
  41.1 1.2 copy-start.5
  43.6 2.2 copy-start.4
  45.8 117.5 %all-to-all-start.1 = ((bf16[128,8,1024]{2,1,0:T(8,128)(2,1)}), bf16[128,8,1024]{2,1,0:T(8,128)(2,1)S(1)}, u32[]{:S(2)}, u32[]{:S(2)}) async-start(bf16[128,8,1024]{2,1,0:T(8,128)(2,1)} %fusion.5), calls=%async_computation.1 | async-start | bytes 4194304 | tf_op jit(solution)/shard_map/all_to_all | solution.py:116
  65.8 4.4 %copy-start.10 = (s32[192]{0:T(256)S(1)}, s32[192]{0:T(256)}, u32[]{:S(2)}) copy-start(s32[192]{0:T(256)} %param.9) | copy-start | bytes 2308
  172.3 1.7 copy-start.7
  174.0 1.2 copy-start.6
  178.9 107.8 %all-to-all-start.2 = ((bf16[128,8,1024]{2,1,0:T(8,128)(2,1)}), bf16[128,8,1024]{2,1,0:T(8,128)(2,1)S(1)}, u32[]{:S(2)}, u32[]{:S(2)}) async-start(bf16[128,8,1024]{2,1,0:T(8,128)(2,1)} %copy.118), calls=%async_computation.2 | async-start | bytes 4194304 | tf_op jit(solution)/shard_map/all_to_all | solution.py:134
  189.2 17.4 %collective-permute-start.1 = (bf16[256,512]{1,0:T(8,128)(2,1)}, bf16[256,512]{1,0:T(8,128)(2,1)}, u32[]{:S(2)}, u32[]{:S(2)}) collective-permute-start(bf16[256,512]{1,0:T(8,128)(2,1)} %get-tuple-element.14), channel_id=1, source_target_pairs={{0,1},{1,2},{2,3},{3,0},{4,5},{5,6},{6,7},{7,4},{8,9},{9,10},{10,1... | collective-permute-start | bytes 786440 | tf_op jit(solution)/shard_map/ppermute | solution.py:138
  191.7 14.9 %collective-permute-start.2 = (bf16[256,512]{1,0:T(8,128)(2,1)}, bf16[256,512]{1,0:T(8,128)(2,1)}, u32[]{:S(2)}, u32[]{:S(2)}) collective-permute-start(bf16[256,512]{1,0:T(8,128)(2,1)} %get-tuple-element.15), channel_id=1, source_target_pairs={{0,2},{1,3},{2,0},{3,1},{4,6},{5,7},{6,4},{7,5},{8,10},{9,11},{10,... | collective-permute-start | bytes 786440 | tf_op jit(solution)/shard_map/ppermute | solution.py:138
  195.7 13.5 %collective-permute-start.3 = (bf16[256,512]{1,0:T(8,128)(2,1)}, bf16[256,512]{1,0:T(8,128)(2,1)}, u32[]{:S(2)}, u32[]{:S(2)}) collective-permute-start(bf16[256,512]{1,0:T(8,128)(2,1)} %get-tuple-element.16), channel_id=1, source_target_pairs={{0,3},{1,0},{2,1},{3,2},{4,7},{5,4},{6,5},{7,6},{8,11},{9,8},{10,9... | collective-permute-start | bytes 786440 | tf_op jit(solution)/shard_map/ppermute | solution.py:138
  289.3 2.4 copy-start.3
  291.8 30.2 %all-to-all-start.3 = ((bf16[4,128,2,1024]{3,2,1,0:T(2,128)(2,1)}), bf16[4,128,2,1024]{3,2,1,0:T(2,128)(2,1)S(1)}, u32[]{:S(2)}, u32[]{:S(2)}) async-start(bf16[4,128,2,1024]{3,2,1,0:T(2,128)(2,1)} %broadcast_in_dim.92), calls=%async_computation.3 | async-start | bytes 4194304 | tf_op jit(solution)/shard_map/all_to_all | solution.py:153
  327.4 3.8 %collective-permute-start.4 = (bf16[4,16,4,1024]{3,1,2,0:T(8,128)(2,1)S(1)}, bf16[4,16,4,1024]{3,1,2,0:T(8,128)(2,1)S(1)}, u32[]{:S(2)}, u32[]{:S(2)}) collective-permute-start(bf16[4,16,4,1024]{3,1,2,0:T(8,128)(2,1)S(1)} %fusion.24), channel_id=1, source_target_pairs={{0,4},{4,0},{1,5},{5,1},{2,6},{6,2},{3,7},{7,3},{8,12},{12,8},{9,1... | collective-permute-start | bytes 1572872 | tf_op jit(solution)/shard_map/ppermute | solution.py:171
  331.2 33.1 %copy-start.1 = (bf16[512,1024]{1,0:T(8,128)(2,1)S(1)}, bf16[512,1024]{1,0:T(8,128)(2,1)}, u32[]{:S(2)}) copy-start(bf16[512,1024]{1,0:T(8,128)(2,1)} %param.6) | copy-start | bytes 3145732
